TPU v7x, 256 devices: a whole 4x4x8 slice. The times are simulated.
256 devices in a mesh: gx: 32 (over z_hi, y, x), gy: 2 (over core), gz: 4 (over z_lo).
Axes of the slice: x: 4, y: 4, z: 8 (z_hi: 2, z_lo: 4; z = z_hi * 4 + z_lo), core: 2. Of those that a mesh axis runs over, the one named last changes fastest.
Arguments:
- inputs: bfloat16 [4, 256, 32, 256], P(None, 'gx', 'gz', 'gy'), may hold values from -6 to 6
- w_in: bfloat16 [16, 4, 3, 3, 3], replicated, may hold values from -0.875 to 0.875
- w_fine_enc: bfloat16 [16, 16, 3, 3, 3], replicated, may hold values from -0.4375 to 0.4375
- w_down_mid: bfloat16 [64, 16, 2, 2, 2], replicated, may hold values from -0.75 to 0.75
- w_mid_enc: bfloat16 [27, 4096], replicated, may hold values from -0.21875 to 0.21875
- w_down_bottom: bfloat16 [8, 16384], replicated, may hold values from -0.375 to 0.375
- w_query: bfloat16 [256, 256], replicated, may hold values from -8 to 8
- w_key: bfloat16 [256, 256], replicated, may hold values from -0.375 to 0.375
- w_value: bfloat16 [256, 256], replicated, may hold values from -0.375 to 0.375
- w_attn_out: bfloat16 [256, 256], replicated, may hold values from -0.375 to 0.375
- w_up_mid: bfloat16 [8, 16384], replicated, may hold values from -0.375 to 0.375
- w_mid_dec: bfloat16 [27, 4096], replicated, may hold values from -0.21875 to 0.21875
- w_up_fine: bfloat16 [64, 16, 2, 2, 2], replicated, may hold values from -0.75 to 0.75
- w_fine_dec: bfloat16 [16, 16, 3, 3, 3], replicated, may hold values from -0.4375 to 0.4375
- w_head: bfloat16 [4, 16], replicated, may hold values from -1.5 to 1.5
Outputs:
- wake: float32 [4, 256, 32, 256], P(None, 'gx', 'gz', 'gy')
All inputs are finite; a program needn't handle non-finite values.
Results may differ from a plain program's by a relative error of at most 0.023.
The roundings to bfloat16 on the way count: a program that leaves them out, or rounds other values in their place, can miss the bound.
Values may be sent and summed in bfloat16 or wider, within the bound.
No kernel may reach another device: no remote copies, remote signals or barrier semaphores. Data moves between devices by JAX's collectives and lax.ppermute only.
A program may use at most 64 MiB of HBM per device.

v0:
```python
import jax
import jax.numpy as jnp
from jax import lax
from jax.experimental import pallas as pl
from jax.experimental.pallas import tpu as pltpu
from jax.sharding import PartitionSpec as P

C1 = 64
C2 = 256
HEADS = 4


NUMS = ("NCDHW", "OIDHW", "NCDHW")
FINE_SIDES = (("gx", 0, 1), ("gy", 3, 1), ("gz", 2, 1))
FINE_CROSS = (("gy", 3, 1), ("gz", 2, 1))
MID_SIDES = (("gx", 1, 1), ("gy", 3, 1), ("gz", 2, 1))
MID_CROSS = (("gy", 3, 1), ("gz", 2, 1))


def extended(block, sides):
    for axis, dim, width in sides:
        count = lax.axis_size(axis)
        top = lax.slice_in_dim(block, block.shape[dim] - width, None, axis=dim)
        bottom = lax.slice_in_dim(block, 0, width, axis=dim)
        if count == 2:
            first = lax.axis_index(axis) == 0
            got = lax.ppermute(jnp.where(first, top, bottom), axis, [(0, 1), (1, 0)])
            low = jnp.where(first, jnp.zeros_like(got), got)
            high = jnp.where(first, got, jnp.zeros_like(got))
        else:
            forward = [(i, i + 1) for i in range(count - 1)]
            backward = [(target, source) for source, target in forward]
            low = lax.ppermute(top, axis, forward)
            high = lax.ppermute(bottom, axis, backward)
        block = jnp.concatenate([low, block, high], axis=dim)
    return block


def inside_rows(field, offset):
    rows = field.shape[0]
    start = lax.axis_index("gx") * (rows + 2 * offset) + offset
    index = start + jnp.arange(rows)
    keep = (index >= 0) & (index < (rows + 2 * offset) * lax.axis_size("gx"))
    return jnp.where(keep[:, None, None, None], field, jnp.zeros_like(field))


def unfold(weight, side, first, second):
    return weight.reshape(side, side, side, first, second).transpose(3, 4, 0, 1, 2)


def round_up(value, step):
    return (value + step - 1) // step * step


def fine_kernel(p_ref, w_ref, *rest, sx, sv, ss, rows, head):
    if head:
        h_ref, o_ref, band_ref = rest
    else:
        o_ref, band_ref = rest
    cout, cin = w_ref.shape[1:]
    depth = cin * rows
    lanes = p_ref.shape[-1]
    sv_bits, row_bits = sv.bit_length() - 1, rows.bit_length() - 1
    r = lax.broadcasted_iota(jnp.int32, (cout * sv, cout), 0)
    q = lax.broadcasted_iota(jnp.int32, (cout * sv, cout), 1)
    widen_rows = ((r >> sv_bits) == q).astype(jnp.bfloat16)
    r = lax.broadcasted_iota(jnp.int32, (cin, depth), 0)
    q = lax.broadcasted_iota(jnp.int32, (cin, depth), 1)
    widen_cols = ((q >> row_bits) == r).astype(jnp.bfloat16)
    r = lax.broadcasted_iota(jnp.int32, (cout * sv, depth), 0)
    q = lax.broadcasted_iota(jnp.int32, (cout * sv, depth), 1)
    offset = (q & (rows - 1)) - (r & (sv - 1))
    for a in range(3):
        for c in range(3):
            band = jnp.zeros((cout * sv, depth), jnp.float32)
            for b in range(3):
                tap = w_ref[(a * 3 + b) * 3 + c]
                grown = jnp.dot(widen_rows, tap, preferred_element_type=jnp.float32)
                grown = jnp.dot(
                    grown.astype(jnp.bfloat16), widen_cols, preferred_element_type=jnp.float32
                )
                band = band + jnp.where(offset == b, grown, 0.0)
            band_ref[a * 3 + c] = band.astype(jnp.bfloat16)
    def row(x, carry):
        acc = jnp.zeros((cout * sv, ss), jnp.float32)
        for a in range(3):
            slab = p_ref[x + a].astype(jnp.float32)
            for c in range(3):
                piece = slab if c == 0 else pltpu.roll(slab, lanes - c, 1)
                piece = piece[:, :ss].astype(jnp.bfloat16)
                acc = acc + jnp.dot(band_ref[a * 3 + c], piece, preferred_element_type=jnp.float32)
        act = (acc * jax.nn.sigmoid(acc)).astype(jnp.bfloat16)
        if head:
            res = jnp.dot(h_ref[...], act, preferred_element_type=jnp.float32)
            o_ref[:, x] = res.reshape(res.shape[0] // sv, sv, ss)
        else:
            o_ref[x] = act.astype(jnp.float32).reshape(cout, sv, ss)
        return carry

    lax.fori_loop(0, sx, row, 0)


def fine_conv(field, weight, sides, head=None):
    _, cin, sv, ss = field.shape
    cout = weight.shape[0]
    rows = round_up(sv + 2, 16)
    lanes = round_up(ss + 2, 128)
    padded = extended(field, sides)
    sx = padded.shape[0] - 2
    padded = jnp.pad(padded, ((0, 0), (0, 0), (0, rows - sv - 2), (0, lanes - ss - 2)))
    padded = padded.reshape(sx + 2, cin * rows, lanes)
    operands = [padded, weight.transpose(2, 3, 4, 0, 1).reshape(27, cout, cin)]
    if head is None:
        out_shape = jax.ShapeDtypeStruct((sx, cout, sv, ss), jnp.float32)
    else:
        eye = jnp.eye(sv, dtype=jnp.float32)
        kron = jnp.einsum("po,vw->pvow", head.astype(jnp.float32), eye)
        operands.append(kron.reshape(head.shape[0] * sv, cout * sv).astype(jnp.bfloat16))
        out_shape = jax.ShapeDtypeStruct((head.shape[0], sx, sv, ss), jnp.float32)
    kernel = lambda *refs: fine_kernel(
        *refs, sx=sx, sv=sv, ss=ss, rows=rows, head=head is not None
    )
    return pl.pallas_call(
        kernel,
        out_shape=out_shape,
        scratch_shapes=[pltpu.VMEM((9, cout * sv, cin * rows), jnp.bfloat16)],
    )(*operands)


def conv_valid(padded, weight):
    return lax.conv_general_dilated(
        padded[None],
        weight,
        (1, 1, 1),
        "VALID",
        dimension_numbers=NUMS,
        preferred_element_type=jnp.float32,
    )[0]


def mid_conv(field, weight, sides=MID_SIDES):
    padded = extended(field, sides)
    return conv_valid(padded, weight)


def conv_down(field, weight):
    return lax.conv_general_dilated(
        field[None],
        weight,
        (2, 2, 2),
        "VALID",
        dimension_numbers=NUMS,
        preferred_element_type=jnp.float32,
    )[0]


def fine_down(field, weight):
    sx, c, sv, ss = field.shape
    blocks = field.reshape(sx // 2, 2, c, sv // 2, 2, ss // 2, 2)
    return jnp.einsum("xaivbsc,oiabc->oxvs", blocks, weight, preferred_element_type=jnp.float32)


def fine_up(field, weight):
    outer = jnp.einsum("ixvs,ioabc->xaovbsc", field, weight, preferred_element_type=jnp.float32)
    chans, sx, sv, ss = (weight.shape[1], field.shape[1], field.shape[2], field.shape[3])
    return outer.reshape(2 * sx, chans, 2 * sv, 2 * ss)


def conv_up(field, weight):
    outer = jnp.einsum("ixvs,ioabc->oxavbsc", field, weight, preferred_element_type=jnp.float32)
    chans, sx, sv, ss = (weight.shape[1], field.shape[1], field.shape[2], field.shape[3])
    return outer.reshape(chans, 2 * sx, 2 * sv, 2 * ss)


def activate(value):
    return jax.nn.silu(value).astype(jnp.bfloat16)


def project(weight, field):
    return jnp.einsum("oc,cxp->oxp", weight, field, preferred_element_type=jnp.float32)


def normalize(block):
    values_f = block.astype(jnp.float32)
    mean_sq = jnp.mean(values_f * values_f, axis=0)
    return (values_f * lax.rsqrt(mean_sq + 1e-05)).astype(jnp.bfloat16)


def split_heads(weight, normed):
    chans, sx, count = normed.shape
    return project(weight, normed).astype(jnp.bfloat16).reshape(HEADS, chans // HEADS, sx, count)


def combine(queries, keys, values):
    scale = 1.0 / jnp.sqrt(jnp.float32(queries.shape[1]))
    scores = (
        jnp.einsum("hdxp,hdyp->hxyp", queries, keys, preferred_element_type=jnp.float32) * scale
    )
    weights = jax.nn.softmax(scores, axis=2).astype(jnp.bfloat16)
    attended = jnp.einsum("hxyp,hdyp->hdxp", weights, values, preferred_element_type=jnp.float32)
    heads, depth, sx, count = attended.shape
    return attended.astype(jnp.bfloat16).reshape(heads * depth, sx, count)


def finish(block, attended, w_attn_out):
    return (block.astype(jnp.float32) + project(w_attn_out, attended)).astype(jnp.bfloat16)


def on_device(
    inputs,
    w_in,
    w_fine_enc,
    w_down_mid,
    w_mid_enc,
    w_down_bottom,
    w_query,
    w_key,
    w_value,
    w_attn_out,
    w_up_mid,
    w_mid_dec,
    w_up_fine,
    w_fine_dec,
    w_head,
):
    fields = extended(inputs.transpose(1, 0, 2, 3), (("gx", 0, 4),))
    first = inside_rows(fine_conv(fields, w_in, FINE_CROSS).astype(jnp.bfloat16), -3)
    fine_wide = inside_rows(fine_conv(first, w_fine_enc, FINE_CROSS).astype(jnp.bfloat16), -2)
    fine_skip = fine_wide[2:-2]
    mid_in = activate(fine_down(fine_wide, w_down_mid))
    mid_skip = activate(mid_conv(mid_in, unfold(w_mid_enc, 3, C1, C1), MID_CROSS))
    bottom = activate(conv_down(mid_skip, unfold(w_down_bottom, 2, C2, C1)))
    chans, sx, sv, ss = bottom.shape
    flat = bottom.reshape(chans, sx, sv * ss)
    rows = lax.all_to_all(flat, "gx", split_axis=2, concat_axis=1, tiled=True)
    normed = normalize(rows)
    queries = split_heads(w_query, normed)
    keys = split_heads(w_key, normed)
    values = split_heads(w_value, normed)
    result = finish(rows, combine(queries, keys, values), w_attn_out)
    mixed = lax.all_to_all(result, "gx", split_axis=1, concat_axis=2, tiled=True)
    bottom_out = mixed.reshape(chans, sx, sv, ss)
    mid_up = (
        conv_up(bottom_out, unfold(w_up_mid, 2, C2, C1)) + mid_skip.astype(jnp.float32)
    ).astype(jnp.bfloat16)
    mid_dec = activate(mid_conv(mid_up, unfold(w_mid_dec, 3, C1, C1)))
    fine_up_field = (fine_up(mid_dec, w_up_fine) + fine_skip.astype(jnp.float32)).astype(
        jnp.bfloat16
    )
    return fine_conv(fine_up_field, w_fine_dec, FINE_SIDES, head=w_head)


def solution(mesh):
    placed = (P(None, "gx", "gz", "gy"),) + (P(),) * 14
    return jax.shard_map(
        on_device, mesh=mesh, in_specs=placed, out_specs=P(None, "gx", "gz", "gy"), check_vma=False
    )
```

profile of v0, /device:TPU:30, one launch (start us, length us, event | category | flops | bytes accessed | tf_op | source)
XLA Modules:
  0.0 236.8 jit_solution(1671844977699338906)
XLA Ops:
  0.8 8.7 %collective-permute-start = (bf16[4,4,8,128]{3,2,0,1:T(8,128)(2,1)S(1)}, bf16[4,4,8,128]{3,2,0,1:T(8,128)(2,1)S(1)}, u32[]{:S(2)}, u32[]{:S(2)}) collective-permute-start(bf16[4,4,8,128]{3,2,0,1:T(8,128)(2,1)S(1)} %get-tuple-element.25), channel_id=1, source_target_pairs={{0,8},{8,16},{16,24},{24,32},{32,40},{40,48},{48,56},{56,64},{64,7... | collective-permute-start | bytes 98312 | tf_op jit(solution)/shard_map/ppermute | solution.py:33
  11.5 12.0 %collective-permute-done.1 = bf16[4,4,8,128]{3,2,0,1:T(8,128)(2,1)S(1)} collective-permute-done((bf16[4,4,8,128]{3,2,0,1:T(8,128)(2,1)S(1)}, bf16[4,4,8,128]{3,2,0,1:T(8,128)(2,1)S(1)}, u32[]{:S(2)}, u32[]{:S(2)}) %collective-permute-start.1) | collective-permute-done | bytes 32800 | tf_op jit(solution)/shard_map/ppermute | solution.py:34
  33.1 3.2 %collective-permute-done.4 = bf16[16,4,1,130]{3,2,0,1:T(2,128)(2,1)S(1)} collective-permute-done((bf16[16,4,1,130]{3,2,0,1:T(2,128)(2,1)S(1)}, bf16[16,4,1,130]{3,2,0,1:T(2,128)(2,1)S(1)}, u32[]{:S(2)}, u32[]{:S(2)}) %collective-permute-start.4) | collective-permute-done | bytes 16672 | tf_op jit(solution)/shard_map/ppermute | solution.py:34
  37.9 7.2 %shard_map.145 = f32[14,16,8,128]{3,2,1,0:T(8,128)} custom-call(bf16[16,64,256]{2,1,0:T(8,128)(2,1)} %bitcast.130, bf16[27,16,4]{2,1,0:T(8,128)(2,1)} %bitcast.141), custom_call_target="tpu_custom_call" | custom-call | tf_op jit(solution)/shard_map/pallas_call | solution.py:123
  53.8 3.8 %collective-permute-done.6 = bf16[14,16,1,130]{3,2,1,0:T(2,128)(2,1)S(1)} collective-permute-done((bf16[14,16,1,130]{3,2,1,0:T(2,128)(2,1)S(1)}, bf16[14,16,1,130]{3,2,1,0:T(2,128)(2,1)S(1)}, u32[]{:S(2)}, u32[]{:S(2)}) %collective-permute-start.6) | collective-permute-done | bytes 58272 | tf_op jit(solution)/shard_map/ppermute | solution.py:33
  57.6 4.1 %collective-permute-done.7 = bf16[14,16,1,130]{3,2,1,0:T(2,128)(2,1)S(1)} collective-permute-done((bf16[14,16,1,130]{3,2,1,0:T(2,128)(2,1)S(1)}, bf16[14,16,1,130]{3,2,1,0:T(2,128)(2,1)S(1)}, u32[]{:S(2)}, u32[]{:S(2)}) %collective-permute-start.7) | collective-permute-done | bytes 58272 | tf_op jit(solution)/shard_map/ppermute | solution.py:34
  61.7 3.6 %fusion.19 = bf16[14,16,16,256]{3,2,1,0:T(8,128)(2,1)} fusion(bf16[14,16,1,130]{3,2,1,0:T(2,128)(2,1)S(1)} %collective-permute-done.7, bf16[14,16,1,130]{3,2,1,0:T(2,128)(2,1)S(1)} %collective-permute-done.6, bf16[14,16,8,1]{3,2,1,0:T(8,128)(2,1)S(1)} %get-tuple-element.10, bf16[14,16,8,128]{3,2,1,0:T(8,128)(2,1)S(1)} %convert_select_fusion, ...), kind=kLoop, calls=%fused_computation.23 | loop fusion | flops 21102592 | bytes 2417408 | tf_op jit(solution)/shard_map/concatenate | solution.py:35
  65.4 10.4 %shard_map.146 = f32[12,16,8,128]{3,2,1,0:T(8,128)} custom-call(bf16[14,256,256]{2,1,0:T(8,128)(2,1)} %bitcast.127, bf16[27,16,16]{2,1,0:T(8,128)(2,1)} %bitcast.147), custom_call_target="tpu_custom_call" | custom-call | tf_op jit(solution)/shard_map/pallas_call | solution.py:123
  85.0 4.7 %collective-permute-start.9 = (bf16[64,6,1,66]{0,3,2,1:T(8,128)(2,1)S(1)}, bf16[64,6,1,66]{0,3,2,1:T(8,128)(2,1)S(1)}, u32[]{:S(2)}, u32[]{:S(2)}) collective-permute-start(bf16[64,6,1,66]{0,3,2,1:T(8,128)(2,1)S(1)} %get-tuple-element.13), channel_id=1, source_target_pairs={{0,1},{1,2},{2,3},{4,5},{5,6},{6,7},{8,9},{9,10},{10,11},{12,13},{... | collective-permute-start | bytes 152072 | tf_op jit(solution)/shard_map/ppermute | solution.py:33
  93.2 11.9 %fusion.44 = f32[1,64,4,4,64]{1,0,4,3,2:T(1,128)S(1)} fusion(bf16[3,3,3,64,64]{4,3,2,1,0:T(8,128)(2,1)S(1)} %reshape.101, bf16[1,64,6,6,66]{1,4,3,2,0:T(8,128)(2,1)S(1)} %maximum_bitcast_fusion), kind=kOutput, calls=%fused_computation.48 | convolution fusion | flops 226492416 | bytes 787456 | tf_op jit(solution)/shard_map/conv_general_dilated | solution.py:131
  106.4 15.7 %all_to_all.24 = bf16[256,2,64]{0,1,2:T(2,128)(2,1)S(1)} all-to-all(bf16[256,2,64]{0,1,2:T(2,128)(2,1)S(1)} %copy.153), channel_id=1, replica_groups=mesh['gx'=32,'gy'=2,'gz'=4] {'gx'}, dimensions={2} | all-to-all | bytes 131072 | tf_op jit(solution)/shard_map/all_to_all | solution.py:235
  125.7 6.9 %all-to-all-start.1 = ((bf16[256,64,2]{0,2,1:T(2,128)(2,1)}), bf16[256,64,2]{0,2,1:T(2,128)(2,1)S(1)}, u32[]{:S(2)}, u32[]{:S(2)}) async-start(bf16[256,64,2]{0,2,1:T(2,128)(2,1)} %copy.162), calls=%async_computation.1 | async-start | bytes 131072 | tf_op jit(solution)/shard_map/all_to_all | solution.py:241
  133.2 8.6 %all-to-all-done.1 = bf16[256,64,2]{0,2,1:T(2,128)(2,1)S(1)} async-done(((bf16[256,64,2]{0,2,1:T(2,128)(2,1)}), bf16[256,64,2]{0,2,1:T(2,128)(2,1)S(1)}, u32[]{:S(2)}, u32[]{:S(2)}) %all-to-all-start.1) | async-done | bytes 65568 | tf_op jit(solution)/shard_map/all_to_all | solution.py:241
  142.7 5.3 %collective-permute-start.11 = (bf16[64,1,4,64]{0,3,2,1:T(8,128)(2,1)S(1)}, bf16[64,1,4,64]{0,3,2,1:T(8,128)(2,1)S(1)}, u32[]{:S(2)}, u32[]{:S(2)}) collective-permute-start(bf16[64,1,4,64]{0,3,2,1:T(8,128)(2,1)S(1)} %get-tuple-element.21), channel_id=1, source_target_pairs={{0,8},{8,16},{16,24},{24,32},{32,40},{40,48},{48,56},{56,64},{64,7... | collective-permute-start | bytes 98312 | tf_op jit(solution)/shard_map/ppermute | solution.py:33
  149.9 12.4 %collective-permute-done.12 = bf16[64,1,4,64]{0,3,2,1:T(8,128)(2,1)S(1)} collective-permute-done((bf16[64,1,4,64]{0,3,2,1:T(8,128)(2,1)S(1)}, bf16[64,1,4,64]{0,3,2,1:T(8,128)(2,1)S(1)}, u32[]{:S(2)}, u32[]{:S(2)}) %collective-permute-start.12) | collective-permute-done | bytes 32800 | tf_op jit(solution)/shard_map/ppermute | solution.py:34
  163.9 5.4 %collective-permute-start.14 = (bf16[64,6,1,66]{0,3,2,1:T(8,128)(2,1)S(1)}, bf16[64,6,1,66]{0,3,2,1:T(8,128)(2,1)S(1)}, u32[]{:S(2)}, u32[]{:S(2)}) collective-permute-start(bf16[64,6,1,66]{0,3,2,1:T(8,128)(2,1)S(1)} %get-tuple-element.11), channel_id=1, source_target_pairs={{0,1},{1,2},{2,3},{4,5},{5,6},{6,7},{8,9},{9,10},{10,11},{12,13},{... | collective-permute-start | bytes 152072 | tf_op jit(solution)/shard_map/ppermute | solution.py:33
  172.0 4.1 %collective-permute-done.15 = bf16[64,6,1,66]{0,3,2,1:T(8,128)(2,1)S(1)} collective-permute-done((bf16[64,6,1,66]{0,3,2,1:T(8,128)(2,1)S(1)}, bf16[64,6,1,66]{0,3,2,1:T(8,128)(2,1)S(1)}, u32[]{:S(2)}, u32[]{:S(2)}) %collective-permute-start.15) | collective-permute-done | bytes 50720 | tf_op jit(solution)/shard_map/ppermute | solution.py:34
  176.4 11.9 %fusion.42 = f32[1,64,4,4,64]{1,0,4,3,2:T(1,128)S(1)} fusion(bf16[3,3,3,64,64]{4,3,2,1,0:T(8,128)(2,1)S(1)} %reshape.110, bf16[1,64,6,6,66]{1,4,3,2,0:T(8,128)(2,1)S(1)} %maximum_bitcast_fusion.1), kind=kOutput, calls=%fused_computation.46 | convolution fusion | flops 226492416 | bytes 787456 | tf_op jit(solution)/shard_map/conv_general_dilated | solution.py:131
  188.7 4.3 %copy.169 = f32[4,2,16,4,2,64,2]{2,6,5,4,3,1,0:T(2,128)} copy(f32[4,2,16,4,2,64,2]{5,2,6,4,1,3,0:T(8,128)S(1)} %convolution_bitcast_fusion) | data formatting | bytes 1048576 | tf_op jit(solution)/shard_map/ixvs,ioabc->xaovbsc/transpose | solution.py:164
  197.9 3.9 %collective-permute-start.17 = (bf16[1,16,8,128]{3,2,1,0:T(8,128)(2,1)S(1)}, bf16[1,16,8,128]{3,2,1,0:T(8,128)(2,1)S(1)}, u32[]{:S(2)}, u32[]{:S(2)}) collective-permute-start(bf16[1,16,8,128]{3,2,1,0:T(8,128)(2,1)S(1)} %get-tuple-element.20), channel_id=1, source_target_pairs={{8,0},{16,8},{24,16},{32,24},{40,32},{48,40},{56,48},{64,56},{72,6... | collective-permute-start | bytes 98312 | tf_op jit(solution)/shard_map/ppermute | solution.py:34
  201.9 10.0 %collective-permute-done.17 = bf16[1,16,8,128]{3,2,1,0:T(8,128)(2,1)S(1)} collective-permute-done((bf16[1,16,8,128]{3,2,1,0:T(8,128)(2,1)S(1)}, bf16[1,16,8,128]{3,2,1,0:T(8,128)(2,1)S(1)}, u32[]{:S(2)}, u32[]{:S(2)}) %collective-permute-start.17) | collective-permute-done | bytes 32800 | tf_op jit(solution)/shard_map/ppermute | solution.py:34
  220.6 4.1 %collective-permute-done.20 = bf16[10,16,1,130]{3,2,1,0:T(2,128)(2,1)S(1)} collective-permute-done((bf16[10,16,1,130]{3,2,1,0:T(2,128)(2,1)S(1)}, bf16[10,16,1,130]{3,2,1,0:T(2,128)(2,1)S(1)}, u32[]{:S(2)}, u32[]{:S(2)}) %collective-permute-start.20) | collective-permute-done | bytes 41632 | tf_op jit(solution)/shard_map/ppermute | solution.py:34
  224.7 3.2 %fusion.28 = bf16[10,16,16,256]{3,2,1,0:T(8,128)(2,1)} fusion(bf16[10,16,1,130]{3,2,1,0:T(2,128)(2,1)S(1)} %collective-permute-done.20, bf16[10,16,1,130]{3,2,1,0:T(2,128)(2,1)S(1)} %collective-permute-done.19, bf16[10,16,8,1]{3,2,1,0:T(8,128)(2,1)S(1)} %get-tuple-element.18, bf16[10,16,8,1]{3,2,1,0:T(8,128)(2,1)S(1)} %get-tuple-element.17, ...), kind=kLoop, calls=%fused_computation.33 | loop fusion | flops 20316160 | bytes 1726720 | tf_op jit(solution)/shard_map/concatenate | solution.py:35
  227.9 8.9 %shard_map.147 = f32[4,8,8,128]{3,2,1,0:T(8,128)} custom-call(bf16[10,256,256]{2,1,0:T(8,128)(2,1)} %bitcast.128, bf16[27,16,16]{2,1,0:T(8,128)(2,1)} %bitcast.146, bf16[32,128]{1,0:T(8,128)(2,1)} %convert_element_type.129.refs_2_), custom_call_target="tpu_custom_call" | custom-call | tf_op jit(solution)/shard_map/pallas_call | solution.py:123
  (132 shorter events, 61.5 us)
Async XLA Ops:
  0.0 122.7 %copy-start = (bf16[256,256]{1,0:T(8,128)(2,1)S(1)}, bf16[256,256]{1,0:T(8,128)(2,1)}, u32[]{:S(2)}) copy-start(bf16[256,256]{1,0:T(8,128)(2,1)} %param.22) | copy-start | bytes 393220
  0.0 36.4 %copy-start.3 = (bf16[4,8,8,128]{3,2,1,0:T(8,128)(2,1)S(1)}, bf16[4,8,8,128]{3,2,1,0:T(8,128)(2,1)}, u32[]{:S(2)}) copy-start(bf16[4,8,8,128]{3,2,1,0:T(8,128)(2,1)} %param.15) | copy-start | bytes 196612
  0.8 10.6 %collective-permute-start = (bf16[4,4,8,128]{3,2,0,1:T(8,128)(2,1)S(1)}, bf16[4,4,8,128]{3,2,0,1:T(8,128)(2,1)S(1)}, u32[]{:S(2)}, u32[]{:S(2)}) collective-permute-start(bf16[4,4,8,128]{3,2,0,1:T(8,128)(2,1)S(1)} %get-tuple-element.25), channel_id=1, source_target_pairs={{0,8},{8,16},{16,24},{24,32},{32,40},{40,48},{48,56},{56,64},{64,7... | collective-permute-start | bytes 98312 | tf_op jit(solution)/shard_map/ppermute | solution.py:33
  9.5 13.9 %collective-permute-start.1 = (bf16[4,4,8,128]{3,2,0,1:T(8,128)(2,1)S(1)}, bf16[4,4,8,128]{3,2,0,1:T(8,128)(2,1)S(1)}, u32[]{:S(2)}, u32[]{:S(2)}) collective-permute-start(bf16[4,4,8,128]{3,2,0,1:T(8,128)(2,1)S(1)} %get-tuple-element.26), channel_id=1, source_target_pairs={{8,0},{16,8},{24,16},{32,24},{40,32},{48,40},{56,48},{64,56},{72,6... | collective-permute-start | bytes 98312 | tf_op jit(solution)/shard_map/ppermute | solution.py:34
  24.4 1.4 collective-permute-start.2
  27.1 6.0 %collective-permute-start.3 = (bf16[16,4,1,130]{3,2,0,1:T(2,128)(2,1)S(1)}, bf16[16,4,1,130]{3,2,0,1:T(2,128)(2,1)S(1)}, u32[]{:S(2)}, u32[]{:S(2)}) collective-permute-start(bf16[16,4,1,130]{3,2,0,1:T(2,128)(2,1)S(1)} %get-tuple-element.15), channel_id=1, source_target_pairs={{0,1},{1,2},{2,3},{4,5},{5,6},{6,7},{8,9},{9,10},{10,11},{12,13},{... | collective-permute-start | bytes 49928 | tf_op jit(solution)/shard_map/ppermute | solution.py:33
  30.2 6.2 %collective-permute-start.4 = (bf16[16,4,1,130]{3,2,0,1:T(2,128)(2,1)S(1)}, bf16[16,4,1,130]{3,2,0,1:T(2,128)(2,1)S(1)}, u32[]{:S(2)}, u32[]{:S(2)}) collective-permute-start(bf16[16,4,1,130]{3,2,0,1:T(2,128)(2,1)S(1)} %get-tuple-element.16), channel_id=1, source_target_pairs={{1,0},{2,1},{3,2},{5,4},{6,5},{7,6},{9,8},{10,9},{11,10},{13,12},{... | collective-permute-start | bytes 49928 | tf_op jit(solution)/shard_map/ppermute | solution.py:34
  46.5 1.9 collective-permute-start.5
  49.6 8.0 %collective-permute-start.6 = (bf16[14,16,1,130]{3,2,1,0:T(2,128)(2,1)S(1)}, bf16[14,16,1,130]{3,2,1,0:T(2,128)(2,1)S(1)}, u32[]{:S(2)}, u32[]{:S(2)}) collective-permute-start(bf16[14,16,1,130]{3,2,1,0:T(2,128)(2,1)S(1)} %get-tuple-element.5), channel_id=1, source_target_pairs={{0,1},{1,2},{2,3},{4,5},{5,6},{6,7},{8,9},{9,10},{10,11},{12,13},{... | collective-permute-start | bytes 174728 | tf_op jit(solution)/shard_map/ppermute | solution.py:33
  52.5 9.3 %collective-permute-start.7 = (bf16[14,16,1,130]{3,2,1,0:T(2,128)(2,1)S(1)}, bf16[14,16,1,130]{3,2,1,0:T(2,128)(2,1)S(1)}, u32[]{:S(2)}, u32[]{:S(2)}) collective-permute-start(bf16[14,16,1,130]{3,2,1,0:T(2,128)(2,1)S(1)} %get-tuple-element.6), channel_id=1, source_target_pairs={{1,0},{2,1},{3,2},{5,4},{6,5},{7,6},{9,8},{10,9},{11,10},{13,12},{... | collective-permute-start | bytes 174728 | tf_op jit(solution)/shard_map/ppermute | solution.py:34
  82.3 1.3 collective-permute-start.8
  83.7 8.0 %collective-permute-start.10 = (bf16[64,6,1,66]{0,3,2,1:T(8,128)(2,1)S(1)}, bf16[64,6,1,66]{0,3,2,1:T(8,128)(2,1)S(1)}, u32[]{:S(2)}, u32[]{:S(2)}) collective-permute-start(bf16[64,6,1,66]{0,3,2,1:T(8,128)(2,1)S(1)} %get-tuple-element.14), channel_id=1, source_target_pairs={{1,0},{2,1},{3,2},{5,4},{6,5},{7,6},{9,8},{10,9},{11,10},{13,12},{... | collective-permute-start | bytes 152072 | tf_op jit(solution)/shard_map/ppermute | solution.py:34
  85.0 6.9 %collective-permute-start.9 = (bf16[64,6,1,66]{0,3,2,1:T(8,128)(2,1)S(1)}, bf16[64,6,1,66]{0,3,2,1:T(8,128)(2,1)S(1)}, u32[]{:S(2)}, u32[]{:S(2)}) collective-permute-start(bf16[64,6,1,66]{0,3,2,1:T(8,128)(2,1)S(1)} %get-tuple-element.13), channel_id=1, source_target_pairs={{0,1},{1,2},{2,3},{4,5},{5,6},{6,7},{8,9},{9,10},{10,11},{12,13},{... | collective-permute-start | bytes 152072 | tf_op jit(solution)/shard_map/ppermute | solution.py:33
  125.7 16.1 %all-to-all-start.1 = ((bf16[256,64,2]{0,2,1:T(2,128)(2,1)}), bf16[256,64,2]{0,2,1:T(2,128)(2,1)S(1)}, u32[]{:S(2)}, u32[]{:S(2)}) async-start(bf16[256,64,2]{0,2,1:T(2,128)(2,1)} %copy.162), calls=%async_computation.1 | async-start | bytes 131072 | tf_op jit(solution)/shard_map/all_to_all | solution.py:241
  142.7 7.2 %collective-permute-start.11 = (bf16[64,1,4,64]{0,3,2,1:T(8,128)(2,1)S(1)}, bf16[64,1,4,64]{0,3,2,1:T(8,128)(2,1)S(1)}, u32[]{:S(2)}, u32[]{:S(2)}) collective-permute-start(bf16[64,1,4,64]{0,3,2,1:T(8,128)(2,1)S(1)} %get-tuple-element.21), channel_id=1, source_target_pairs={{0,8},{8,16},{16,24},{24,32},{32,40},{40,48},{48,56},{56,64},{64,7... | collective-permute-start | bytes 98312 | tf_op jit(solution)/shard_map/ppermute | solution.py:33
  148.0 14.3 %collective-permute-start.12 = (bf16[64,1,4,64]{0,3,2,1:T(8,128)(2,1)S(1)}, bf16[64,1,4,64]{0,3,2,1:T(8,128)(2,1)S(1)}, u32[]{:S(2)}, u32[]{:S(2)}) collective-permute-start(bf16[64,1,4,64]{0,3,2,1:T(8,128)(2,1)S(1)} %get-tuple-element.22), channel_id=1, source_target_pairs={{8,0},{16,8},{24,16},{32,24},{40,32},{48,40},{56,48},{64,56},{72,6... | collective-permute-start | bytes 98312 | tf_op jit(solution)/shard_map/ppermute | solution.py:34
  162.3 1.5 collective-permute-start.13
  163.9 8.1 %collective-permute-start.14 = (bf16[64,6,1,66]{0,3,2,1:T(8,128)(2,1)S(1)}, bf16[64,6,1,66]{0,3,2,1:T(8,128)(2,1)S(1)}, u32[]{:S(2)}, u32[]{:S(2)}) collective-permute-start(bf16[64,6,1,66]{0,3,2,1:T(8,128)(2,1)S(1)} %get-tuple-element.11), channel_id=1, source_target_pairs={{0,1},{1,2},{2,3},{4,5},{5,6},{6,7},{8,9},{9,10},{10,11},{12,13},{... | collective-permute-start | bytes 152072 | tf_op jit(solution)/shard_map/ppermute | solution.py:33
  169.4 6.7 %collective-permute-start.15 = (bf16[64,6,1,66]{0,3,2,1:T(8,128)(2,1)S(1)}, bf16[64,6,1,66]{0,3,2,1:T(8,128)(2,1)S(1)}, u32[]{:S(2)}, u32[]{:S(2)}) collective-permute-start(bf16[64,6,1,66]{0,3,2,1:T(8,128)(2,1)S(1)} %get-tuple-element.12), channel_id=1, source_target_pairs={{1,0},{2,1},{3,2},{5,4},{6,5},{7,6},{9,8},{10,9},{11,10},{13,12},{... | collective-permute-start | bytes 152072 | tf_op jit(solution)/shard_map/ppermute | solution.py:34
  196.0 5.9 %collective-permute-start.16 = (bf16[1,16,8,128]{3,2,1,0:T(8,128)(2,1)S(1)}, bf16[1,16,8,128]{3,2,1,0:T(8,128)(2,1)S(1)}, u32[]{:S(2)}, u32[]{:S(2)}) collective-permute-start(bf16[1,16,8,128]{3,2,1,0:T(8,128)(2,1)S(1)} %get-tuple-element.19), channel_id=1, source_target_pairs={{0,8},{8,16},{16,24},{24,32},{32,40},{40,48},{48,56},{56,64},{64,7... | collective-permute-start | bytes 98312 | tf_op jit(solution)/shard_map/ppermute | solution.py:33
  197.9 13.9 %collective-permute-start.17 = (bf16[1,16,8,128]{3,2,1,0:T(8,128)(2,1)S(1)}, bf16[1,16,8,128]{3,2,1,0:T(8,128)(2,1)S(1)}, u32[]{:S(2)}, u32[]{:S(2)}) collective-permute-start(bf16[1,16,8,128]{3,2,1,0:T(8,128)(2,1)S(1)} %get-tuple-element.20), channel_id=1, source_target_pairs={{8,0},{16,8},{24,16},{32,24},{40,32},{48,40},{56,48},{64,56},{72,6... | collective-permute-start | bytes 98312 | tf_op jit(solution)/shard_map/ppermute | solution.py:34
  212.1 1.7 collective-permute-start.18
  214.6 5.9 %collective-permute-start.19 = (bf16[10,16,1,130]{3,2,1,0:T(2,128)(2,1)S(1)}, bf16[10,16,1,130]{3,2,1,0:T(2,128)(2,1)S(1)}, u32[]{:S(2)}, u32[]{:S(2)}) collective-permute-start(bf16[10,16,1,130]{3,2,1,0:T(2,128)(2,1)S(1)} %get-tuple-element.7), channel_id=1, source_target_pairs={{0,1},{1,2},{2,3},{4,5},{5,6},{6,7},{8,9},{9,10},{10,11},{12,13},{... | collective-permute-start | bytes 124808 | tf_op jit(solution)/shard_map/ppermute | solution.py:33
  216.9 7.9 %collective-permute-start.20 = (bf16[10,16,1,130]{3,2,1,0:T(2,128)(2,1)S(1)}, bf16[10,16,1,130]{3,2,1,0:T(2,128)(2,1)S(1)}, u32[]{:S(2)}, u32[]{:S(2)}) collective-permute-start(bf16[10,16,1,130]{3,2,1,0:T(2,128)(2,1)S(1)} %get-tuple-element.8), channel_id=1, source_target_pairs={{1,0},{2,1},{3,2},{5,4},{6,5},{7,6},{9,8},{10,9},{11,10},{13,12},{... | collective-permute-start | bytes 124808 | tf_op jit(solution)/shard_map/ppermute | solution.py:34
  (10 other events, 116.8 us)
where the time goes:
time: 238 us; the launch traced here: 237 us
  waiting for transfers between devices  71.7 us (30%)
  starting transfers between devices  56.2 us (24%)
  matrix products  27.8 us (12%)
  Pallas kernels  26.5 us (11%)
  local copies, waits for them, and re-layouts  20 us (8%)
  other arithmetic  18 us (8%)
  blocking collectives  15.7 us (7%)
    ppermute x8, waiting for transfers between devices, extended(): high = lax.ppermute(bottom, axis, backward)  49.9 us
    ppermute x8, starting transfers between devices, extended(): low = lax.ppermute(top, axis, forward)  34.1 us
    pallas_call x3, Pallas kernels, fine_conv(): pl.pallas_call(kernel, out_shape=out_shape, scratch_shapes=[pltpu.VMEM((9...  26.5 us
    conv_general_dilated x2, matrix products, conv_valid(): lax.conv_general_dilated(padded[None], weight, (1, 1, 1), 'VALID', dimens...  23.8 us
    all_to_all x1, blocking collectives, on_device(): rows = lax.all_to_all(flat, 'gx', split_axis=2, concat_axis=1, tiled=True)  15.7 us
    ppermute x8, starting transfers between devices, extended(): high = lax.ppermute(bottom, axis, backward)  14.5 us
    all_to_all x1, waiting for transfers between devices, on_device(): lax.all_to_all(result, 'gx', split_axis=1, concat_axis=2, tiled=True)  8.59 us
    concatenate x5, other arithmetic, extended(): block = jnp.concatenate([low, block, high], axis=dim)  8.28 us
  transfers between devices with their start and end apart: 22, of which 17 were waited for; matrix products, arithmetic and copies ran while one was open for 2% of the time, Pallas kernels for 0%

commit v1 on v0

--- a/solution.py
+++ b/solution.py
@@ -54,9 +54,9 @@
 
 def fine_kernel(p_ref, w_ref, *rest, sx, sv, ss, rows, head):
     if head:
-        h_ref, o_ref, band_ref = rest
+        h_ref, o_ref, band_ref, shifted_ref = rest
     else:
-        o_ref, band_ref = rest
+        o_ref, band_ref, shifted_ref = rest
     cout, cin = w_ref.shape[1:]
     depth = cin * rows
     lanes = p_ref.shape[-1]
@@ -80,15 +80,20 @@
                     grown.astype(jnp.bfloat16), widen_cols, preferred_element_type=jnp.float32
                 )
                 band = band + jnp.where(offset == b, grown, 0.0)
-            band_ref[a * 3 + c] = band.astype(jnp.bfloat16)
+            band_ref[:, pl.ds((a * 3 + c) * depth, depth)] = band.astype(jnp.bfloat16)
+
+    def shift(x, carry):
+        slab = p_ref[x].astype(jnp.float32)
+        for c in range(3):
+            piece = slab if c == 0 else pltpu.roll(slab, lanes - c, 1)
+            shifted_ref[x, c] = piece[:, :ss].astype(jnp.bfloat16)
+        return carry
+
+    lax.fori_loop(0, sx + 2, shift, 0)
+
     def row(x, carry):
-        acc = jnp.zeros((cout * sv, ss), jnp.float32)
-        for a in range(3):
-            slab = p_ref[x + a].astype(jnp.float32)
-            for c in range(3):
-                piece = slab if c == 0 else pltpu.roll(slab, lanes - c, 1)
-                piece = piece[:, :ss].astype(jnp.bfloat16)
-                acc = acc + jnp.dot(band_ref[a * 3 + c], piece, preferred_element_type=jnp.float32)
+        stack = shifted_ref[pl.ds(x, 3)].reshape(9 * depth, ss)
+        acc = jnp.dot(band_ref[...], stack, preferred_element_type=jnp.float32)
         act = (acc * jax.nn.sigmoid(acc)).astype(jnp.bfloat16)
         if head:
             res = jnp.dot(h_ref[...], act, preferred_element_type=jnp.float32)
@@ -105,11 +110,15 @@
     cout = weight.shape[0]
     rows = round_up(sv + 2, 16)
     lanes = round_up(ss + 2, 128)
+    wide = round_up(cin * rows, 128) // rows
     padded = extended(field, sides)
     sx = padded.shape[0] - 2
-    padded = jnp.pad(padded, ((0, 0), (0, 0), (0, rows - sv - 2), (0, lanes - ss - 2)))
-    padded = padded.reshape(sx + 2, cin * rows, lanes)
-    operands = [padded, weight.transpose(2, 3, 4, 0, 1).reshape(27, cout, cin)]
+    padded = jnp.pad(
+        padded, ((0, 0), (0, wide - cin), (0, rows - sv - 2), (0, lanes - ss - 2))
+    )
+    padded = padded.reshape(sx + 2, wide * rows, lanes)
+    taps = jnp.pad(weight, ((0, 0), (0, wide - cin), (0, 0), (0, 0), (0, 0)))
+    operands = [padded, taps.transpose(2, 3, 4, 0, 1).reshape(27, cout, wide)]
     if head is None:
         out_shape = jax.ShapeDtypeStruct((sx, cout, sv, ss), jnp.float32)
     else:
@@ -123,7 +132,10 @@
     return pl.pallas_call(
         kernel,
         out_shape=out_shape,
-        scratch_shapes=[pltpu.VMEM((9, cout * sv, cin * rows), jnp.bfloat16)],
+        scratch_shapes=[
+            pltpu.VMEM((cout * sv, 9 * wide * rows), jnp.bfloat16),
+            pltpu.VMEM((sx + 2, 3, wide * rows, ss), jnp.bfloat16),
+        ],
     )(*operands)
 
 

time: 238 us -> 239 us (level)
  no operation moved by 1% of the time
where the time goes in v1:
time: 239 us; the launch traced here: 238 us
  waiting for transfers between devices  71.9 us (30%)
  starting transfers between devices  56.2 us (24%)
  matrix products  27.8 us (12%)
  Pallas kernels  27.7 us (12%)
  local copies, waits for them, and re-layouts  20.2 us (8%)
  other arithmetic  18 us (8%)
  blocking collectives  15.7 us (7%)
    ppermute x8, waiting for transfers between devices, extended(): high = lax.ppermute(bottom, axis, backward)  50.8 us
    ppermute x8, starting transfers between devices, extended(): low = lax.ppermute(top, axis, forward)  34.1 us
    pallas_call x3, Pallas kernels, fine_conv(): pl.pallas_call(kernel, out_shape=out_shape, scratch_shapes=[pltpu.VMEM((c...  27.7 us
    conv_general_dilated x2, matrix products, conv_valid(): lax.conv_general_dilated(padded[None], weight, (1, 1, 1), 'VALID', dimens...  23.8 us
    all_to_all x1, blocking collectives, on_device(): rows = lax.all_to_all(flat, 'gx', split_axis=2, concat_axis=1, tiled=True)  15.7 us
    ppermute x8, starting transfers between devices, extended(): high = lax.ppermute(bottom, axis, backward)  14.5 us
    all_to_all x1, waiting for transfers between devices, on_device(): lax.all_to_all(result, 'gx', split_axis=1, concat_axis=2, tiled=True)  8.59 us
    concatenate x5, other arithmetic, extended(): block = jnp.concatenate([low, block, high], axis=dim)  8.29 us
  transfers between devices with their start and end apart: 22, of which 17 were waited for; matrix products, arithmetic and copies ran while one was open for 2% of the time, Pallas kernels for 0%

profile of v1, /device:TPU:30, one launch (start us, length us, event | category | flops | bytes accessed | tf_op | source)
XLA Modules:
  0.0 238.3 jit_solution(9598966388796353691)
XLA Ops:
  0.8 8.7 %collective-permute-start = (bf16[4,4,8,128]{3,2,0,1:T(8,128)(2,1)S(1)}, bf16[4,4,8,128]{3,2,0,1:T(8,128)(2,1)S(1)}, u32[]{:S(2)}, u32[]{:S(2)}) collective-permute-start(bf16[4,4,8,128]{3,2,0,1:T(8,128)(2,1)S(1)} %get-tuple-element.25), channel_id=1, source_target_pairs={{0,8},{8,16},{16,24},{24,32},{32,40},{40,48},{48,56},{56,64},{64,7... | collective-permute-start | bytes 98312 | tf_op jit(solution)/shard_map/ppermute | solution.py:33
  11.5 12.0 %collective-permute-done.1 = bf16[4,4,8,128]{3,2,0,1:T(8,128)(2,1)S(1)} collective-permute-done((bf16[4,4,8,128]{3,2,0,1:T(8,128)(2,1)S(1)}, bf16[4,4,8,128]{3,2,0,1:T(8,128)(2,1)S(1)}, u32[]{:S(2)}, u32[]{:S(2)}) %collective-permute-start.1) | collective-permute-done | bytes 32800 | tf_op jit(solution)/shard_map/ppermute | solution.py:34
  32.3 4.1 %collective-permute-done.4 = bf16[16,4,1,130]{3,2,0,1:T(2,128)(2,1)S(1)} collective-permute-done((bf16[16,4,1,130]{3,2,0,1:T(2,128)(2,1)S(1)}, bf16[16,4,1,130]{3,2,0,1:T(2,128)(2,1)S(1)}, u32[]{:S(2)}, u32[]{:S(2)}) %collective-permute-start.4) | collective-permute-done | bytes 16672 | tf_op jit(solution)/shard_map/ppermute | solution.py:34
  38.1 7.9 %shard_map.145 = f32[14,16,8,128]{3,2,1,0:T(8,128)} custom-call(bf16[16,128,256]{2,1,0:T(8,128)(2,1)} %bitcast.130, bf16[27,16,8]{2,1,0:T(8,128)(2,1)} %bitcast.142), custom_call_target="tpu_custom_call" | custom-call | tf_op jit(solution)/shard_map/pallas_call | solution.py:132
  54.8 3.8 %collective-permute-done.6 = bf16[14,16,1,130]{3,2,1,0:T(2,128)(2,1)S(1)} collective-permute-done((bf16[14,16,1,130]{3,2,1,0:T(2,128)(2,1)S(1)}, bf16[14,16,1,130]{3,2,1,0:T(2,128)(2,1)S(1)}, u32[]{:S(2)}, u32[]{:S(2)}) %collective-permute-start.6) | collective-permute-done | bytes 58272 | tf_op jit(solution)/shard_map/ppermute | solution.py:33
  58.6 4.1 %collective-permute-done.7 = bf16[14,16,1,130]{3,2,1,0:T(2,128)(2,1)S(1)} collective-permute-done((bf16[14,16,1,130]{3,2,1,0:T(2,128)(2,1)S(1)}, bf16[14,16,1,130]{3,2,1,0:T(2,128)(2,1)S(1)}, u32[]{:S(2)}, u32[]{:S(2)}) %collective-permute-start.7) | collective-permute-done | bytes 58272 | tf_op jit(solution)/shard_map/ppermute | solution.py:34
  62.8 3.6 %fusion.19 = bf16[14,16,16,256]{3,2,1,0:T(8,128)(2,1)} fusion(bf16[14,16,1,130]{3,2,1,0:T(2,128)(2,1)S(1)} %collective-permute-done.7, bf16[14,16,1,130]{3,2,1,0:T(2,128)(2,1)S(1)} %collective-permute-done.6, bf16[14,16,8,1]{3,2,1,0:T(8,128)(2,1)S(1)} %get-tuple-element.10, bf16[14,16,8,128]{3,2,1,0:T(8,128)(2,1)S(1)} %convert_select_fusion, ...), kind=kLoop, calls=%fused_computation.23 | loop fusion | flops 21102592 | bytes 2417408 | tf_op jit(solution)/shard_map/concatenate | solution.py:35
  66.4 10.5 %shard_map.146 = f32[12,16,8,128]{3,2,1,0:T(8,128)} custom-call(bf16[14,256,256]{2,1,0:T(8,128)(2,1)} %bitcast.128, bf16[27,16,16]{2,1,0:T(8,128)(2,1)} %bitcast.148), custom_call_target="tpu_custom_call" | custom-call | tf_op jit(solution)/shard_map/pallas_call | solution.py:132
  86.2 4.7 %collective-permute-start.9 = (bf16[64,6,1,66]{0,3,2,1:T(8,128)(2,1)S(1)}, bf16[64,6,1,66]{0,3,2,1:T(8,128)(2,1)S(1)}, u32[]{:S(2)}, u32[]{:S(2)}) collective-permute-start(bf16[64,6,1,66]{0,3,2,1:T(8,128)(2,1)S(1)} %get-tuple-element.13), channel_id=1, source_target_pairs={{0,1},{1,2},{2,3},{4,5},{5,6},{6,7},{8,9},{9,10},{10,11},{12,13},{... | collective-permute-start | bytes 152072 | tf_op jit(solution)/shard_map/ppermute | solution.py:33
  94.3 11.9 %fusion.44 = f32[1,64,4,4,64]{1,0,4,3,2:T(1,128)S(1)} fusion(bf16[3,3,3,64,64]{4,3,2,1,0:T(8,128)(2,1)S(1)} %reshape.101, bf16[1,64,6,6,66]{1,4,3,2,0:T(8,128)(2,1)S(1)} %maximum_bitcast_fusion), kind=kOutput, calls=%fused_computation.48 | convolution fusion | flops 226492416 | bytes 787456 | tf_op jit(solution)/shard_map/conv_general_dilated | solution.py:143
  107.6 15.7 %all_to_all.24 = bf16[256,2,64]{0,1,2:T(2,128)(2,1)S(1)} all-to-all(bf16[256,2,64]{0,1,2:T(2,128)(2,1)S(1)} %copy.153), channel_id=1, replica_groups=mesh['gx'=32,'gy'=2,'gz'=4] {'gx'}, dimensions={2} | all-to-all | bytes 131072 | tf_op jit(solution)/shard_map/all_to_all | solution.py:247
  126.8 6.9 %all-to-all-start.1 = ((bf16[256,64,2]{0,2,1:T(2,128)(2,1)}), bf16[256,64,2]{0,2,1:T(2,128)(2,1)S(1)}, u32[]{:S(2)}, u32[]{:S(2)}) async-start(bf16[256,64,2]{0,2,1:T(2,128)(2,1)} %copy.162), calls=%async_computation.1 | async-start | bytes 131072 | tf_op jit(solution)/shard_map/all_to_all | solution.py:253
  134.3 8.6 %all-to-all-done.1 = bf16[256,64,2]{0,2,1:T(2,128)(2,1)S(1)} async-done(((bf16[256,64,2]{0,2,1:T(2,128)(2,1)}), bf16[256,64,2]{0,2,1:T(2,128)(2,1)S(1)}, u32[]{:S(2)}, u32[]{:S(2)}) %all-to-all-start.1) | async-done | bytes 65568 | tf_op jit(solution)/shard_map/all_to_all | solution.py:253
  143.8 5.3 %collective-permute-start.11 = (bf16[64,1,4,64]{0,3,2,1:T(8,128)(2,1)S(1)}, bf16[64,1,4,64]{0,3,2,1:T(8,128)(2,1)S(1)}, u32[]{:S(2)}, u32[]{:S(2)}) collective-permute-start(bf16[64,1,4,64]{0,3,2,1:T(8,128)(2,1)S(1)} %get-tuple-element.21), channel_id=1, source_target_pairs={{0,8},{8,16},{16,24},{24,32},{32,40},{40,48},{48,56},{56,64},{64,7... | collective-permute-start | bytes 98312 | tf_op jit(solution)/shard_map/ppermute | solution.py:33
  151.0 12.4 %collective-permute-done.12 = bf16[64,1,4,64]{0,3,2,1:T(8,128)(2,1)S(1)} collective-permute-done((bf16[64,1,4,64]{0,3,2,1:T(8,128)(2,1)S(1)}, bf16[64,1,4,64]{0,3,2,1:T(8,128)(2,1)S(1)}, u32[]{:S(2)}, u32[]{:S(2)}) %collective-permute-start.12) | collective-permute-done | bytes 32800 | tf_op jit(solution)/shard_map/ppermute | solution.py:34
  165.1 5.4 %collective-permute-start.14 = (bf16[64,6,1,66]{0,3,2,1:T(8,128)(2,1)S(1)}, bf16[64,6,1,66]{0,3,2,1:T(8,128)(2,1)S(1)}, u32[]{:S(2)}, u32[]{:S(2)}) collective-permute-start(bf16[64,6,1,66]{0,3,2,1:T(8,128)(2,1)S(1)} %get-tuple-element.11), channel_id=1, source_target_pairs={{0,1},{1,2},{2,3},{4,5},{5,6},{6,7},{8,9},{9,10},{10,11},{12,13},{... | collective-permute-start | bytes 152072 | tf_op jit(solution)/shard_map/ppermute | solution.py:33
  173.1 4.1 %collective-permute-done.15 = bf16[64,6,1,66]{0,3,2,1:T(8,128)(2,1)S(1)} collective-permute-done((bf16[64,6,1,66]{0,3,2,1:T(8,128)(2,1)S(1)}, bf16[64,6,1,66]{0,3,2,1:T(8,128)(2,1)S(1)}, u32[]{:S(2)}, u32[]{:S(2)}) %collective-permute-start.15) | collective-permute-done | bytes 50720 | tf_op jit(solution)/shard_map/ppermute | solution.py:34
  177.5 11.9 %fusion.42 = f32[1,64,4,4,64]{1,0,4,3,2:T(1,128)S(1)} fusion(bf16[3,3,3,64,64]{4,3,2,1,0:T(8,128)(2,1)S(1)} %reshape.110, bf16[1,64,6,6,66]{1,4,3,2,0:T(8,128)(2,1)S(1)} %maximum_bitcast_fusion.1), kind=kOutput, calls=%fused_computation.46 | convolution fusion | flops 226492416 | bytes 787456 | tf_op jit(solution)/shard_map/conv_general_dilated | solution.py:143
  189.8 4.3 %copy.169 = f32[4,2,16,4,2,64,2]{2,6,5,4,3,1,0:T(2,128)} copy(f32[4,2,16,4,2,64,2]{5,2,6,4,1,3,0:T(8,128)S(1)} %convolution_bitcast_fusion) | data formatting | bytes 1048576 | tf_op jit(solution)/shard_map/ixvs,ioabc->xaovbsc/transpose | solution.py:176
  199.1 3.9 %collective-permute-start.17 = (bf16[1,16,8,128]{3,2,1,0:T(8,128)(2,1)S(1)}, bf16[1,16,8,128]{3,2,1,0:T(8,128)(2,1)S(1)}, u32[]{:S(2)}, u32[]{:S(2)}) collective-permute-start(bf16[1,16,8,128]{3,2,1,0:T(8,128)(2,1)S(1)} %get-tuple-element.20), channel_id=1, source_target_pairs={{8,0},{16,8},{24,16},{32,24},{40,32},{48,40},{56,48},{64,56},{72,6... | collective-permute-start | bytes 98312 | tf_op jit(solution)/shard_map/ppermute | solution.py:34
  203.0 10.0 %collective-permute-done.17 = bf16[1,16,8,128]{3,2,1,0:T(8,128)(2,1)S(1)} collective-permute-done((bf16[1,16,8,128]{3,2,1,0:T(8,128)(2,1)S(1)}, bf16[1,16,8,128]{3,2,1,0:T(8,128)(2,1)S(1)}, u32[]{:S(2)}, u32[]{:S(2)}) %collective-permute-start.17) | collective-permute-done | bytes 32800 | tf_op jit(solution)/shard_map/ppermute | solution.py:34
  221.7 4.1 %collective-permute-done.20 = bf16[10,16,1,130]{3,2,1,0:T(2,128)(2,1)S(1)} collective-permute-done((bf16[10,16,1,130]{3,2,1,0:T(2,128)(2,1)S(1)}, bf16[10,16,1,130]{3,2,1,0:T(2,128)(2,1)S(1)}, u32[]{:S(2)}, u32[]{:S(2)}) %collective-permute-start.20) | collective-permute-done | bytes 41632 | tf_op jit(solution)/shard_map/ppermute | solution.py:34
  225.8 3.2 %fusion.28 = bf16[10,16,16,256]{3,2,1,0:T(8,128)(2,1)} fusion(bf16[10,16,1,130]{3,2,1,0:T(2,128)(2,1)S(1)} %collective-permute-done.20, bf16[10,16,1,130]{3,2,1,0:T(2,128)(2,1)S(1)} %collective-permute-done.19, bf16[10,16,8,1]{3,2,1,0:T(8,128)(2,1)S(1)} %get-tuple-element.18, bf16[10,16,8,1]{3,2,1,0:T(8,128)(2,1)S(1)} %get-tuple-element.17, ...), kind=kLoop, calls=%fused_computation.33 | loop fusion | flops 20316160 | bytes 1726720 | tf_op jit(solution)/shard_map/concatenate | solution.py:35
  229.0 9.2 %shard_map.147 = f32[4,8,8,128]{3,2,1,0:T(8,128)} custom-call(bf16[10,256,256]{2,1,0:T(8,128)(2,1)} %bitcast.129, bf16[27,16,16]{2,1,0:T(8,128)(2,1)} %bitcast.147, bf16[32,128]{1,0:T(8,128)(2,1)} %convert_element_type.131.refs_2_), custom_call_target="tpu_custom_call" | custom-call | tf_op jit(solution)/shard_map/pallas_call | solution.py:132
  (133 shorter events, 60.9 us)
Async XLA Ops:
  0.0 123.8 %copy-start = (bf16[256,256]{1,0:T(8,128)(2,1)S(1)}, bf16[256,256]{1,0:T(8,128)(2,1)}, u32[]{:S(2)}) copy-start(bf16[256,256]{1,0:T(8,128)(2,1)} %param.22) | copy-start | bytes 393220
  0.0 36.4 %copy-start.3 = (bf16[4,8,8,128]{3,2,1,0:T(8,128)(2,1)S(1)}, bf16[4,8,8,128]{3,2,1,0:T(8,128)(2,1)}, u32[]{:S(2)}) copy-start(bf16[4,8,8,128]{3,2,1,0:T(8,128)(2,1)} %param.15) | copy-start | bytes 196612
  0.8 10.6 %collective-permute-start = (bf16[4,4,8,128]{3,2,0,1:T(8,128)(2,1)S(1)}, bf16[4,4,8,128]{3,2,0,1:T(8,128)(2,1)S(1)}, u32[]{:S(2)}, u32[]{:S(2)}) collective-permute-start(bf16[4,4,8,128]{3,2,0,1:T(8,128)(2,1)S(1)} %get-tuple-element.25), channel_id=1, source_target_pairs={{0,8},{8,16},{16,24},{24,32},{32,40},{40,48},{48,56},{56,64},{64,7... | collective-permute-start | bytes 98312 | tf_op jit(solution)/shard_map/ppermute | solution.py:33
  9.5 13.9 %collective-permute-start.1 = (bf16[4,4,8,128]{3,2,0,1:T(8,128)(2,1)S(1)}, bf16[4,4,8,128]{3,2,0,1:T(8,128)(2,1)S(1)}, u32[]{:S(2)}, u32[]{:S(2)}) collective-permute-start(bf16[4,4,8,128]{3,2,0,1:T(8,128)(2,1)S(1)} %get-tuple-element.26), channel_id=1, source_target_pairs={{8,0},{16,8},{24,16},{32,24},{40,32},{48,40},{56,48},{64,56},{72,6... | collective-permute-start | bytes 98312 | tf_op jit(solution)/shard_map/ppermute | solution.py:34
  24.4 1.4 collective-permute-start.2
  27.1 5.1 %collective-permute-start.3 = (bf16[16,4,1,130]{3,2,0,1:T(2,128)(2,1)S(1)}, bf16[16,4,1,130]{3,2,0,1:T(2,128)(2,1)S(1)}, u32[]{:S(2)}, u32[]{:S(2)}) collective-permute-start(bf16[16,4,1,130]{3,2,0,1:T(2,128)(2,1)S(1)} %get-tuple-element.15), channel_id=1, source_target_pairs={{0,1},{1,2},{2,3},{4,5},{5,6},{6,7},{8,9},{9,10},{10,11},{12,13},{... | collective-permute-start | bytes 49928 | tf_op jit(solution)/shard_map/ppermute | solution.py:33
  30.2 6.2 %collective-permute-start.4 = (bf16[16,4,1,130]{3,2,0,1:T(2,128)(2,1)S(1)}, bf16[16,4,1,130]{3,2,0,1:T(2,128)(2,1)S(1)}, u32[]{:S(2)}, u32[]{:S(2)}) collective-permute-start(bf16[16,4,1,130]{3,2,0,1:T(2,128)(2,1)S(1)} %get-tuple-element.16), channel_id=1, source_target_pairs={{1,0},{2,1},{3,2},{5,4},{6,5},{7,6},{9,8},{10,9},{11,10},{13,12},{... | collective-permute-start | bytes 49928 | tf_op jit(solution)/shard_map/ppermute | solution.py:34
  47.6 1.9 collective-permute-start.5
  50.7 8.0 %collective-permute-start.6 = (bf16[14,16,1,130]{3,2,1,0:T(2,128)(2,1)S(1)}, bf16[14,16,1,130]{3,2,1,0:T(2,128)(2,1)S(1)}, u32[]{:S(2)}, u32[]{:S(2)}) collective-permute-start(bf16[14,16,1,130]{3,2,1,0:T(2,128)(2,1)S(1)} %get-tuple-element.5), channel_id=1, source_target_pairs={{0,1},{1,2},{2,3},{4,5},{5,6},{6,7},{8,9},{9,10},{10,11},{12,13},{... | collective-permute-start | bytes 174728 | tf_op jit(solution)/shard_map/ppermute | solution.py:33
  53.5 9.3 %collective-permute-start.7 = (bf16[14,16,1,130]{3,2,1,0:T(2,128)(2,1)S(1)}, bf16[14,16,1,130]{3,2,1,0:T(2,128)(2,1)S(1)}, u32[]{:S(2)}, u32[]{:S(2)}) collective-permute-start(bf16[14,16,1,130]{3,2,1,0:T(2,128)(2,1)S(1)} %get-tuple-element.6), channel_id=1, source_target_pairs={{1,0},{2,1},{3,2},{5,4},{6,5},{7,6},{9,8},{10,9},{11,10},{13,12},{... | collective-permute-start | bytes 174728 | tf_op jit(solution)/shard_map/ppermute | solution.py:34
  83.5 1.3 collective-permute-start.8
  84.9 8.0 %collective-permute-start.10 = (bf16[64,6,1,66]{0,3,2,1:T(8,128)(2,1)S(1)}, bf16[64,6,1,66]{0,3,2,1:T(8,128)(2,1)S(1)}, u32[]{:S(2)}, u32[]{:S(2)}) collective-permute-start(bf16[64,6,1,66]{0,3,2,1:T(8,128)(2,1)S(1)} %get-tuple-element.14), channel_id=1, source_target_pairs={{1,0},{2,1},{3,2},{5,4},{6,5},{7,6},{9,8},{10,9},{11,10},{13,12},{... | collective-permute-start | bytes 152072 | tf_op jit(solution)/shard_map/ppermute | solution.py:34
  86.2 6.9 %collective-permute-start.9 = (bf16[64,6,1,66]{0,3,2,1:T(8,128)(2,1)S(1)}, bf16[64,6,1,66]{0,3,2,1:T(8,128)(2,1)S(1)}, u32[]{:S(2)}, u32[]{:S(2)}) collective-permute-start(bf16[64,6,1,66]{0,3,2,1:T(8,128)(2,1)S(1)} %get-tuple-element.13), channel_id=1, source_target_pairs={{0,1},{1,2},{2,3},{4,5},{5,6},{6,7},{8,9},{9,10},{10,11},{12,13},{... | collective-permute-start | bytes 152072 | tf_op jit(solution)/shard_map/ppermute | solution.py:33
  126.8 16.1 %all-to-all-start.1 = ((bf16[256,64,2]{0,2,1:T(2,128)(2,1)}), bf16[256,64,2]{0,2,1:T(2,128)(2,1)S(1)}, u32[]{:S(2)}, u32[]{:S(2)}) async-start(bf16[256,64,2]{0,2,1:T(2,128)(2,1)} %copy.162), calls=%async_computation.1 | async-start | bytes 131072 | tf_op jit(solution)/shard_map/all_to_all | solution.py:253
  143.8 7.2 %collective-permute-start.11 = (bf16[64,1,4,64]{0,3,2,1:T(8,128)(2,1)S(1)}, bf16[64,1,4,64]{0,3,2,1:T(8,128)(2,1)S(1)}, u32[]{:S(2)}, u32[]{:S(2)}) collective-permute-start(bf16[64,1,4,64]{0,3,2,1:T(8,128)(2,1)S(1)} %get-tuple-element.21), channel_id=1, source_target_pairs={{0,8},{8,16},{16,24},{24,32},{32,40},{40,48},{48,56},{56,64},{64,7... | collective-permute-start | bytes 98312 | tf_op jit(solution)/shard_map/ppermute | solution.py:33
  149.1 14.3 %collective-permute-start.12 = (bf16[64,1,4,64]{0,3,2,1:T(8,128)(2,1)S(1)}, bf16[64,1,4,64]{0,3,2,1:T(8,128)(2,1)S(1)}, u32[]{:S(2)}, u32[]{:S(2)}) collective-permute-start(bf16[64,1,4,64]{0,3,2,1:T(8,128)(2,1)S(1)} %get-tuple-element.22), channel_id=1, source_target_pairs={{8,0},{16,8},{24,16},{32,24},{40,32},{48,40},{56,48},{64,56},{72,6... | collective-permute-start | bytes 98312 | tf_op jit(solution)/shard_map/ppermute | solution.py:34
  163.4 1.5 collective-permute-start.13
  165.1 8.1 %collective-permute-start.14 = (bf16[64,6,1,66]{0,3,2,1:T(8,128)(2,1)S(1)}, bf16[64,6,1,66]{0,3,2,1:T(8,128)(2,1)S(1)}, u32[]{:S(2)}, u32[]{:S(2)}) collective-permute-start(bf16[64,6,1,66]{0,3,2,1:T(8,128)(2,1)S(1)} %get-tuple-element.11), channel_id=1, source_target_pairs={{0,1},{1,2},{2,3},{4,5},{5,6},{6,7},{8,9},{9,10},{10,11},{12,13},{... | collective-permute-start | bytes 152072 | tf_op jit(solution)/shard_map/ppermute | solution.py:33
  170.5 6.7 %collective-permute-start.15 = (bf16[64,6,1,66]{0,3,2,1:T(8,128)(2,1)S(1)}, bf16[64,6,1,66]{0,3,2,1:T(8,128)(2,1)S(1)}, u32[]{:S(2)}, u32[]{:S(2)}) collective-permute-start(bf16[64,6,1,66]{0,3,2,1:T(8,128)(2,1)S(1)} %get-tuple-element.12), channel_id=1, source_target_pairs={{1,0},{2,1},{3,2},{5,4},{6,5},{7,6},{9,8},{10,9},{11,10},{13,12},{... | collective-permute-start | bytes 152072 | tf_op jit(solution)/shard_map/ppermute | solution.py:34
  197.1 5.9 %collective-permute-start.16 = (bf16[1,16,8,128]{3,2,1,0:T(8,128)(2,1)S(1)}, bf16[1,16,8,128]{3,2,1,0:T(8,128)(2,1)S(1)}, u32[]{:S(2)}, u32[]{:S(2)}) collective-permute-start(bf16[1,16,8,128]{3,2,1,0:T(8,128)(2,1)S(1)} %get-tuple-element.19), channel_id=1, source_target_pairs={{0,8},{8,16},{16,24},{24,32},{32,40},{40,48},{48,56},{56,64},{64,7... | collective-permute-start | bytes 98312 | tf_op jit(solution)/shard_map/ppermute | solution.py:33
  199.1 13.9 %collective-permute-start.17 = (bf16[1,16,8,128]{3,2,1,0:T(8,128)(2,1)S(1)}, bf16[1,16,8,128]{3,2,1,0:T(8,128)(2,1)S(1)}, u32[]{:S(2)}, u32[]{:S(2)}) collective-permute-start(bf16[1,16,8,128]{3,2,1,0:T(8,128)(2,1)S(1)} %get-tuple-element.20), channel_id=1, source_target_pairs={{8,0},{16,8},{24,16},{32,24},{40,32},{48,40},{56,48},{64,56},{72,6... | collective-permute-start | bytes 98312 | tf_op jit(solution)/shard_map/ppermute | solution.py:34
  213.2 1.7 collective-permute-start.18
  215.8 5.9 %collective-permute-start.19 = (bf16[10,16,1,130]{3,2,1,0:T(2,128)(2,1)S(1)}, bf16[10,16,1,130]{3,2,1,0:T(2,128)(2,1)S(1)}, u32[]{:S(2)}, u32[]{:S(2)}) collective-permute-start(bf16[10,16,1,130]{3,2,1,0:T(2,128)(2,1)S(1)} %get-tuple-element.7), channel_id=1, source_target_pairs={{0,1},{1,2},{2,3},{4,5},{5,6},{6,7},{8,9},{9,10},{10,11},{12,13},{... | collective-permute-start | bytes 124808 | tf_op jit(solution)/shard_map/ppermute | solution.py:33
  218.0 7.9 %collective-permute-start.20 = (bf16[10,16,1,130]{3,2,1,0:T(2,128)(2,1)S(1)}, bf16[10,16,1,130]{3,2,1,0:T(2,128)(2,1)S(1)}, u32[]{:S(2)}, u32[]{:S(2)}) collective-permute-start(bf16[10,16,1,130]{3,2,1,0:T(2,128)(2,1)S(1)} %get-tuple-element.8), channel_id=1, source_target_pairs={{1,0},{2,1},{3,2},{5,4},{6,5},{7,6},{9,8},{10,9},{11,10},{13,12},{... | collective-permute-start | bytes 124808 | tf_op jit(solution)/shard_map/ppermute | solution.py:34
  (10 other events, 116.8 us)

commit v2 on v1

--- a/solution.py
+++ b/solution.py
@@ -150,9 +150,53 @@
     )[0]
 
 
+def mid_kernel(p_ref, w_ref, o_ref, shifted_ref, *, sx, sv, ss, span):
+    lanes = p_ref.shape[-1]
+    pitch = ss + 2
+
+    def shift(x, carry):
+        slab = p_ref[x].astype(jnp.float32)
+        for b in range(3):
+            for c in range(3):
+                step = b * pitch + c
+                piece = slab if step == 0 else pltpu.roll(slab, lanes - step, 1)
+                shifted_ref[x, b * 3 + c] = piece[:, :span].astype(jnp.bfloat16)
+        return carry
+
+    lax.fori_loop(0, sx + 2, shift, 0)
+    chans = shifted_ref.shape[2]
+
+    def row(x, carry):
+        stack = shifted_ref[pl.ds(x, 3)].reshape(27 * chans, span)
+        acc = jnp.dot(w_ref[...], stack, preferred_element_type=jnp.float32)
+        act = (acc * jax.nn.sigmoid(acc)).astype(jnp.bfloat16).astype(jnp.float32)
+        for v in range(sv):
+            piece = act if v == 0 else pltpu.roll(act, span - v * pitch, 1)
+            o_ref[x, v] = piece[:, :ss]
+        return carry
+
+    lax.fori_loop(0, sx, row, 0)
+
+
 def mid_conv(field, weight, sides=MID_SIDES):
+    chans = field.shape[0]
     padded = extended(field, sides)
-    return conv_valid(padded, weight)
+    _, sx, sv, ss = padded.shape
+    sx, sv, ss = sx - 2, sv - 2, ss - 2
+    flat = (sv + 2) * (ss + 2)
+    lanes = round_up(flat, 128)
+    span = round_up((sv - 1) * (ss + 2) + ss, 128)
+    padded = padded.transpose(1, 0, 2, 3).reshape(sx + 2, chans, flat)
+    padded = jnp.pad(padded, ((0, 0), (0, 0), (0, lanes - flat)))
+    cout = weight.shape[1] // chans
+    taps = weight.reshape(27, cout, chans).transpose(1, 0, 2).reshape(cout, 27 * chans)
+    kernel = lambda *refs: mid_kernel(*refs, sx=sx, sv=sv, ss=ss, span=span)
+    out = pl.pallas_call(
+        kernel,
+        out_shape=jax.ShapeDtypeStruct((sx, sv, cout, ss), jnp.float32),
+        scratch_shapes=[pltpu.VMEM((sx + 2, 9, chans, span), jnp.bfloat16)],
+    )(padded, taps)
+    return out.transpose(2, 0, 1, 3).astype(jnp.bfloat16)
 
 
 def conv_down(field, weight):
@@ -240,7 +284,7 @@
     fine_wide = inside_rows(fine_conv(first, w_fine_enc, FINE_CROSS).astype(jnp.bfloat16), -2)
     fine_skip = fine_wide[2:-2]
     mid_in = activate(fine_down(fine_wide, w_down_mid))
-    mid_skip = activate(mid_conv(mid_in, unfold(w_mid_enc, 3, C1, C1), MID_CROSS))
+    mid_skip = mid_conv(mid_in, w_mid_enc, MID_CROSS)
     bottom = activate(conv_down(mid_skip, unfold(w_down_bottom, 2, C2, C1)))
     chans, sx, sv, ss = bottom.shape
     flat = bottom.reshape(chans, sx, sv * ss)
@@ -255,7 +299,7 @@
     mid_up = (
         conv_up(bottom_out, unfold(w_up_mid, 2, C2, C1)) + mid_skip.astype(jnp.float32)
     ).astype(jnp.bfloat16)
-    mid_dec = activate(mid_conv(mid_up, unfold(w_mid_dec, 3, C1, C1)))
+    mid_dec = mid_conv(mid_up, w_mid_dec)
     fine_up_field = (fine_up(mid_dec, w_up_fine) + fine_skip.astype(jnp.float32)).astype(
         jnp.bfloat16
     )

time: 239 us -> 233 us (0.975)
  matrix products: 27.8 us -> 7.64 us
  Pallas kernels: 27.7 us -> 37.3 us
  local copies, waits for them, and re-layouts: 20.2 us -> 25 us
    conv_general_dilated x2 -> x0, matrix products: 23.8 us -> none  [conv_valid(): lax.conv_general_dilated(padded[None], weight, (1, 1, 1), 'VALID', dimens...]
    pallas_call x0 -> x2, Pallas kernels: none -> 9.65 us  [mid_conv(): pl.pallas_call(kernel, out_shape=jax.ShapeDtypeStruct((sx, sv, cout, ss),...]
    reshape x0 -> x9, local copies, waits for them, and re-layouts: none -> 4.72 us  [the longest x6 3.67 us: mid_conv(): weight.reshape(27, cout, chans).transpose(1, 0, 2).reshape(cout, 27 * chans)]
    concatenate x5 -> x6, other arithmetic: 8.29 us -> 8.35 us  [extended(): block = jnp.concatenate([low, block, high], axis=dim)]
  transfers between devices with their start and end apart: 22 -> 22, of which waited for: 17 -> 15; matrix products, arithmetic and copies ran while one was open for 2% -> 3% of each run, Pallas kernels for 0% -> 0%
where the time goes in v2:
time: 233 us; the launch traced here: 232 us
  waiting for transfers between devices  71.3 us (31%)
  starting transfers between devices  55.8 us (24%)
  Pallas kernels  37.3 us (16%)
  local copies, waits for them, and re-layouts  25 us (11%)
  other arithmetic  18 us (8%)
  blocking collectives  15.7 us (7%)
  matrix products  7.64 us (3%)
    ppermute x8, waiting for transfers between devices, extended(): high = lax.ppermute(bottom, axis, backward)  49.8 us
    ppermute x8, starting transfers between devices, extended(): low = lax.ppermute(top, axis, forward)  33.9 us
    pallas_call x3, Pallas kernels, fine_conv(): pl.pallas_call(kernel, out_shape=out_shape, scratch_shapes=[pltpu.VMEM((c...  27.7 us
    all_to_all x1, blocking collectives, on_device(): rows = lax.all_to_all(flat, 'gx', split_axis=2, concat_axis=1, tiled=True)  15.7 us
    ppermute x8, starting transfers between devices, extended(): high = lax.ppermute(bottom, axis, backward)  14.4 us
    pallas_call x2, Pallas kernels, mid_conv(): pl.pallas_call(kernel, out_shape=jax.ShapeDtypeStruct((sx, sv, cout, ss),...  9.65 us
    all_to_all x1, waiting for transfers between devices, on_device(): lax.all_to_all(result, 'gx', split_axis=1, concat_axis=2, tiled=True)  8.7 us
    concatenate x6, other arithmetic, extended(): block = jnp.concatenate([low, block, high], axis=dim)  8.35 us
  transfers between devices with their start and end apart: 22, of which 15 were waited for; matrix products, arithmetic and copies ran while one was open for 3% of the time, Pallas kernels for 0%

profile of v2, /device:TPU:30, one launch (start us, length us, event | category | flops | bytes accessed | tf_op | source)
XLA Modules:
  0.0 231.7 jit_solution(9574090805187626081)
XLA Ops:
  0.8 8.7 %collective-permute-start = (bf16[4,4,8,128]{3,2,0,1:T(8,128)(2,1)S(1)}, bf16[4,4,8,128]{3,2,0,1:T(8,128)(2,1)S(1)}, u32[]{:S(2)}, u32[]{:S(2)}) collective-permute-start(bf16[4,4,8,128]{3,2,0,1:T(8,128)(2,1)S(1)} %get-tuple-element.29), channel_id=1, source_target_pairs={{0,8},{8,16},{16,24},{24,32},{32,40},{40,48},{48,56},{56,64},{64,7... | collective-permute-start | bytes 98312 | tf_op jit(solution)/shard_map/ppermute | solution.py:33
  11.5 12.0 %collective-permute-done.1 = bf16[4,4,8,128]{3,2,0,1:T(8,128)(2,1)S(1)} collective-permute-done((bf16[4,4,8,128]{3,2,0,1:T(8,128)(2,1)S(1)}, bf16[4,4,8,128]{3,2,0,1:T(8,128)(2,1)S(1)}, u32[]{:S(2)}, u32[]{:S(2)}) %collective-permute-start.1) | collective-permute-done | bytes 32800 | tf_op jit(solution)/shard_map/ppermute | solution.py:34
  32.3 4.1 %collective-permute-done.4 = bf16[16,4,1,130]{3,2,0,1:T(2,128)(2,1)S(1)} collective-permute-done((bf16[16,4,1,130]{3,2,0,1:T(2,128)(2,1)S(1)}, bf16[16,4,1,130]{3,2,0,1:T(2,128)(2,1)S(1)}, u32[]{:S(2)}, u32[]{:S(2)}) %collective-permute-start.4) | collective-permute-done | bytes 16672 | tf_op jit(solution)/shard_map/ppermute | solution.py:34
  38.1 7.9 %shard_map.145 = f32[14,16,8,128]{3,2,1,0:T(8,128)} custom-call(bf16[16,128,256]{2,1,0:T(8,128)(2,1)} %bitcast.144, bf16[27,16,8]{2,1,0:T(8,128)(2,1)} %bitcast.154), custom_call_target="tpu_custom_call" | custom-call | tf_op jit(solution)/shard_map/pallas_call | solution.py:132
  54.8 3.8 %collective-permute-done.6 = bf16[14,16,1,130]{3,2,1,0:T(2,128)(2,1)S(1)} collective-permute-done((bf16[14,16,1,130]{3,2,1,0:T(2,128)(2,1)S(1)}, bf16[14,16,1,130]{3,2,1,0:T(2,128)(2,1)S(1)}, u32[]{:S(2)}, u32[]{:S(2)}) %collective-permute-start.6) | collective-permute-done | bytes 58272 | tf_op jit(solution)/shard_map/ppermute | solution.py:33
  58.6 4.1 %collective-permute-done.7 = bf16[14,16,1,130]{3,2,1,0:T(2,128)(2,1)S(1)} collective-permute-done((bf16[14,16,1,130]{3,2,1,0:T(2,128)(2,1)S(1)}, bf16[14,16,1,130]{3,2,1,0:T(2,128)(2,1)S(1)}, u32[]{:S(2)}, u32[]{:S(2)}) %collective-permute-start.7) | collective-permute-done | bytes 58272 | tf_op jit(solution)/shard_map/ppermute | solution.py:34
  62.8 3.6 %fusion.19 = bf16[14,16,16,256]{3,2,1,0:T(8,128)(2,1)} fusion(bf16[14,16,1,130]{3,2,1,0:T(2,128)(2,1)S(1)} %collective-permute-done.7, bf16[14,16,1,130]{3,2,1,0:T(2,128)(2,1)S(1)} %collective-permute-done.6, bf16[14,16,8,1]{3,2,1,0:T(8,128)(2,1)S(1)} %get-tuple-element.14, bf16[14,16,8,128]{3,2,1,0:T(8,128)(2,1)S(1)} %convert_select_fusion, ...), kind=kLoop, calls=%fused_computation.23 | loop fusion | flops 21102592 | bytes 2417408 | tf_op jit(solution)/shard_map/concatenate | solution.py:35
  66.4 10.5 %shard_map.146 = f32[12,16,8,128]{3,2,1,0:T(8,128)} custom-call(bf16[14,256,256]{2,1,0:T(8,128)(2,1)} %bitcast.142, bf16[27,16,16]{2,1,0:T(8,128)(2,1)} %bitcast.160), custom_call_target="tpu_custom_call" | custom-call | tf_op jit(solution)/shard_map/pallas_call | solution.py:132
  80.9 3.6 %multiply_convert_fusion = bf16[64,6,4,64]{3,0,2,1:T(8,128)(2,1)S(1)} fusion(bf16[6,2,16,4,2,64,2]{2,6,5,4,3,1,0:T(2,128)(2,1)} %bitcast.145, bf16[64,16,2,2,2,1,1]{0,4,3,2,1,6,5:T(2,128)(2,1)S(1)} %bitcast.162), kind=kOutput, calls=%fused_computation.61 | convolution fusion | flops 25657344 | bytes 606208 | tf_op jit(solution)/shard_map/xaivbsc,oiabc->oxvs/dot_general | solution.py:216
  88.1 4.7 %collective-permute-start.9 = (bf16[64,6,1,66]{3,0,2,1:T(8,128)(2,1)S(1)}, bf16[64,6,1,66]{3,0,2,1:T(8,128)(2,1)S(1)}, u32[]{:S(2)}, u32[]{:S(2)}) collective-permute-start(bf16[64,6,1,66]{3,0,2,1:T(8,128)(2,1)S(1)} %get-tuple-element.9), channel_id=1, source_target_pairs={{0,1},{1,2},{2,3},{4,5},{5,6},{6,7},{8,9},{9,10},{10,11},{12,13},{... | collective-permute-start | bytes 152072 | tf_op jit(solution)/shard_map/ppermute | solution.py:33
  97.3 4.8 %shard_map.147 = f32[4,4,64,64]{3,2,1,0:T(8,128)} custom-call(bf16[6,64,512]{2,1,0:T(8,128)(2,1)} %pad.26.refs_0_, bf16[64,1728]{1,0:T(8,128)(2,1)} %reshape.115.refs_1_), custom_call_target="tpu_custom_call" | custom-call | tf_op jit(solution)/shard_map/pallas_call | solution.py:194
  104.9 15.7 %all_to_all.24 = bf16[256,2,64]{0,1,2:T(2,128)(2,1)S(1)} all-to-all(bf16[256,2,64]{0,1,2:T(2,128)(2,1)S(1)} %copy.128), channel_id=1, replica_groups=mesh['gx'=32,'gy'=2,'gz'=4] {'gx'}, dimensions={2} | all-to-all | bytes 131072 | tf_op jit(solution)/shard_map/all_to_all | solution.py:291
  124.1 7.0 %all-to-all-start.1 = ((bf16[256,64,2]{0,2,1:T(2,128)(2,1)}), bf16[256,64,2]{0,2,1:T(2,128)(2,1)S(1)}, u32[]{:S(2)}, u32[]{:S(2)}) async-start(bf16[256,64,2]{0,2,1:T(2,128)(2,1)} %copy.137), calls=%async_computation.1 | async-start | bytes 131072 | tf_op jit(solution)/shard_map/all_to_all | solution.py:297
  131.6 8.7 %all-to-all-done.1 = bf16[256,64,2]{0,2,1:T(2,128)(2,1)S(1)} async-done(((bf16[256,64,2]{0,2,1:T(2,128)(2,1)}), bf16[256,64,2]{0,2,1:T(2,128)(2,1)S(1)}, u32[]{:S(2)}, u32[]{:S(2)}) %all-to-all-start.1) | async-done | bytes 65568 | tf_op jit(solution)/shard_map/all_to_all | solution.py:297
  141.4 5.2 %collective-permute-start.11 = (bf16[64,1,4,64]{3,0,2,1:T(8,128)(2,1)S(1)}, bf16[64,1,4,64]{3,0,2,1:T(8,128)(2,1)S(1)}, u32[]{:S(2)}, u32[]{:S(2)}) collective-permute-start(bf16[64,1,4,64]{3,0,2,1:T(8,128)(2,1)S(1)} %get-tuple-element.25), channel_id=1, source_target_pairs={{0,8},{8,16},{16,24},{24,32},{32,40},{40,48},{48,56},{56,64},{64,7... | collective-permute-start | bytes 98312 | tf_op jit(solution)/shard_map/ppermute | solution.py:33
  148.5 12.4 %collective-permute-done.12 = bf16[64,1,4,64]{3,0,2,1:T(8,128)(2,1)S(1)} collective-permute-done((bf16[64,1,4,64]{3,0,2,1:T(8,128)(2,1)S(1)}, bf16[64,1,4,64]{3,0,2,1:T(8,128)(2,1)S(1)}, u32[]{:S(2)}, u32[]{:S(2)}) %collective-permute-start.12) | collective-permute-done | bytes 32800 | tf_op jit(solution)/shard_map/ppermute | solution.py:34
  163.2 4.8 %collective-permute-start.14 = (bf16[64,6,1,66]{3,0,2,1:T(8,128)(2,1)S(1)}, bf16[64,6,1,66]{3,0,2,1:T(8,128)(2,1)S(1)}, u32[]{:S(2)}, u32[]{:S(2)}) collective-permute-start(bf16[64,6,1,66]{3,0,2,1:T(8,128)(2,1)S(1)} %get-tuple-element.7), channel_id=1, source_target_pairs={{0,1},{1,2},{2,3},{4,5},{5,6},{6,7},{8,9},{9,10},{10,11},{12,13},{... | collective-permute-start | bytes 152072 | tf_op jit(solution)/shard_map/ppermute | solution.py:33
  176.7 4.8 %shard_map.148 = f32[4,4,64,64]{3,2,1,0:T(8,128)} custom-call(bf16[6,64,512]{2,1,0:T(8,128)(2,1)} %pad.27.refs_0_, bf16[64,1728]{1,0:T(8,128)(2,1)} %reshape.126.refs_1_), custom_call_target="tpu_custom_call" | custom-call | tf_op jit(solution)/shard_map/pallas_call | solution.py:194
  182.8 4.3 %copy.145 = f32[4,2,16,4,2,64,2]{2,6,5,4,3,1,0:T(2,128)} copy(f32[4,2,16,4,2,64,2]{5,2,6,4,1,3,0:T(8,128)S(1)} %convolution_bitcast_fusion) | data formatting | bytes 1048576 | tf_op jit(solution)/shard_map/ixvs,ioabc->xaovbsc/transpose | solution.py:220
  192.0 3.9 %collective-permute-start.17 = (bf16[1,16,8,128]{3,2,1,0:T(8,128)(2,1)S(1)}, bf16[1,16,8,128]{3,2,1,0:T(8,128)(2,1)S(1)}, u32[]{:S(2)}, u32[]{:S(2)}) collective-permute-start(bf16[1,16,8,128]{3,2,1,0:T(8,128)(2,1)S(1)} %get-tuple-element.24), channel_id=1, source_target_pairs={{8,0},{16,8},{24,16},{32,24},{40,32},{48,40},{56,48},{64,56},{72,6... | collective-permute-start | bytes 98312 | tf_op jit(solution)/shard_map/ppermute | solution.py:34
  195.9 10.0 %collective-permute-done.17 = bf16[1,16,8,128]{3,2,1,0:T(8,128)(2,1)S(1)} collective-permute-done((bf16[1,16,8,128]{3,2,1,0:T(8,128)(2,1)S(1)}, bf16[1,16,8,128]{3,2,1,0:T(8,128)(2,1)S(1)}, u32[]{:S(2)}, u32[]{:S(2)}) %collective-permute-start.17) | collective-permute-done | bytes 32800 | tf_op jit(solution)/shard_map/ppermute | solution.py:34
  215.2 4.1 %collective-permute-done.20 = bf16[10,16,1,130]{3,2,1,0:T(2,128)(2,1)S(1)} collective-permute-done((bf16[10,16,1,130]{3,2,1,0:T(2,128)(2,1)S(1)}, bf16[10,16,1,130]{3,2,1,0:T(2,128)(2,1)S(1)}, u32[]{:S(2)}, u32[]{:S(2)}) %collective-permute-start.20) | collective-permute-done | bytes 41632 | tf_op jit(solution)/shard_map/ppermute | solution.py:34
  219.3 3.2 %fusion.28 = bf16[10,16,16,256]{3,2,1,0:T(8,128)(2,1)} fusion(bf16[10,16,1,130]{3,2,1,0:T(2,128)(2,1)S(1)} %collective-permute-done.20, bf16[10,16,1,130]{3,2,1,0:T(2,128)(2,1)S(1)} %collective-permute-done.19, bf16[10,16,8,1]{3,2,1,0:T(8,128)(2,1)S(1)} %get-tuple-element.22, bf16[10,16,8,1]{3,2,1,0:T(8,128)(2,1)S(1)} %get-tuple-element.21, ...), kind=kLoop, calls=%fused_computation.33 | loop fusion | flops 20316160 | bytes 1726720 | tf_op jit(solution)/shard_map/concatenate | solution.py:35
  222.5 9.2 %shard_map.149 = f32[4,8,8,128]{3,2,1,0:T(8,128)} custom-call(bf16[10,256,256]{2,1,0:T(8,128)(2,1)} %bitcast.143, bf16[27,16,16]{2,1,0:T(8,128)(2,1)} %bitcast.159, bf16[32,128]{1,0:T(8,128)(2,1)} %convert_element_type.138.refs_2_), custom_call_target="tpu_custom_call" | custom-call | tf_op jit(solution)/shard_map/pallas_call | solution.py:132
  (142 shorter events, 69.5 us)
Async XLA Ops:
  0.0 121.2 %copy-start = (bf16[256,256]{1,0:T(8,128)(2,1)S(1)}, bf16[256,256]{1,0:T(8,128)(2,1)}, u32[]{:S(2)}) copy-start(bf16[256,256]{1,0:T(8,128)(2,1)} %param.22) | copy-start | bytes 393220
  0.0 36.4 %copy-start.2 = (bf16[4,8,8,128]{3,2,1,0:T(8,128)(2,1)S(1)}, bf16[4,8,8,128]{3,2,1,0:T(8,128)(2,1)}, u32[]{:S(2)}) copy-start(bf16[4,8,8,128]{3,2,1,0:T(8,128)(2,1)} %param.15) | copy-start | bytes 196612
  0.8 10.6 %collective-permute-start = (bf16[4,4,8,128]{3,2,0,1:T(8,128)(2,1)S(1)}, bf16[4,4,8,128]{3,2,0,1:T(8,128)(2,1)S(1)}, u32[]{:S(2)}, u32[]{:S(2)}) collective-permute-start(bf16[4,4,8,128]{3,2,0,1:T(8,128)(2,1)S(1)} %get-tuple-element.29), channel_id=1, source_target_pairs={{0,8},{8,16},{16,24},{24,32},{32,40},{40,48},{48,56},{56,64},{64,7... | collective-permute-start | bytes 98312 | tf_op jit(solution)/shard_map/ppermute | solution.py:33
  9.5 13.9 %collective-permute-start.1 = (bf16[4,4,8,128]{3,2,0,1:T(8,128)(2,1)S(1)}, bf16[4,4,8,128]{3,2,0,1:T(8,128)(2,1)S(1)}, u32[]{:S(2)}, u32[]{:S(2)}) collective-permute-start(bf16[4,4,8,128]{3,2,0,1:T(8,128)(2,1)S(1)} %get-tuple-element.30), channel_id=1, source_target_pairs={{8,0},{16,8},{24,16},{32,24},{40,32},{48,40},{56,48},{64,56},{72,6... | collective-permute-start | bytes 98312 | tf_op jit(solution)/shard_map/ppermute | solution.py:34
  24.4 1.4 collective-permute-start.2
  27.1 5.1 %collective-permute-start.3 = (bf16[16,4,1,130]{3,2,0,1:T(2,128)(2,1)S(1)}, bf16[16,4,1,130]{3,2,0,1:T(2,128)(2,1)S(1)}, u32[]{:S(2)}, u32[]{:S(2)}) collective-permute-start(bf16[16,4,1,130]{3,2,0,1:T(2,128)(2,1)S(1)} %get-tuple-element.19), channel_id=1, source_target_pairs={{0,1},{1,2},{2,3},{4,5},{5,6},{6,7},{8,9},{9,10},{10,11},{12,13},{... | collective-permute-start | bytes 49928 | tf_op jit(solution)/shard_map/ppermute | solution.py:33
  30.2 6.2 %collective-permute-start.4 = (bf16[16,4,1,130]{3,2,0,1:T(2,128)(2,1)S(1)}, bf16[16,4,1,130]{3,2,0,1:T(2,128)(2,1)S(1)}, u32[]{:S(2)}, u32[]{:S(2)}) collective-permute-start(bf16[16,4,1,130]{3,2,0,1:T(2,128)(2,1)S(1)} %get-tuple-element.20), channel_id=1, source_target_pairs={{1,0},{2,1},{3,2},{5,4},{6,5},{7,6},{9,8},{10,9},{11,10},{13,12},{... | collective-permute-start | bytes 49928 | tf_op jit(solution)/shard_map/ppermute | solution.py:34
  47.5 1.9 collective-permute-start.5
  50.7 8.0 %collective-permute-start.6 = (bf16[14,16,1,130]{3,2,1,0:T(2,128)(2,1)S(1)}, bf16[14,16,1,130]{3,2,1,0:T(2,128)(2,1)S(1)}, u32[]{:S(2)}, u32[]{:S(2)}) collective-permute-start(bf16[14,16,1,130]{3,2,1,0:T(2,128)(2,1)S(1)} %get-tuple-element.5), channel_id=1, source_target_pairs={{0,1},{1,2},{2,3},{4,5},{5,6},{6,7},{8,9},{9,10},{10,11},{12,13},{... | collective-permute-start | bytes 174728 | tf_op jit(solution)/shard_map/ppermute | solution.py:33
  53.5 9.3 %collective-permute-start.7 = (bf16[14,16,1,130]{3,2,1,0:T(2,128)(2,1)S(1)}, bf16[14,16,1,130]{3,2,1,0:T(2,128)(2,1)S(1)}, u32[]{:S(2)}, u32[]{:S(2)}) collective-permute-start(bf16[14,16,1,130]{3,2,1,0:T(2,128)(2,1)S(1)} %get-tuple-element.6), channel_id=1, source_target_pairs={{1,0},{2,1},{3,2},{5,4},{6,5},{7,6},{9,8},{10,9},{11,10},{13,12},{... | collective-permute-start | bytes 174728 | tf_op jit(solution)/shard_map/ppermute | solution.py:34
  84.7 1.8 collective-permute-start.8
  86.8 8.4 %collective-permute-start.10 = (bf16[64,6,1,66]{3,0,2,1:T(8,128)(2,1)S(1)}, bf16[64,6,1,66]{3,0,2,1:T(8,128)(2,1)S(1)}, u32[]{:S(2)}, u32[]{:S(2)}) collective-permute-start(bf16[64,6,1,66]{3,0,2,1:T(8,128)(2,1)S(1)} %get-tuple-element.10), channel_id=1, source_target_pairs={{1,0},{2,1},{3,2},{5,4},{6,5},{7,6},{9,8},{10,9},{11,10},{13,12},{... | collective-permute-start | bytes 152072 | tf_op jit(solution)/shard_map/ppermute | solution.py:34
  88.1 7.2 %collective-permute-start.9 = (bf16[64,6,1,66]{3,0,2,1:T(8,128)(2,1)S(1)}, bf16[64,6,1,66]{3,0,2,1:T(8,128)(2,1)S(1)}, u32[]{:S(2)}, u32[]{:S(2)}) collective-permute-start(bf16[64,6,1,66]{3,0,2,1:T(8,128)(2,1)S(1)} %get-tuple-element.9), channel_id=1, source_target_pairs={{0,1},{1,2},{2,3},{4,5},{5,6},{6,7},{8,9},{9,10},{10,11},{12,13},{... | collective-permute-start | bytes 152072 | tf_op jit(solution)/shard_map/ppermute | solution.py:33
  124.1 16.2 %all-to-all-start.1 = ((bf16[256,64,2]{0,2,1:T(2,128)(2,1)}), bf16[256,64,2]{0,2,1:T(2,128)(2,1)S(1)}, u32[]{:S(2)}, u32[]{:S(2)}) async-start(bf16[256,64,2]{0,2,1:T(2,128)(2,1)} %copy.137), calls=%async_computation.1 | async-start | bytes 131072 | tf_op jit(solution)/shard_map/all_to_all | solution.py:297
  141.4 7.1 %collective-permute-start.11 = (bf16[64,1,4,64]{3,0,2,1:T(8,128)(2,1)S(1)}, bf16[64,1,4,64]{3,0,2,1:T(8,128)(2,1)S(1)}, u32[]{:S(2)}, u32[]{:S(2)}) collective-permute-start(bf16[64,1,4,64]{3,0,2,1:T(8,128)(2,1)S(1)} %get-tuple-element.25), channel_id=1, source_target_pairs={{0,8},{8,16},{16,24},{24,32},{32,40},{40,48},{48,56},{56,64},{64,7... | collective-permute-start | bytes 98312 | tf_op jit(solution)/shard_map/ppermute | solution.py:33
  146.6 14.3 %collective-permute-start.12 = (bf16[64,1,4,64]{3,0,2,1:T(8,128)(2,1)S(1)}, bf16[64,1,4,64]{3,0,2,1:T(8,128)(2,1)S(1)}, u32[]{:S(2)}, u32[]{:S(2)}) collective-permute-start(bf16[64,1,4,64]{3,0,2,1:T(8,128)(2,1)S(1)} %get-tuple-element.26), channel_id=1, source_target_pairs={{8,0},{16,8},{24,16},{32,24},{40,32},{48,40},{56,48},{64,56},{72,6... | collective-permute-start | bytes 98312 | tf_op jit(solution)/shard_map/ppermute | solution.py:34
  161.2 1.8 collective-permute-start.13
  163.2 8.2 %collective-permute-start.14 = (bf16[64,6,1,66]{3,0,2,1:T(8,128)(2,1)S(1)}, bf16[64,6,1,66]{3,0,2,1:T(8,128)(2,1)S(1)}, u32[]{:S(2)}, u32[]{:S(2)}) collective-permute-start(bf16[64,6,1,66]{3,0,2,1:T(8,128)(2,1)S(1)} %get-tuple-element.7), channel_id=1, source_target_pairs={{0,1},{1,2},{2,3},{4,5},{5,6},{6,7},{8,9},{9,10},{10,11},{12,13},{... | collective-permute-start | bytes 152072 | tf_op jit(solution)/shard_map/ppermute | solution.py:33
  168.1 6.5 %collective-permute-start.15 = (bf16[64,6,1,66]{3,0,2,1:T(8,128)(2,1)S(1)}, bf16[64,6,1,66]{3,0,2,1:T(8,128)(2,1)S(1)}, u32[]{:S(2)}, u32[]{:S(2)}) collective-permute-start(bf16[64,6,1,66]{3,0,2,1:T(8,128)(2,1)S(1)} %get-tuple-element.8), channel_id=1, source_target_pairs={{1,0},{2,1},{3,2},{5,4},{6,5},{7,6},{9,8},{10,9},{11,10},{13,12},{... | collective-permute-start | bytes 152072 | tf_op jit(solution)/shard_map/ppermute | solution.py:34
  190.1 5.9 %collective-permute-start.16 = (bf16[1,16,8,128]{3,2,1,0:T(8,128)(2,1)S(1)}, bf16[1,16,8,128]{3,2,1,0:T(8,128)(2,1)S(1)}, u32[]{:S(2)}, u32[]{:S(2)}) collective-permute-start(bf16[1,16,8,128]{3,2,1,0:T(8,128)(2,1)S(1)} %get-tuple-element.23), channel_id=1, source_target_pairs={{0,8},{8,16},{16,24},{24,32},{32,40},{40,48},{48,56},{56,64},{64,7... | collective-permute-start | bytes 98312 | tf_op jit(solution)/shard_map/ppermute | solution.py:33
  192.0 13.9 %collective-permute-start.17 = (bf16[1,16,8,128]{3,2,1,0:T(8,128)(2,1)S(1)}, bf16[1,16,8,128]{3,2,1,0:T(8,128)(2,1)S(1)}, u32[]{:S(2)}, u32[]{:S(2)}) collective-permute-start(bf16[1,16,8,128]{3,2,1,0:T(8,128)(2,1)S(1)} %get-tuple-element.24), channel_id=1, source_target_pairs={{8,0},{16,8},{24,16},{32,24},{40,32},{48,40},{56,48},{64,56},{72,6... | collective-permute-start | bytes 98312 | tf_op jit(solution)/shard_map/ppermute | solution.py:34
  206.1 1.7 collective-permute-start.18
  208.7 6.5 %collective-permute-start.19 = (bf16[10,16,1,130]{3,2,1,0:T(2,128)(2,1)S(1)}, bf16[10,16,1,130]{3,2,1,0:T(2,128)(2,1)S(1)}, u32[]{:S(2)}, u32[]{:S(2)}) collective-permute-start(bf16[10,16,1,130]{3,2,1,0:T(2,128)(2,1)S(1)} %get-tuple-element.11), channel_id=1, source_target_pairs={{0,1},{1,2},{2,3},{4,5},{5,6},{6,7},{8,9},{9,10},{10,11},{12,13},{... | collective-permute-start | bytes 124808 | tf_op jit(solution)/shard_map/ppermute | solution.py:33
  211.5 7.9 %collective-permute-start.20 = (bf16[10,16,1,130]{3,2,1,0:T(2,128)(2,1)S(1)}, bf16[10,16,1,130]{3,2,1,0:T(2,128)(2,1)S(1)}, u32[]{:S(2)}, u32[]{:S(2)}) collective-permute-start(bf16[10,16,1,130]{3,2,1,0:T(2,128)(2,1)S(1)} %get-tuple-element.12), channel_id=1, source_target_pairs={{1,0},{2,1},{3,2},{5,4},{6,5},{7,6},{9,8},{10,9},{11,10},{13,12},{... | collective-permute-start | bytes 124808 | tf_op jit(solution)/shard_map/ppermute | solution.py:34
  (11 other events, 104.7 us)

commit v3 on v2

--- a/solution.py
+++ b/solution.py
@@ -36,12 +36,14 @@
     return block
 
 
-def inside_rows(field, offset):
-    rows = field.shape[0]
-    start = lax.axis_index("gx") * (rows + 2 * offset) + offset
-    index = start + jnp.arange(rows)
-    keep = (index >= 0) & (index < (rows + 2 * offset) * lax.axis_size("gx"))
-    return jnp.where(keep[:, None, None, None], field, jnp.zeros_like(field))
+def inside_rows(field, offset, dim=0):
+    rows = field.shape[dim]
+    own = rows + 2 * offset
+    index = lax.axis_index("gx") * own + offset + jnp.arange(rows)
+    keep = (index >= 0) & (index < own * lax.axis_size("gx"))
+    shape = [1] * field.ndim
+    shape[dim] = rows
+    return jnp.where(keep.reshape(shape), field, jnp.zeros_like(field))
 
 
 def unfold(weight, side, first, second):
@@ -279,12 +281,12 @@
     w_fine_dec,
     w_head,
 ):
-    fields = extended(inputs.transpose(1, 0, 2, 3), (("gx", 0, 4),))
-    first = inside_rows(fine_conv(fields, w_in, FINE_CROSS).astype(jnp.bfloat16), -3)
-    fine_wide = inside_rows(fine_conv(first, w_fine_enc, FINE_CROSS).astype(jnp.bfloat16), -2)
-    fine_skip = fine_wide[2:-2]
+    fields = extended(inputs.transpose(1, 0, 2, 3), (("gx", 0, inputs.shape[1]),))
+    first = inside_rows(fine_conv(fields, w_in, FINE_CROSS).astype(jnp.bfloat16), -7)
+    fine_wide = inside_rows(fine_conv(first, w_fine_enc, FINE_CROSS).astype(jnp.bfloat16), -6)
     mid_in = activate(fine_down(fine_wide, w_down_mid))
-    mid_skip = mid_conv(mid_in, w_mid_enc, MID_CROSS)
+    mid_wide = inside_rows(mid_conv(mid_in, w_mid_enc, MID_CROSS), -2, 1)
+    mid_skip = mid_wide[:, 2:-2]
     bottom = activate(conv_down(mid_skip, unfold(w_down_bottom, 2, C2, C1)))
     chans, sx, sv, ss = bottom.shape
     flat = bottom.reshape(chans, sx, sv * ss)
@@ -294,16 +296,22 @@
     keys = split_heads(w_key, normed)
     values = split_heads(w_value, normed)
     result = finish(rows, combine(queries, keys, values), w_attn_out)
-    mixed = lax.all_to_all(result, "gx", split_axis=1, concat_axis=2, tiled=True)
-    bottom_out = mixed.reshape(chans, sx, sv, ss)
+    count = result.shape[2]
+    groups = result.shape[1] // sx
+    rim = jnp.pad(result, ((0, 0), (1, 1), (0, 0)))
+    low = rim[:, : groups * sx].reshape(chans, groups, sx, count)
+    high = rim[:, 2 : groups * sx + 2].reshape(chans, groups, sx, count)
+    windows = jnp.concatenate([low, high], axis=2).reshape(chans, groups * 2 * sx, count)
+    mixed = lax.all_to_all(windows, "gx", split_axis=1, concat_axis=2, tiled=True)
+    bottom_out = mixed.reshape(chans, 2 * sx, sv, ss)
     mid_up = (
-        conv_up(bottom_out, unfold(w_up_mid, 2, C2, C1)) + mid_skip.astype(jnp.float32)
+        conv_up(bottom_out, unfold(w_up_mid, 2, C2, C1)) + mid_wide.astype(jnp.float32)
     ).astype(jnp.bfloat16)
-    mid_dec = mid_conv(mid_up, w_mid_dec)
-    fine_up_field = (fine_up(mid_dec, w_up_fine) + fine_skip.astype(jnp.float32)).astype(
+    mid_dec = inside_rows(mid_conv(mid_up, w_mid_dec, MID_CROSS), -1, 1)
+    fine_up_field = (fine_up(mid_dec, w_up_fine) + fine_wide[4:-4].astype(jnp.float32)).astype(
         jnp.bfloat16
     )
-    return fine_conv(fine_up_field, w_fine_dec, FINE_SIDES, head=w_head)
+    return fine_conv(fine_up_field[1:-1], w_fine_dec, FINE_CROSS, head=w_head)
 
 
 def solution(mesh):

time: 233 us -> 235 us (level)
  the two profiles are of different devices: /device:TPU:30 before, /device:TPU:1 now
where the time goes in v3:
time: 235 us; the launch traced here: 234 us
  Pallas kernels  48.9 us (21%)
  starting transfers between devices  46 us (20%)
  waiting for transfers between devices  43.4 us (18%)
  local copies, waits for them, and re-layouts  37.7 us (16%)
  blocking collectives  28.5 us (12%)
  other arithmetic  20.6 us (9%)
  matrix products  8.21 us (3%)
    pallas_call x3, Pallas kernels, fine_conv(): pl.pallas_call(kernel, out_shape=out_shape, scratch_shapes=[pltpu.VMEM((c...  35 us
    all_to_all x1, blocking collectives, on_device(): rows = lax.all_to_all(flat, 'gx', split_axis=2, concat_axis=1, tiled=True)  28.5 us
    ppermute x6, starting transfers between devices, extended(): low = lax.ppermute(top, axis, forward)  22.8 us
    ppermute x6, waiting for transfers between devices, extended(): high = lax.ppermute(bottom, axis, backward)  21.5 us
    pallas_call x2, Pallas kernels, mid_conv(): pl.pallas_call(kernel, out_shape=jax.ShapeDtypeStruct((sx, sv, cout, ss),...  13.9 us
    ppermute x5, starting transfers between devices, extended(): got = lax.ppermute(jnp.where(first, top, bottom), axis, [(0, 1), (1, 0)])  11.1 us
    all_to_all x1, waiting for transfers between devices, on_device(): lax.all_to_all(windows, 'gx', split_axis=1, concat_axis=2, tiled=True)  10.8 us
    concatenate x4, other arithmetic, extended(): block = jnp.concatenate([low, block, high], axis=dim)  9.83 us
  transfers between devices with their start and end apart: 18, of which 15 were waited for; matrix products, arithmetic and copies ran while one was open for 3% of the time, Pallas kernels for 0%

profile of v3, /device:TPU:1, one launch (start us, length us, event | category | flops | bytes accessed | tf_op | source)
XLA Modules:
  0.0 234.1 jit_solution(17306543784209906522)
XLA Ops:
  0.0 4.1 %collective-permute-start = (bf16[8,4,8,128]{3,2,0,1:T(8,128)(2,1)}, bf16[8,4,8,128]{3,2,0,1:T(8,128)(2,1)S(1)}, u32[]{:S(2)}, u32[]{:S(2)}) collective-permute-start(bf16[8,4,8,128]{3,2,0,1:T(8,128)(2,1)} %bitcast.158), channel_id=1, source_target_pairs={{0,8},{8,16},{16,24},{24,32},{32,40},{40,48},{48,56},{56,64},{64,7... | collective-permute-start | bytes 196616 | tf_op jit(solution)/shard_map/ppermute | solution.py:33
  5.7 3.6 %collective-permute-done.1 = bf16[8,4,8,128]{3,2,0,1:T(8,128)(2,1)S(1)} collective-permute-done((bf16[8,4,8,128]{3,2,0,1:T(8,128)(2,1)}, bf16[8,4,8,128]{3,2,0,1:T(8,128)(2,1)S(1)}, u32[]{:S(2)}, u32[]{:S(2)}) %collective-permute-start.1) | collective-permute-done | bytes 65568 | tf_op jit(solution)/shard_map/ppermute | solution.py:34
  14.1 3.5 %collective-permute-start.3 = (bf16[24,4,1,130]{3,2,0,1:T(2,128)(2,1)S(1)}, bf16[24,4,1,130]{3,2,0,1:T(2,128)(2,1)S(1)}, u32[]{:S(2)}, u32[]{:S(2)}) collective-permute-start(bf16[24,4,1,130]{3,2,0,1:T(2,128)(2,1)S(1)} %get-tuple-element.13), channel_id=1, source_target_pairs={{0,1},{1,2},{2,3},{4,5},{5,6},{6,7},{8,9},{9,10},{10,11},{12,13},{... | collective-permute-start | bytes 74888 | tf_op jit(solution)/shard_map/ppermute | solution.py:33
  19.7 3.9 %collective-permute-done.4 = bf16[24,4,1,130]{3,2,0,1:T(2,128)(2,1)S(1)} collective-permute-done((bf16[24,4,1,130]{3,2,0,1:T(2,128)(2,1)S(1)}, bf16[24,4,1,130]{3,2,0,1:T(2,128)(2,1)S(1)}, u32[]{:S(2)}, u32[]{:S(2)}) %collective-permute-start.4) | collective-permute-done | bytes 24992 | tf_op jit(solution)/shard_map/ppermute | solution.py:34
  26.0 11.1 %shard_map.145 = f32[22,16,8,128]{3,2,1,0:T(8,128)} custom-call(bf16[24,128,256]{2,1,0:T(8,128)(2,1)} %bitcast.152, bf16[27,16,8]{2,1,0:T(8,128)(2,1)} %bitcast.165), custom_call_target="tpu_custom_call" | custom-call | tf_op jit(solution)/shard_map/pallas_call | solution.py:134
  47.1 4.4 %collective-permute-start.6 = (bf16[22,16,1,130]{3,2,1,0:T(2,128)(2,1)S(1)}, bf16[22,16,1,130]{3,2,1,0:T(2,128)(2,1)S(1)}, u32[]{:S(2)}, u32[]{:S(2)}) collective-permute-start(bf16[22,16,1,130]{3,2,1,0:T(2,128)(2,1)S(1)} %get-tuple-element.5), channel_id=1, source_target_pairs={{0,1},{1,2},{2,3},{4,5},{5,6},{6,7},{8,9},{9,10},{10,11},{12,13},{... | collective-permute-start | bytes 274568 | tf_op jit(solution)/shard_map/ppermute | solution.py:33
  52.9 5.9 %collective-permute-done.6 = bf16[22,16,1,130]{3,2,1,0:T(2,128)(2,1)S(1)} collective-permute-done((bf16[22,16,1,130]{3,2,1,0:T(2,128)(2,1)S(1)}, bf16[22,16,1,130]{3,2,1,0:T(2,128)(2,1)S(1)}, u32[]{:S(2)}, u32[]{:S(2)}) %collective-permute-start.6) | collective-permute-done | bytes 91552 | tf_op jit(solution)/shard_map/ppermute | solution.py:33
  58.9 3.8 %collective-permute-done.7 = bf16[22,16,1,130]{3,2,1,0:T(2,128)(2,1)S(1)} collective-permute-done((bf16[22,16,1,130]{3,2,1,0:T(2,128)(2,1)S(1)}, bf16[22,16,1,130]{3,2,1,0:T(2,128)(2,1)S(1)}, u32[]{:S(2)}, u32[]{:S(2)}) %collective-permute-start.7) | collective-permute-done | bytes 91552 | tf_op jit(solution)/shard_map/ppermute | solution.py:34
  62.7 5.4 %fusion.11 = bf16[22,16,16,256]{3,2,1,0:T(8,128)(2,1)} fusion(bf16[22,16,1,130]{3,2,1,0:T(2,128)(2,1)S(1)} %collective-permute-done.7, bf16[22,16,1,130]{3,2,1,0:T(2,128)(2,1)S(1)} %collective-permute-done.6, bf16[22,16,8,1]{3,2,1,0:T(8,128)(2,1)S(1)} %copy.135, bf16[22,16,8,128]{3,2,1,0:T(8,128)(2,1)S(1)} %convert_select_fusion, ...), kind=kLoop, calls=%fused_computation.13 | loop fusion | flops 33161216 | bytes 3798784 | tf_op jit(solution)/shard_map/concatenate | solution.py:35
  68.0 14.7 %shard_map.146 = f32[20,16,8,128]{3,2,1,0:T(8,128)} custom-call(bf16[22,256,256]{2,1,0:T(8,128)(2,1)} %bitcast.151, bf16[27,16,16]{2,1,0:T(8,128)(2,1)} %bitcast.168), custom_call_target="tpu_custom_call" | custom-call | tf_op jit(solution)/shard_map/pallas_call | solution.py:134
  87.8 3.8 %multiply_convert_fusion = bf16[64,10,4,64]{0,3,2,1:T(8,128)(2,1)S(1)} fusion(bf16[10,2,16,4,2,64,2]{2,6,5,4,3,1,0:T(2,128)(2,1)} %bitcast.153, bf16[64,16,2,2,2,1,1]{0,4,3,2,1,6,5:T(2,128)(2,1)S(1)} %bitcast.171), kind=kOutput, calls=%fused_computation.40 | convolution fusion | flops 42762240 | bytes 999424 | tf_op jit(solution)/shard_map/xaivbsc,oiabc->oxvs/dot_general | solution.py:218
  98.0 4.0 %collective-permute-start.9 = (bf16[64,10,1,66]{0,3,2,1:T(8,128)(2,1)S(1)}, bf16[64,10,1,66]{0,3,2,1:T(8,128)(2,1)S(1)}, u32[]{:S(2)}, u32[]{:S(2)}) collective-permute-start(bf16[64,10,1,66]{0,3,2,1:T(8,128)(2,1)S(1)} %get-tuple-element.11), channel_id=1, source_target_pairs={{0,1},{1,2},{2,3},{4,5},{5,6},{6,7},{8,9},{9,10},{10,11},{12,13},{... | collective-permute-start | bytes 253448 | tf_op jit(solution)/shard_map/ppermute | solution.py:33
  108.0 7.6 %shard_map.147 = f32[8,4,64,64]{3,2,1,0:T(8,128)} custom-call(bf16[10,64,512]{2,1,0:T(8,128)(2,1)} %pad.31.refs_0_, bf16[64,1728]{1,0:T(8,128)(2,1)} %reshape.142.refs_1_), custom_call_target="tpu_custom_call" | custom-call | tf_op jit(solution)/shard_map/pallas_call | solution.py:196
  118.8 28.5 %all_to_all.24 = bf16[256,2,64]{0,1,2:T(2,128)(2,1)S(1)} all-to-all(bf16[256,2,64]{0,1,2:T(2,128)(2,1)S(1)} %copy.142), channel_id=1, replica_groups=mesh['gx'=32,'gy'=2,'gz'=4] {'gx'}, dimensions={2} | all-to-all | bytes 131072 | tf_op jit(solution)/shard_map/all_to_all | solution.py:293
  151.1 3.9 %all-to-all-start.1 = ((bf16[256,128,2]{0,2,1:T(2,128)(2,1)}), bf16[256,128,2]{0,2,1:T(2,128)(2,1)S(1)}, u32[]{:S(2)}, u32[]{:S(2)}) async-start(bf16[256,128,2]{0,2,1:T(2,128)(2,1)} %bitcast.31), calls=%async_computation.1 | async-start | bytes 262144 | tf_op jit(solution)/shard_map/all_to_all | solution.py:305
  155.5 10.8 %all-to-all-done.1 = bf16[256,128,2]{0,2,1:T(2,128)(2,1)S(1)} async-done(((bf16[256,128,2]{0,2,1:T(2,128)(2,1)}), bf16[256,128,2]{0,2,1:T(2,128)(2,1)S(1)}, u32[]{:S(2)}, u32[]{:S(2)}) %all-to-all-start.1) | async-done | bytes 131104 | tf_op jit(solution)/shard_map/all_to_all | solution.py:305
  170.8 3.8 %collective-permute-start.11 = (bf16[64,8,4,1]{3,0,2,1:T(8,128)(2,1)S(1)}, bf16[64,8,4,1]{3,0,2,1:T(8,128)(2,1)S(1)}, u32[]{:S(2)}, u32[]{:S(2)}) collective-permute-start(bf16[64,8,4,1]{3,0,2,1:T(8,128)(2,1)S(1)} %slice_select_fusion.1), channel_id=1, source_target_pairs={{0,4},{4,0},{1,5},{5,1},{2,6},{6,2},{3,7},{7,3},{8,12},{12,8},{9,1... | collective-permute-start | bytes 12296 | tf_op jit(solution)/shard_map/ppermute | solution.py:27
  176.8 4.9 %collective-permute-start.12 = (bf16[64,8,1,66]{3,0,2,1:T(8,128)(2,1)S(1)}, bf16[64,8,1,66]{3,0,2,1:T(8,128)(2,1)S(1)}, u32[]{:S(2)}, u32[]{:S(2)}) collective-permute-start(bf16[64,8,1,66]{3,0,2,1:T(8,128)(2,1)S(1)} %get-tuple-element.7), channel_id=1, source_target_pairs={{0,1},{1,2},{2,3},{4,5},{5,6},{6,7},{8,9},{9,10},{10,11},{12,13},{... | collective-permute-start | bytes 202760 | tf_op jit(solution)/shard_map/ppermute | solution.py:33
  183.9 3.5 %collective-permute-done.13 = bf16[64,8,1,66]{3,0,2,1:T(8,128)(2,1)S(1)} collective-permute-done((bf16[64,8,1,66]{3,0,2,1:T(8,128)(2,1)S(1)}, bf16[64,8,1,66]{3,0,2,1:T(8,128)(2,1)S(1)}, u32[]{:S(2)}, u32[]{:S(2)}) %collective-permute-start.13) | collective-permute-done | bytes 67616 | tf_op jit(solution)/shard_map/ppermute | solution.py:34
  190.0 6.2 %shard_map.148 = f32[6,4,64,64]{3,2,1,0:T(8,128)} custom-call(bf16[8,64,512]{2,1,0:T(8,128)(2,1)} %pad.33.refs_0_, bf16[64,1728]{1,0:T(8,128)(2,1)} %reshape.156.refs_1_), custom_call_target="tpu_custom_call" | custom-call | tf_op jit(solution)/shard_map/pallas_call | solution.py:196
  197.8 6.4 %copy.159 = f32[6,2,16,4,2,64,2]{2,6,5,4,3,1,0:T(2,128)} copy(f32[6,2,16,4,2,64,2]{5,2,6,4,1,3,0:T(8,128)S(1)} %convolution_bitcast_fusion) | data formatting | bytes 1572864 | tf_op jit(solution)/shard_map/ixvs,ioabc->xaovbsc/transpose | solution.py:222
  204.2 4.4 %copy.160 = f32[12,16,8,128]{3,2,1,0:T(8,128)S(1)} copy(f32[12,16,8,128]{1,3,2,0:T(8,128)} %bitcast.150) | data formatting | bytes 1572864 | tf_op jit(solution)/shard_map/reshape | solution.py:224
  218.3 3.8 %collective-permute-done.16 = bf16[10,16,1,130]{3,2,1,0:T(2,128)(2,1)S(1)} collective-permute-done((bf16[10,16,1,130]{3,2,1,0:T(2,128)(2,1)S(1)}, bf16[10,16,1,130]{3,2,1,0:T(2,128)(2,1)S(1)}, u32[]{:S(2)}, u32[]{:S(2)}) %collective-permute-start.16) | collective-permute-done | bytes 41632 | tf_op jit(solution)/shard_map/ppermute | solution.py:34
  224.8 9.2 %shard_map.149 = f32[4,8,8,128]{3,2,1,0:T(8,128)} custom-call(bf16[10,256,256]{2,1,0:T(8,128)(2,1)} %bitcast.154, bf16[27,16,16]{2,1,0:T(8,128)(2,1)} %bitcast.169, bf16[32,128]{1,0:T(8,128)(2,1)} %convert_element_type.135.refs_2_), custom_call_target="tpu_custom_call" | custom-call | tf_op jit(solution)/shard_map/pallas_call | solution.py:134
  (142 shorter events, 72.0 us)
Async XLA Ops:
  0.0 147.8 %copy-start = (bf16[256,256]{1,0:T(8,128)(2,1)S(1)}, bf16[256,256]{1,0:T(8,128)(2,1)}, u32[]{:S(2)}) copy-start(bf16[256,256]{1,0:T(8,128)(2,1)} %param.22) | copy-start | bytes 393220
  0.0 13.6 %copy-start.2 = (bf16[4,8,8,128]{3,2,1,0:T(8,128)(2,1)S(1)}, bf16[4,8,8,128]{3,2,1,0:T(8,128)(2,1)}, u32[]{:S(2)}) copy-start(bf16[4,8,8,128]{3,2,1,0:T(8,128)(2,1)} %param.15) | copy-start | bytes 196612
  0.0 5.7 %collective-permute-start = (bf16[8,4,8,128]{3,2,0,1:T(8,128)(2,1)}, bf16[8,4,8,128]{3,2,0,1:T(8,128)(2,1)S(1)}, u32[]{:S(2)}, u32[]{:S(2)}) collective-permute-start(bf16[8,4,8,128]{3,2,0,1:T(8,128)(2,1)} %bitcast.158), channel_id=1, source_target_pairs={{0,8},{8,16},{16,24},{24,32},{32,40},{40,48},{48,56},{56,64},{64,7... | collective-permute-start | bytes 196616 | tf_op jit(solution)/shard_map/ppermute | solution.py:33
  4.1 5.2 %collective-permute-start.1 = (bf16[8,4,8,128]{3,2,0,1:T(8,128)(2,1)}, bf16[8,4,8,128]{3,2,0,1:T(8,128)(2,1)S(1)}, u32[]{:S(2)}, u32[]{:S(2)}) collective-permute-start(bf16[8,4,8,128]{3,2,0,1:T(8,128)(2,1)} %bitcast.159), channel_id=1, source_target_pairs={{8,0},{16,8},{24,16},{32,24},{40,32},{48,40},{56,48},{64,56},{72,6... | collective-permute-start | bytes 196616 | tf_op jit(solution)/shard_map/ppermute | solution.py:34
  10.3 3.3 %collective-permute-start.2 = (bf16[24,4,8,1]{3,2,0,1:T(8,128)(2,1)S(1)}, bf16[24,4,8,1]{3,2,0,1:T(8,128)(2,1)S(1)}, u32[]{:S(2)}, u32[]{:S(2)}) collective-permute-start(bf16[24,4,8,1]{3,2,0,1:T(8,128)(2,1)S(1)} %slice_select_fusion.3), channel_id=1, source_target_pairs={{0,4},{4,0},{1,5},{5,1},{2,6},{6,2},{3,7},{7,3},{8,12},{12,8},{9,1... | collective-permute-start | bytes 4616 | tf_op jit(solution)/shard_map/ppermute | solution.py:27
  14.1 5.6 %collective-permute-start.3 = (bf16[24,4,1,130]{3,2,0,1:T(2,128)(2,1)S(1)}, bf16[24,4,1,130]{3,2,0,1:T(2,128)(2,1)S(1)}, u32[]{:S(2)}, u32[]{:S(2)}) collective-permute-start(bf16[24,4,1,130]{3,2,0,1:T(2,128)(2,1)S(1)} %get-tuple-element.13), channel_id=1, source_target_pairs={{0,1},{1,2},{2,3},{4,5},{5,6},{6,7},{8,9},{9,10},{10,11},{12,13},{... | collective-permute-start | bytes 74888 | tf_op jit(solution)/shard_map/ppermute | solution.py:33
  17.7 6.0 %collective-permute-start.4 = (bf16[24,4,1,130]{3,2,0,1:T(2,128)(2,1)S(1)}, bf16[24,4,1,130]{3,2,0,1:T(2,128)(2,1)S(1)}, u32[]{:S(2)}, u32[]{:S(2)}) collective-permute-start(bf16[24,4,1,130]{3,2,0,1:T(2,128)(2,1)S(1)} %get-tuple-element.14), channel_id=1, source_target_pairs={{1,0},{2,1},{3,2},{5,4},{6,5},{7,6},{9,8},{10,9},{11,10},{13,12},{... | collective-permute-start | bytes 74888 | tf_op jit(solution)/shard_map/ppermute | solution.py:34
  40.1 2.2 collective-permute-start.5
  47.1 11.8 %collective-permute-start.6 = (bf16[22,16,1,130]{3,2,1,0:T(2,128)(2,1)S(1)}, bf16[22,16,1,130]{3,2,1,0:T(2,128)(2,1)S(1)}, u32[]{:S(2)}, u32[]{:S(2)}) collective-permute-start(bf16[22,16,1,130]{3,2,1,0:T(2,128)(2,1)S(1)} %get-tuple-element.5), channel_id=1, source_target_pairs={{0,1},{1,2},{2,3},{4,5},{5,6},{6,7},{8,9},{9,10},{10,11},{12,13},{... | collective-permute-start | bytes 274568 | tf_op jit(solution)/shard_map/ppermute | solution.py:33
  51.5 11.2 %collective-permute-start.7 = (bf16[22,16,1,130]{3,2,1,0:T(2,128)(2,1)S(1)}, bf16[22,16,1,130]{3,2,1,0:T(2,128)(2,1)S(1)}, u32[]{:S(2)}, u32[]{:S(2)}) collective-permute-start(bf16[22,16,1,130]{3,2,1,0:T(2,128)(2,1)S(1)} %get-tuple-element.6), channel_id=1, source_target_pairs={{1,0},{2,1},{3,2},{5,4},{6,5},{7,6},{9,8},{10,9},{11,10},{13,12},{... | collective-permute-start | bytes 274568 | tf_op jit(solution)/shard_map/ppermute | solution.py:34
  91.7 4.8 %collective-permute-start.8 = (bf16[64,10,4,1]{0,3,2,1:T(2,128)(2,1)S(1)}, bf16[64,10,4,1]{0,3,2,1:T(2,128)(2,1)S(1)}, u32[]{:S(2)}, u32[]{:S(2)}) collective-permute-start(bf16[64,10,4,1]{0,3,2,1:T(2,128)(2,1)S(1)} %broadcast_select_fusion.8), channel_id=1, source_target_pairs={{0,4},{4,0},{1,5},{5,1},{2,6},{6,2},{3,7},{7,3},{8,12},{12,8},{9,1... | collective-permute-start | bytes 15368 | tf_op jit(solution)/shard_map/ppermute | solution.py:27
  96.7 8.1 %collective-permute-start.10 = (bf16[64,10,1,66]{0,3,2,1:T(8,128)(2,1)S(1)}, bf16[64,10,1,66]{0,3,2,1:T(8,128)(2,1)S(1)}, u32[]{:S(2)}, u32[]{:S(2)}) collective-permute-start(bf16[64,10,1,66]{0,3,2,1:T(8,128)(2,1)S(1)} %get-tuple-element.12), channel_id=1, source_target_pairs={{1,0},{2,1},{3,2},{5,4},{6,5},{7,6},{9,8},{10,9},{11,10},{13,12},{... | collective-permute-start | bytes 253448 | tf_op jit(solution)/shard_map/ppermute | solution.py:34
  98.0 7.7 %collective-permute-start.9 = (bf16[64,10,1,66]{0,3,2,1:T(8,128)(2,1)S(1)}, bf16[64,10,1,66]{0,3,2,1:T(8,128)(2,1)S(1)}, u32[]{:S(2)}, u32[]{:S(2)}) collective-permute-start(bf16[64,10,1,66]{0,3,2,1:T(8,128)(2,1)S(1)} %get-tuple-element.11), channel_id=1, source_target_pairs={{0,1},{1,2},{2,3},{4,5},{5,6},{6,7},{8,9},{9,10},{10,11},{12,13},{... | collective-permute-start | bytes 253448 | tf_op jit(solution)/shard_map/ppermute | solution.py:33
  118.6 29.5 %copy-start.9 = (bf16[256,256]{1,0:T(8,128)(2,1)S(1)}, bf16[256,256]{1,0:T(8,128)(2,1)}, u32[]{:S(2)}) copy-start(bf16[256,256]{1,0:T(8,128)(2,1)} %param.21) | copy-start | bytes 393220
  118.8 30.2 %copy-start.10 = (bf16[256,256]{1,0:T(8,128)(2,1)S(1)}, bf16[256,256]{1,0:T(8,128)(2,1)}, u32[]{:S(2)}) copy-start(bf16[256,256]{1,0:T(8,128)(2,1)} %param.23) | copy-start | bytes 393220
  149.3 5.7 %copy-start.5 = (bf16[8,16384]{1,0:T(8,128)(2,1)S(1)}, bf16[8,16384]{1,0:T(8,128)(2,1)}, u32[]{:S(2)}) copy-start(bf16[8,16384]{1,0:T(8,128)(2,1)} %param.25) | copy-start | bytes 786436
  151.1 15.3 %all-to-all-start.1 = ((bf16[256,128,2]{0,2,1:T(2,128)(2,1)}), bf16[256,128,2]{0,2,1:T(2,128)(2,1)S(1)}, u32[]{:S(2)}, u32[]{:S(2)}) async-start(bf16[256,128,2]{0,2,1:T(2,128)(2,1)} %bitcast.31), calls=%async_computation.1 | async-start | bytes 262144 | tf_op jit(solution)/shard_map/all_to_all | solution.py:305
  170.8 5.7 %collective-permute-start.11 = (bf16[64,8,4,1]{3,0,2,1:T(8,128)(2,1)S(1)}, bf16[64,8,4,1]{3,0,2,1:T(8,128)(2,1)S(1)}, u32[]{:S(2)}, u32[]{:S(2)}) collective-permute-start(bf16[64,8,4,1]{3,0,2,1:T(8,128)(2,1)S(1)} %slice_select_fusion.1), channel_id=1, source_target_pairs={{0,4},{4,0},{1,5},{5,1},{2,6},{6,2},{3,7},{7,3},{8,12},{12,8},{9,1... | collective-permute-start | bytes 12296 | tf_op jit(solution)/shard_map/ppermute | solution.py:27
  176.8 7.1 %collective-permute-start.12 = (bf16[64,8,1,66]{3,0,2,1:T(8,128)(2,1)S(1)}, bf16[64,8,1,66]{3,0,2,1:T(8,128)(2,1)S(1)}, u32[]{:S(2)}, u32[]{:S(2)}) collective-permute-start(bf16[64,8,1,66]{3,0,2,1:T(8,128)(2,1)S(1)} %get-tuple-element.7), channel_id=1, source_target_pairs={{0,1},{1,2},{2,3},{4,5},{5,6},{6,7},{8,9},{9,10},{10,11},{12,13},{... | collective-permute-start | bytes 202760 | tf_op jit(solution)/shard_map/ppermute | solution.py:33
  181.7 5.7 %collective-permute-start.13 = (bf16[64,8,1,66]{3,0,2,1:T(8,128)(2,1)S(1)}, bf16[64,8,1,66]{3,0,2,1:T(8,128)(2,1)S(1)}, u32[]{:S(2)}, u32[]{:S(2)}) collective-permute-start(bf16[64,8,1,66]{3,0,2,1:T(8,128)(2,1)S(1)} %get-tuple-element.8), channel_id=1, source_target_pairs={{1,0},{2,1},{3,2},{5,4},{6,5},{7,6},{9,8},{10,9},{11,10},{13,12},{... | collective-permute-start | bytes 202760 | tf_op jit(solution)/shard_map/ppermute | solution.py:34
  189.1 7.2 %copy-start.11 = (bf16[64,16,2,2,2]{0,4,3,2,1:T(2,128)(2,1)S(1)}, bf16[64,16,2,2,2]{0,4,3,2,1:T(2,128)(2,1)}, u32[]{:S(2)}) copy-start(bf16[64,16,2,2,2]{0,4,3,2,1:T(2,128)(2,1)} %param.27) | copy-start | bytes 49156
  208.9 3.4 %collective-permute-start.14 = (bf16[10,16,8,1]{3,2,1,0:T(8,128)(2,1)S(1)}, bf16[10,16,8,1]{3,2,1,0:T(8,128)(2,1)S(1)}, u32[]{:S(2)}, u32[]{:S(2)}) collective-permute-start(bf16[10,16,8,1]{3,2,1,0:T(8,128)(2,1)S(1)} %slice_select_fusion.2), channel_id=1, source_target_pairs={{0,4},{4,0},{1,5},{5,1},{2,6},{6,2},{3,7},{7,3},{8,12},{12,8},{9,1... | collective-permute-start | bytes 7688 | tf_op jit(solution)/shard_map/ppermute | solution.py:27
  213.2 5.1 %collective-permute-start.15 = (bf16[10,16,1,130]{3,2,1,0:T(2,128)(2,1)S(1)}, bf16[10,16,1,130]{3,2,1,0:T(2,128)(2,1)S(1)}, u32[]{:S(2)}, u32[]{:S(2)}) collective-permute-start(bf16[10,16,1,130]{3,2,1,0:T(2,128)(2,1)S(1)} %get-tuple-element.9), channel_id=1, source_target_pairs={{0,1},{1,2},{2,3},{4,5},{5,6},{6,7},{8,9},{9,10},{10,11},{12,13},{... | collective-permute-start | bytes 124808 | tf_op jit(solution)/shard_map/ppermute | solution.py:33
  215.1 7.0 %collective-permute-start.16 = (bf16[10,16,1,130]{3,2,1,0:T(2,128)(2,1)S(1)}, bf16[10,16,1,130]{3,2,1,0:T(2,128)(2,1)S(1)}, u32[]{:S(2)}, u32[]{:S(2)}) collective-permute-start(bf16[10,16,1,130]{3,2,1,0:T(2,128)(2,1)S(1)} %get-tuple-element.10), channel_id=1, source_target_pairs={{1,0},{2,1},{3,2},{5,4},{6,5},{7,6},{9,8},{10,9},{11,10},{13,12},{... | collective-permute-start | bytes 124808 | tf_op jit(solution)/shard_map/ppermute | solution.py:34
  (8 other events, 23.9 us)

commit v4 on v3

--- a/solution.py
+++ b/solution.py
@@ -54,14 +54,13 @@
     return (value + step - 1) // step * step
 
 
-def fine_kernel(p_ref, w_ref, *rest, sx, sv, ss, rows, head):
+def fine_kernel(p_ref, e_ref, w_ref, *rest, sx, sv, ss, rows, head):
     if head:
         h_ref, o_ref, band_ref, shifted_ref = rest
     else:
         o_ref, band_ref, shifted_ref = rest
     cout, cin = w_ref.shape[1:]
     depth = cin * rows
-    lanes = p_ref.shape[-1]
     sv_bits, row_bits = sv.bit_length() - 1, rows.bit_length() - 1
     r = lax.broadcasted_iota(jnp.int32, (cout * sv, cout), 0)
     q = lax.broadcasted_iota(jnp.int32, (cout * sv, cout), 1)
@@ -71,7 +70,9 @@
     widen_cols = ((q >> row_bits) == r).astype(jnp.bfloat16)
     r = lax.broadcasted_iota(jnp.int32, (cout * sv, depth), 0)
     q = lax.broadcasted_iota(jnp.int32, (cout * sv, depth), 1)
-    offset = (q & (rows - 1)) - (r & (sv - 1))
+    w = q & (rows - 1)
+    place = jnp.where(w < sv, w + 1, jnp.where(w == sv, 0, jnp.where(w == sv + 1, sv + 1, -8)))
+    offset = place - (r & (sv - 1))
     for a in range(3):
         for c in range(3):
             band = jnp.zeros((cout * sv, depth), jnp.float32)
@@ -84,11 +85,16 @@
                 band = band + jnp.where(offset == b, grown, 0.0)
             band_ref[:, pl.ds((a * 3 + c) * depth, depth)] = band.astype(jnp.bfloat16)
 
+    lane = lax.broadcasted_iota(jnp.int32, (depth, ss), 1)
+
     def shift(x, carry):
         slab = p_ref[x].astype(jnp.float32)
-        for c in range(3):
-            piece = slab if c == 0 else pltpu.roll(slab, lanes - c, 1)
-            shifted_ref[x, c] = piece[:, :ss].astype(jnp.bfloat16)
+        edges = jnp.transpose(e_ref[x].astype(jnp.float32))
+        low = jnp.where(lane == 0, edges[:, 0:1], pltpu.roll(slab, 1, 1))
+        high = jnp.where(lane == ss - 1, edges[:, 1:2], pltpu.roll(slab, ss - 1, 1))
+        shifted_ref[x, 0] = low.astype(jnp.bfloat16)
+        shifted_ref[x, 1] = slab.astype(jnp.bfloat16)
+        shifted_ref[x, 2] = high.astype(jnp.bfloat16)
         return carry
 
     lax.fori_loop(0, sx + 2, shift, 0)
@@ -107,20 +113,35 @@
     lax.fori_loop(0, sx, row, 0)
 
 
-def fine_conv(field, weight, sides, head=None):
-    _, cin, sv, ss = field.shape
+def faces(block, axis, dim):
+    count = lax.axis_size(axis)
+    top = lax.slice_in_dim(block, block.shape[dim] - 1, None, axis=dim)
+    bottom = lax.slice_in_dim(block, 0, 1, axis=dim)
+    if count == 2:
+        first = lax.axis_index(axis) == 0
+        got = lax.ppermute(jnp.where(first, top, bottom), axis, [(0, 1), (1, 0)])
+        return jnp.where(first, jnp.zeros_like(got), got), jnp.where(first, got, jnp.zeros_like(got))
+    forward = [(i, i + 1) for i in range(count - 1)]
+    backward = [(target, source) for source, target in forward]
+    return lax.ppermute(top, axis, forward), lax.ppermute(bottom, axis, backward)
+
+
+def fine_conv(field, weight, head=None):
+    rows_x, cin, sv, ss = field.shape
+    sx = rows_x - 2
     cout = weight.shape[0]
     rows = round_up(sv + 2, 16)
-    lanes = round_up(ss + 2, 128)
     wide = round_up(cin * rows, 128) // rows
-    padded = extended(field, sides)
-    sx = padded.shape[0] - 2
-    padded = jnp.pad(
-        padded, ((0, 0), (0, wide - cin), (0, rows - sv - 2), (0, lanes - ss - 2))
-    )
-    padded = padded.reshape(sx + 2, wide * rows, lanes)
+    block = jnp.pad(field, ((0, 0), (0, wide - cin), (0, 0), (0, 0)))
+    below, above = faces(block, "gz", 2)
+    spare = jnp.zeros((rows_x, wide, rows - sv - 2, ss), block.dtype)
+    padded = jnp.concatenate([block, below, above, spare], axis=2)
+    left, right = faces(padded, "gy", 3)
+    edges = jnp.concatenate([left, right], axis=3).transpose(0, 3, 1, 2)
+    edges = jnp.pad(edges.reshape(rows_x, 2, wide * rows), ((0, 0), (0, 6), (0, 0)))
+    padded = padded.reshape(rows_x, wide * rows, ss)
     taps = jnp.pad(weight, ((0, 0), (0, wide - cin), (0, 0), (0, 0), (0, 0)))
-    operands = [padded, taps.transpose(2, 3, 4, 0, 1).reshape(27, cout, wide)]
+    operands = [padded, edges, taps.transpose(2, 3, 4, 0, 1).reshape(27, cout, wide)]
     if head is None:
         out_shape = jax.ShapeDtypeStruct((sx, cout, sv, ss), jnp.float32)
     else:
@@ -139,17 +160,6 @@
             pltpu.VMEM((sx + 2, 3, wide * rows, ss), jnp.bfloat16),
         ],
     )(*operands)
-
-
-def conv_valid(padded, weight):
-    return lax.conv_general_dilated(
-        padded[None],
-        weight,
-        (1, 1, 1),
-        "VALID",
-        dimension_numbers=NUMS,
-        preferred_element_type=jnp.float32,
-    )[0]
 
 
 def mid_kernel(p_ref, w_ref, o_ref, shifted_ref, *, sx, sv, ss, span):
@@ -282,8 +292,8 @@
     w_head,
 ):
     fields = extended(inputs.transpose(1, 0, 2, 3), (("gx", 0, inputs.shape[1]),))
-    first = inside_rows(fine_conv(fields, w_in, FINE_CROSS).astype(jnp.bfloat16), -7)
-    fine_wide = inside_rows(fine_conv(first, w_fine_enc, FINE_CROSS).astype(jnp.bfloat16), -6)
+    first = inside_rows(fine_conv(fields, w_in).astype(jnp.bfloat16), -7)
+    fine_wide = inside_rows(fine_conv(first, w_fine_enc).astype(jnp.bfloat16), -6)
     mid_in = activate(fine_down(fine_wide, w_down_mid))
     mid_wide = inside_rows(mid_conv(mid_in, w_mid_enc, MID_CROSS), -2, 1)
     mid_skip = mid_wide[:, 2:-2]
@@ -311,7 +321,7 @@
     fine_up_field = (fine_up(mid_dec, w_up_fine) + fine_wide[4:-4].astype(jnp.float32)).astype(
         jnp.bfloat16
     )
-    return fine_conv(fine_up_field[1:-1], w_fine_dec, FINE_CROSS, head=w_head)
+    return fine_conv(fine_up_field[1:-1], w_fine_dec, head=w_head)
 
 
 def solution(mesh):

time: 235 us -> 229 us (0.974)
  other arithmetic: 20.6 us -> 9.91 us
  local copies, waits for them, and re-layouts: 37.7 us -> 43.1 us
  waiting for transfers between devices: 43.4 us -> 38.6 us
  Pallas kernels: 48.9 us -> 53 us
    ppermute x0 -> x9, starting transfers between devices: none -> 21.3 us  [the longest x3 9.02 us: faces(): lax.ppermute(top, axis, forward)]
    ppermute x0 -> x9, waiting for transfers between devices: none -> 16.1 us  [the longest x3 12.8 us: faces(): lax.ppermute(bottom, axis, backward)]
    ppermute x6 -> x3, waiting for transfers between devices: 21.5 us -> 9.91 us  [extended(): high = lax.ppermute(bottom, axis, backward)]
    ppermute x6 -> x3, starting transfers between devices: 22.8 us -> 12.8 us  [extended(): low = lax.ppermute(top, axis, forward)]
    concatenate x4 -> x1, other arithmetic: 9.83 us -> 0.05 us  [extended(): block = jnp.concatenate([low, block, high], axis=dim)]
    ppermute x6 -> x3, waiting for transfers between devices: 8.73 us -> 1.73 us  [extended(): low = lax.ppermute(top, axis, forward)]
    ppermute x5 -> x2, starting transfers between devices: 11.1 us -> 4.38 us  [extended(): got = lax.ppermute(jnp.where(first, top, bottom), axis, [(0, 1), (1, 0)])]
    ppermute x6 -> x3, starting transfers between devices: 8.19 us -> 3.88 us  [extended(): high = lax.ppermute(bottom, axis, backward)]
  transfers between devices with their start and end apart: 18 -> 18, of which waited for: 15 -> 13; matrix products, arithmetic and copies ran while one was open for 3% -> 4% of each run, Pallas kernels for 0% -> 0%
where the time goes in v4:
time: 229 us; the launch traced here: 228 us
  Pallas kernels  53 us (23%)
  starting transfers between devices  46.5 us (20%)
  local copies, waits for them, and re-layouts  43.1 us (19%)
  waiting for transfers between devices  38.6 us (17%)
  blocking collectives  27.8 us (12%)
  other arithmetic  9.91 us (4%)
  matrix products  8.2 us (4%)
    pallas_call x3, Pallas kernels, fine_conv(): pl.pallas_call(kernel, out_shape=out_shape, scratch_shapes=[pltpu.VMEM((c...  39.1 us
    all_to_all x1, blocking collectives, on_device(): rows = lax.all_to_all(flat, 'gx', split_axis=2, concat_axis=1, tiled=True)  27.8 us
    pallas_call x2, Pallas kernels, mid_conv(): pl.pallas_call(kernel, out_shape=jax.ShapeDtypeStruct((sx, sv, cout, ss),...  13.9 us
    ppermute x3, starting transfers between devices, extended(): low = lax.ppermute(top, axis, forward)  12.8 us
    ppermute x3, waiting for transfers between devices, faces(): lax.ppermute(bottom, axis, backward)  12.8 us
    all_to_all x1, waiting for transfers between devices, on_device(): lax.all_to_all(windows, 'gx', split_axis=1, concat_axis=2, tiled=True)  10.8 us
    ppermute x3, waiting for transfers between devices, extended(): high = lax.ppermute(bottom, axis, backward)  9.91 us
    ppermute x3, starting transfers between devices, faces(): lax.ppermute(top, axis, forward)  9.02 us
  transfers between devices with their start and end apart: 18, of which 13 were waited for; matrix products, arithmetic and copies ran while one was open for 4% of the time, Pallas kernels for 0%

profile of v4, /device:TPU:1, one launch (start us, length us, event | category | flops | bytes accessed | tf_op | source)
XLA Modules:
  0.0 228.0 jit_solution(38110313192951012)
XLA Ops:
  0.9 3.9 %collective-permute-start = (bf16[8,4,8,128]{3,2,1,0:T(8,128)(2,1)S(1)}, bf16[8,4,8,128]{3,2,1,0:T(8,128)(2,1)S(1)}, u32[]{:S(2)}, u32[]{:S(2)}) collective-permute-start(bf16[8,4,8,128]{3,2,1,0:T(8,128)(2,1)S(1)} %bitcast.175), channel_id=1, source_target_pairs={{0,8},{8,16},{16,24},{24,32},{32,40},{40,48},{48,56},{56,64},{64,7... | collective-permute-start | bytes 196616 | tf_op jit(solution)/shard_map/ppermute | solution.py:33
  6.2 3.7 %collective-permute-done.1 = bf16[8,4,8,128]{3,2,1,0:T(8,128)(2,1)S(1)} collective-permute-done((bf16[8,4,8,128]{3,2,1,0:T(8,128)(2,1)S(1)}, bf16[8,4,8,128]{3,2,1,0:T(8,128)(2,1)S(1)}, u32[]{:S(2)}, u32[]{:S(2)}) %collective-permute-start.1) | collective-permute-done | bytes 65568 | tf_op jit(solution)/shard_map/ppermute | solution.py:34
  10.1 3.5 %collective-permute-start.2 = (bf16[24,8,1,128]{3,2,1,0:T(2,128)(2,1)S(1)}, bf16[24,8,1,128]{3,2,1,0:T(2,128)(2,1)S(1)}, u32[]{:S(2)}, u32[]{:S(2)}) collective-permute-start(bf16[24,8,1,128]{3,2,1,0:T(2,128)(2,1)S(1)} %get-tuple-element.17), channel_id=1, source_target_pairs={{0,1},{1,2},{2,3},{4,5},{5,6},{6,7},{8,9},{9,10},{10,11},{12,13},{... | collective-permute-start | bytes 147464 | tf_op jit(solution)/shard_map/ppermute | solution.py:126
  22.6 3.4 %collective-permute-start.4 = (bf16[24,8,16,1]{0,2,3,1:T(8,128)(2,1)S(1)}, bf16[24,8,16,1]{0,2,3,1:T(8,128)(2,1)S(1)}, u32[]{:S(2)}, u32[]{:S(2)}) collective-permute-start(bf16[24,8,16,1]{0,2,3,1:T(8,128)(2,1)S(1)} %broadcast_select_fusion.11), channel_id=1, source_target_pairs={{0,4},{4,0},{1,5},{5,1},{2,6},{6,2},{3,7},{7,3},{8,12},{12,8},{9,1... | collective-permute-start | bytes 18440 | tf_op jit(solution)/shard_map/ppermute | solution.py:122
  27.9 13.3 %shard_map.145 = f32[22,16,8,128]{3,2,1,0:T(8,128)} custom-call(bf16[24,128,128]{2,1,0:T(8,128)(2,1)} %bitcast.166, bf16[24,8,128]{2,1,0:T(8,128)(2,1)} %pad.33.refs_1_, bf16[27,16,8]{2,1,0:T(8,128)(2,1)} %bitcast.174), custom_call_target="tpu_custom_call" | custom-call | tf_op jit(solution)/shard_map/pallas_call | solution.py:155
  43.0 3.6 %collective-permute-start.5 = (bf16[22,16,1,128]{3,2,1,0:T(2,128)(2,1)S(1)}, bf16[22,16,1,128]{3,2,1,0:T(2,128)(2,1)S(1)}, u32[]{:S(2)}, u32[]{:S(2)}) collective-permute-start(bf16[22,16,1,128]{3,2,1,0:T(2,128)(2,1)S(1)} %get-tuple-element.9), channel_id=1, source_target_pairs={{0,1},{1,2},{2,3},{4,5},{5,6},{6,7},{8,9},{9,10},{10,11},{12,13},{... | collective-permute-start | bytes 270344 | tf_op jit(solution)/shard_map/ppermute | solution.py:126
  50.1 5.7 %collective-permute-done.6 = bf16[22,16,1,128]{3,2,1,0:T(2,128)(2,1)S(1)} collective-permute-done((bf16[22,16,1,128]{3,2,1,0:T(2,128)(2,1)S(1)}, bf16[22,16,1,128]{3,2,1,0:T(2,128)(2,1)S(1)}, u32[]{:S(2)}, u32[]{:S(2)}) %collective-permute-start.6) | collective-permute-done | bytes 90144 | tf_op jit(solution)/shard_map/ppermute | solution.py:126
  63.7 16.0 %shard_map.146 = f32[20,16,8,128]{3,2,1,0:T(8,128)} custom-call(bf16[22,256,128]{2,1,0:T(8,128)(2,1)} %bitcast.165, bf16[22,8,256]{2,1,0:T(8,128)(2,1)} %pad.35.refs_1_, bf16[27,16,16]{2,1,0:T(8,128)(2,1)} %bitcast.180), custom_call_target="tpu_custom_call" | custom-call | tf_op jit(solution)/shard_map/pallas_call | solution.py:155
  81.3 3.5 %copy.161 = bf16[20,16,8,128]{1,3,2,0:T(8,128)(2,1)} copy(bf16[20,16,8,128]{3,2,1,0:T(8,128)(2,1)S(1)} %convert_select_fusion.1) | data formatting | bytes 1310720 | tf_op jit(solution)/shard_map/jit(_where)/select_n | solution.py:46
  84.8 3.8 %multiply_convert_fusion = bf16[64,10,4,64]{0,3,2,1:T(8,128)(2,1)S(1)} fusion(bf16[10,2,16,4,2,64,2]{2,6,5,4,3,1,0:T(2,128)(2,1)} %bitcast.168, bf16[64,16,2,2,2,1,1]{0,4,3,2,1,6,5:T(2,128)(2,1)S(1)} %bitcast.183), kind=kOutput, calls=%fused_computation.8 | convolution fusion | flops 42762240 | bytes 999424 | tf_op jit(solution)/shard_map/xaivbsc,oiabc->oxvs/dot_general | solution.py:228
  93.8 4.0 %collective-permute-start.9 = (bf16[64,10,1,66]{0,3,2,1:T(8,128)(2,1)S(1)}, bf16[64,10,1,66]{0,3,2,1:T(8,128)(2,1)S(1)}, u32[]{:S(2)}, u32[]{:S(2)}) collective-permute-start(bf16[64,10,1,66]{0,3,2,1:T(8,128)(2,1)S(1)} %get-tuple-element.11), channel_id=1, source_target_pairs={{0,1},{1,2},{2,3},{4,5},{5,6},{6,7},{8,9},{9,10},{10,11},{12,13},{... | collective-permute-start | bytes 253448 | tf_op jit(solution)/shard_map/ppermute | solution.py:33
  103.7 7.6 %shard_map.147 = f32[8,4,64,64]{3,2,1,0:T(8,128)} custom-call(bf16[10,64,512]{2,1,0:T(8,128)(2,1)} %pad.36.refs_0_, bf16[64,1728]{1,0:T(8,128)(2,1)} %reshape.153.refs_1_), custom_call_target="tpu_custom_call" | custom-call | tf_op jit(solution)/shard_map/pallas_call | solution.py:206
  114.5 27.8 %all_to_all.24 = bf16[256,2,64]{0,1,2:T(2,128)(2,1)S(1)} all-to-all(bf16[256,2,64]{0,1,2:T(2,128)(2,1)S(1)} %copy.167), channel_id=1, replica_groups=mesh['gx'=32,'gy'=2,'gz'=4] {'gx'}, dimensions={2} | all-to-all | bytes 131072 | tf_op jit(solution)/shard_map/all_to_all | solution.py:303
  146.2 4.1 %all-to-all-start.1 = ((bf16[256,128,2]{0,2,1:T(2,128)(2,1)}), bf16[256,128,2]{0,2,1:T(2,128)(2,1)S(1)}, u32[]{:S(2)}, u32[]{:S(2)}) async-start(bf16[256,128,2]{0,2,1:T(2,128)(2,1)} %bitcast.33), calls=%async_computation.1 | async-start | bytes 262144 | tf_op jit(solution)/shard_map/all_to_all | solution.py:315
  150.8 10.8 %all-to-all-done.1 = bf16[256,128,2]{0,2,1:T(2,128)(2,1)S(1)} async-done(((bf16[256,128,2]{0,2,1:T(2,128)(2,1)}), bf16[256,128,2]{0,2,1:T(2,128)(2,1)S(1)}, u32[]{:S(2)}, u32[]{:S(2)}) %all-to-all-start.1) | async-done | bytes 131104 | tf_op jit(solution)/shard_map/all_to_all | solution.py:315
  166.0 3.9 %collective-permute-start.11 = (bf16[64,8,4,1]{3,0,2,1:T(8,128)(2,1)S(1)}, bf16[64,8,4,1]{3,0,2,1:T(8,128)(2,1)S(1)}, u32[]{:S(2)}, u32[]{:S(2)}) collective-permute-start(bf16[64,8,4,1]{3,0,2,1:T(8,128)(2,1)S(1)} %slice_select_fusion.2), channel_id=1, source_target_pairs={{0,4},{4,0},{1,5},{5,1},{2,6},{6,2},{3,7},{7,3},{8,12},{12,8},{9,1... | collective-permute-start | bytes 12296 | tf_op jit(solution)/shard_map/ppermute | solution.py:27
  172.2 4.9 %collective-permute-start.12 = (bf16[64,8,1,66]{3,0,2,1:T(8,128)(2,1)S(1)}, bf16[64,8,1,66]{3,0,2,1:T(8,128)(2,1)S(1)}, u32[]{:S(2)}, u32[]{:S(2)}) collective-permute-start(bf16[64,8,1,66]{3,0,2,1:T(8,128)(2,1)S(1)} %get-tuple-element.5), channel_id=1, source_target_pairs={{0,1},{1,2},{2,3},{4,5},{5,6},{6,7},{8,9},{9,10},{10,11},{12,13},{... | collective-permute-start | bytes 202760 | tf_op jit(solution)/shard_map/ppermute | solution.py:33
  179.2 3.5 %collective-permute-done.13 = bf16[64,8,1,66]{3,0,2,1:T(8,128)(2,1)S(1)} collective-permute-done((bf16[64,8,1,66]{3,0,2,1:T(8,128)(2,1)S(1)}, bf16[64,8,1,66]{3,0,2,1:T(8,128)(2,1)S(1)}, u32[]{:S(2)}, u32[]{:S(2)}) %collective-permute-start.13) | collective-permute-done | bytes 67616 | tf_op jit(solution)/shard_map/ppermute | solution.py:34
  185.3 6.2 %shard_map.148 = f32[6,4,64,64]{3,2,1,0:T(8,128)} custom-call(bf16[8,64,512]{2,1,0:T(8,128)(2,1)} %pad.38.refs_0_, bf16[64,1728]{1,0:T(8,128)(2,1)} %reshape.167.refs_1_), custom_call_target="tpu_custom_call" | custom-call | tf_op jit(solution)/shard_map/pallas_call | solution.py:206
  193.1 6.4 %copy.184 = f32[6,2,16,4,2,64,2]{2,6,5,4,3,1,0:T(2,128)} copy(f32[6,2,16,4,2,64,2]{5,2,6,4,1,3,0:T(8,128)S(1)} %convolution_bitcast_fusion) | data formatting | bytes 1572864 | tf_op jit(solution)/shard_map/ixvs,ioabc->xaovbsc/transpose | solution.py:232
  199.5 4.4 %copy.185 = f32[12,16,8,128]{3,2,1,0:T(8,128)S(1)} copy(f32[12,16,8,128]{1,3,2,0:T(8,128)} %bitcast.164) | data formatting | bytes 1572864 | tf_op jit(solution)/shard_map/reshape | solution.py:234
  207.5 3.7 %collective-permute-done.15 = bf16[10,16,1,128]{3,2,1,0:T(2,128)(2,1)S(1)} collective-permute-done((bf16[10,16,1,128]{3,2,1,0:T(2,128)(2,1)S(1)}, bf16[10,16,1,128]{3,2,1,0:T(2,128)(2,1)S(1)}, u32[]{:S(2)}, u32[]{:S(2)}) %collective-permute-start.15) | collective-permute-done | bytes 40992 | tf_op jit(solution)/shard_map/ppermute | solution.py:126
  213.0 3.6 %collective-permute-start.16 = (bf16[10,16,16,1]{2,1,3,0:T(8,128)(2,1)S(1)}, bf16[10,16,16,1]{2,1,3,0:T(8,128)(2,1)S(1)}, u32[]{:S(2)}, u32[]{:S(2)}) collective-permute-start(bf16[10,16,16,1]{2,1,3,0:T(8,128)(2,1)S(1)} %copy.186), channel_id=1, source_target_pairs={{0,4},{4,0},{1,5},{5,1},{2,6},{6,2},{3,7},{7,3},{8,12},{12,8},{9,1... | collective-permute-start | bytes 15368 | tf_op jit(solution)/shard_map/ppermute | solution.py:122
  218.3 9.8 %shard_map.149 = f32[4,8,8,128]{3,2,1,0:T(8,128)} custom-call(bf16[10,256,128]{2,1,0:T(8,128)(2,1)} %bitcast.167, bf16[10,8,256]{2,1,0:T(8,128)(2,1)} %pad.39.refs_1_, bf16[27,16,16]{2,1,0:T(8,128)(2,1)} %bitcast.181, bf16[32,128]{1,0:T(8,128)(2,1)} %convert_element_type.137.refs_3_), custom_call_target="tpu_custom_call" | custom-call | tf_op jit(solution)/shard_map/pallas_call | solution.py:155
  (160 shorter events, 65.8 us)
Async XLA Ops:
  0.0 142.9 %copy-start = (bf16[256,256]{1,0:T(8,128)(2,1)S(1)}, bf16[256,256]{1,0:T(8,128)(2,1)}, u32[]{:S(2)}) copy-start(bf16[256,256]{1,0:T(8,128)(2,1)} %param.22) | copy-start | bytes 393220
  0.9 5.3 %collective-permute-start = (bf16[8,4,8,128]{3,2,1,0:T(8,128)(2,1)S(1)}, bf16[8,4,8,128]{3,2,1,0:T(8,128)(2,1)S(1)}, u32[]{:S(2)}, u32[]{:S(2)}) collective-permute-start(bf16[8,4,8,128]{3,2,1,0:T(8,128)(2,1)S(1)} %bitcast.175), channel_id=1, source_target_pairs={{0,8},{8,16},{16,24},{24,32},{32,40},{40,48},{48,56},{56,64},{64,7... | collective-permute-start | bytes 196616 | tf_op jit(solution)/shard_map/ppermute | solution.py:33
  4.8 5.0 %collective-permute-start.1 = (bf16[8,4,8,128]{3,2,1,0:T(8,128)(2,1)S(1)}, bf16[8,4,8,128]{3,2,1,0:T(8,128)(2,1)S(1)}, u32[]{:S(2)}, u32[]{:S(2)}) collective-permute-start(bf16[8,4,8,128]{3,2,1,0:T(8,128)(2,1)S(1)} %bitcast.176), channel_id=1, source_target_pairs={{8,0},{16,8},{24,16},{32,24},{40,32},{48,40},{56,48},{64,56},{72,6... | collective-permute-start | bytes 196616 | tf_op jit(solution)/shard_map/ppermute | solution.py:34
  10.1 5.7 %collective-permute-start.2 = (bf16[24,8,1,128]{3,2,1,0:T(2,128)(2,1)S(1)}, bf16[24,8,1,128]{3,2,1,0:T(2,128)(2,1)S(1)}, u32[]{:S(2)}, u32[]{:S(2)}) collective-permute-start(bf16[24,8,1,128]{3,2,1,0:T(2,128)(2,1)S(1)} %get-tuple-element.17), channel_id=1, source_target_pairs={{0,1},{1,2},{2,3},{4,5},{5,6},{6,7},{8,9},{9,10},{10,11},{12,13},{... | collective-permute-start | bytes 147464 | tf_op jit(solution)/shard_map/ppermute | solution.py:126
  13.6 5.5 %collective-permute-start.3 = (bf16[24,8,1,128]{3,2,1,0:T(2,128)(2,1)S(1)}, bf16[24,8,1,128]{3,2,1,0:T(2,128)(2,1)S(1)}, u32[]{:S(2)}, u32[]{:S(2)}) collective-permute-start(bf16[24,8,1,128]{3,2,1,0:T(2,128)(2,1)S(1)} %get-tuple-element.18), channel_id=1, source_target_pairs={{1,0},{2,1},{3,2},{5,4},{6,5},{7,6},{9,8},{10,9},{11,10},{13,12},{... | collective-permute-start | bytes 147464 | tf_op jit(solution)/shard_map/ppermute | solution.py:126
  22.6 4.3 %collective-permute-start.4 = (bf16[24,8,16,1]{0,2,3,1:T(8,128)(2,1)S(1)}, bf16[24,8,16,1]{0,2,3,1:T(8,128)(2,1)S(1)}, u32[]{:S(2)}, u32[]{:S(2)}) collective-permute-start(bf16[24,8,16,1]{0,2,3,1:T(8,128)(2,1)S(1)} %broadcast_select_fusion.11), channel_id=1, source_target_pairs={{0,4},{4,0},{1,5},{5,1},{2,6},{6,2},{3,7},{7,3},{8,12},{12,8},{9,1... | collective-permute-start | bytes 18440 | tf_op jit(solution)/shard_map/ppermute | solution.py:122
  43.0 7.1 %collective-permute-start.5 = (bf16[22,16,1,128]{3,2,1,0:T(2,128)(2,1)S(1)}, bf16[22,16,1,128]{3,2,1,0:T(2,128)(2,1)S(1)}, u32[]{:S(2)}, u32[]{:S(2)}) collective-permute-start(bf16[22,16,1,128]{3,2,1,0:T(2,128)(2,1)S(1)} %get-tuple-element.9), channel_id=1, source_target_pairs={{0,1},{1,2},{2,3},{4,5},{5,6},{6,7},{8,9},{9,10},{10,11},{12,13},{... | collective-permute-start | bytes 270344 | tf_op jit(solution)/shard_map/ppermute | solution.py:126
  46.6 9.2 %collective-permute-start.6 = (bf16[22,16,1,128]{3,2,1,0:T(2,128)(2,1)S(1)}, bf16[22,16,1,128]{3,2,1,0:T(2,128)(2,1)S(1)}, u32[]{:S(2)}, u32[]{:S(2)}) collective-permute-start(bf16[22,16,1,128]{3,2,1,0:T(2,128)(2,1)S(1)} %get-tuple-element.10), channel_id=1, source_target_pairs={{1,0},{2,1},{3,2},{5,4},{6,5},{7,6},{9,8},{10,9},{11,10},{13,12},{... | collective-permute-start | bytes 270344 | tf_op jit(solution)/shard_map/ppermute | solution.py:126
  60.0 2.3 %collective-permute-start.7 = (bf16[22,16,16,1]{0,2,3,1:T(8,128)(2,1)S(1)}, bf16[22,16,16,1]{0,2,3,1:T(8,128)(2,1)S(1)}, u32[]{:S(2)}, u32[]{:S(2)}) collective-permute-start(bf16[22,16,16,1]{0,2,3,1:T(8,128)(2,1)S(1)} %copy.157), channel_id=1, source_target_pairs={{0,4},{4,0},{1,5},{5,1},{2,6},{6,2},{3,7},{7,3},{8,12},{12,8},{9,1... | collective-permute-start | bytes 33800 | tf_op jit(solution)/shard_map/ppermute | solution.py:122
  88.7 3.6 %collective-permute-start.8 = (bf16[64,10,4,1]{0,3,2,1:T(2,128)(2,1)S(1)}, bf16[64,10,4,1]{0,3,2,1:T(2,128)(2,1)S(1)}, u32[]{:S(2)}, u32[]{:S(2)}) collective-permute-start(bf16[64,10,4,1]{0,3,2,1:T(2,128)(2,1)S(1)} %broadcast_select_fusion.8), channel_id=1, source_target_pairs={{0,4},{4,0},{1,5},{5,1},{2,6},{6,2},{3,7},{7,3},{8,12},{12,8},{9,1... | collective-permute-start | bytes 15368 | tf_op jit(solution)/shard_map/ppermute | solution.py:27
  92.5 8.0 %collective-permute-start.10 = (bf16[64,10,1,66]{0,3,2,1:T(8,128)(2,1)S(1)}, bf16[64,10,1,66]{0,3,2,1:T(8,128)(2,1)S(1)}, u32[]{:S(2)}, u32[]{:S(2)}) collective-permute-start(bf16[64,10,1,66]{0,3,2,1:T(8,128)(2,1)S(1)} %get-tuple-element.12), channel_id=1, source_target_pairs={{1,0},{2,1},{3,2},{5,4},{6,5},{7,6},{9,8},{10,9},{11,10},{13,12},{... | collective-permute-start | bytes 253448 | tf_op jit(solution)/shard_map/ppermute | solution.py:34
  93.8 7.6 %collective-permute-start.9 = (bf16[64,10,1,66]{0,3,2,1:T(8,128)(2,1)S(1)}, bf16[64,10,1,66]{0,3,2,1:T(8,128)(2,1)S(1)}, u32[]{:S(2)}, u32[]{:S(2)}) collective-permute-start(bf16[64,10,1,66]{0,3,2,1:T(8,128)(2,1)S(1)} %get-tuple-element.11), channel_id=1, source_target_pairs={{0,1},{1,2},{2,3},{4,5},{5,6},{6,7},{8,9},{9,10},{10,11},{12,13},{... | collective-permute-start | bytes 253448 | tf_op jit(solution)/shard_map/ppermute | solution.py:33
  114.3 28.9 %copy-start.11 = (bf16[256,256]{1,0:T(8,128)(2,1)S(1)}, bf16[256,256]{1,0:T(8,128)(2,1)}, u32[]{:S(2)}) copy-start(bf16[256,256]{1,0:T(8,128)(2,1)} %param.21) | copy-start | bytes 393220
  114.5 29.5 %copy-start.12 = (bf16[256,256]{1,0:T(8,128)(2,1)S(1)}, bf16[256,256]{1,0:T(8,128)(2,1)}, u32[]{:S(2)}) copy-start(bf16[256,256]{1,0:T(8,128)(2,1)} %param.23) | copy-start | bytes 393220
  144.3 5.9 %copy-start.7 = (bf16[8,16384]{1,0:T(8,128)(2,1)S(1)}, bf16[8,16384]{1,0:T(8,128)(2,1)}, u32[]{:S(2)}) copy-start(bf16[8,16384]{1,0:T(8,128)(2,1)} %param.25) | copy-start | bytes 786436
  146.2 15.5 %all-to-all-start.1 = ((bf16[256,128,2]{0,2,1:T(2,128)(2,1)}), bf16[256,128,2]{0,2,1:T(2,128)(2,1)S(1)}, u32[]{:S(2)}, u32[]{:S(2)}) async-start(bf16[256,128,2]{0,2,1:T(2,128)(2,1)} %bitcast.33), calls=%async_computation.1 | async-start | bytes 262144 | tf_op jit(solution)/shard_map/all_to_all | solution.py:315
  166.0 5.8 %collective-permute-start.11 = (bf16[64,8,4,1]{3,0,2,1:T(8,128)(2,1)S(1)}, bf16[64,8,4,1]{3,0,2,1:T(8,128)(2,1)S(1)}, u32[]{:S(2)}, u32[]{:S(2)}) collective-permute-start(bf16[64,8,4,1]{3,0,2,1:T(8,128)(2,1)S(1)} %slice_select_fusion.2), channel_id=1, source_target_pairs={{0,4},{4,0},{1,5},{5,1},{2,6},{6,2},{3,7},{7,3},{8,12},{12,8},{9,1... | collective-permute-start | bytes 12296 | tf_op jit(solution)/shard_map/ppermute | solution.py:27
  172.2 7.1 %collective-permute-start.12 = (bf16[64,8,1,66]{3,0,2,1:T(8,128)(2,1)S(1)}, bf16[64,8,1,66]{3,0,2,1:T(8,128)(2,1)S(1)}, u32[]{:S(2)}, u32[]{:S(2)}) collective-permute-start(bf16[64,8,1,66]{3,0,2,1:T(8,128)(2,1)S(1)} %get-tuple-element.5), channel_id=1, source_target_pairs={{0,1},{1,2},{2,3},{4,5},{5,6},{6,7},{8,9},{9,10},{10,11},{12,13},{... | collective-permute-start | bytes 202760 | tf_op jit(solution)/shard_map/ppermute | solution.py:33
  177.1 5.7 %collective-permute-start.13 = (bf16[64,8,1,66]{3,0,2,1:T(8,128)(2,1)S(1)}, bf16[64,8,1,66]{3,0,2,1:T(8,128)(2,1)S(1)}, u32[]{:S(2)}, u32[]{:S(2)}) collective-permute-start(bf16[64,8,1,66]{3,0,2,1:T(8,128)(2,1)S(1)} %get-tuple-element.6), channel_id=1, source_target_pairs={{1,0},{2,1},{3,2},{5,4},{6,5},{7,6},{9,8},{10,9},{11,10},{13,12},{... | collective-permute-start | bytes 202760 | tf_op jit(solution)/shard_map/ppermute | solution.py:34
  184.5 7.1 %copy-start.13 = (bf16[64,16,2,2,2]{0,4,3,2,1:T(2,128)(2,1)S(1)}, bf16[64,16,2,2,2]{0,4,3,2,1:T(2,128)(2,1)}, u32[]{:S(2)}) copy-start(bf16[64,16,2,2,2]{0,4,3,2,1:T(2,128)(2,1)} %param.27) | copy-start | bytes 49156
  204.1 3.4 %collective-permute-start.14 = (bf16[10,16,1,128]{3,2,1,0:T(2,128)(2,1)S(1)}, bf16[10,16,1,128]{3,2,1,0:T(2,128)(2,1)S(1)}, u32[]{:S(2)}, u32[]{:S(2)}) collective-permute-start(bf16[10,16,1,128]{3,2,1,0:T(2,128)(2,1)S(1)} %get-tuple-element.15), channel_id=1, source_target_pairs={{0,1},{1,2},{2,3},{4,5},{5,6},{6,7},{8,9},{9,10},{10,11},{12,13},{... | collective-permute-start | bytes 122888 | tf_op jit(solution)/shard_map/ppermute | solution.py:126
  206.0 5.2 %collective-permute-start.15 = (bf16[10,16,1,128]{3,2,1,0:T(2,128)(2,1)S(1)}, bf16[10,16,1,128]{3,2,1,0:T(2,128)(2,1)S(1)}, u32[]{:S(2)}, u32[]{:S(2)}) collective-permute-start(bf16[10,16,1,128]{3,2,1,0:T(2,128)(2,1)S(1)} %get-tuple-element.16), channel_id=1, source_target_pairs={{1,0},{2,1},{3,2},{5,4},{6,5},{7,6},{9,8},{10,9},{11,10},{13,12},{... | collective-permute-start | bytes 122888 | tf_op jit(solution)/shard_map/ppermute | solution.py:126
  211.7 5.8 %copy-start.3 = (bf16[10,16,16,128]{3,2,1,0:T(8,128)(2,1)}, bf16[10,16,16,128]{3,2,1,0:T(8,128)(2,1)S(1)}, u32[]{:S(2)}) copy-start(bf16[10,16,16,128]{3,2,1,0:T(8,128)(2,1)S(1)} %maximum_maximum_fusion.2) | copy-start | bytes 1966084
  213.0 4.5 %collective-permute-start.16 = (bf16[10,16,16,1]{2,1,3,0:T(8,128)(2,1)S(1)}, bf16[10,16,16,1]{2,1,3,0:T(8,128)(2,1)S(1)}, u32[]{:S(2)}, u32[]{:S(2)}) collective-permute-start(bf16[10,16,16,1]{2,1,3,0:T(8,128)(2,1)S(1)} %copy.186), channel_id=1, source_target_pairs={{0,4},{4,0},{1,5},{5,1},{2,6},{6,2},{3,7},{7,3},{8,12},{12,8},{9,1... | collective-permute-start | bytes 15368 | tf_op jit(solution)/shard_map/ppermute | solution.py:122
  (10 other events, 24.8 us)

commit v5 on v4

--- a/solution.py
+++ b/solution.py
@@ -99,18 +99,27 @@
 
     lax.fori_loop(0, sx + 2, shift, 0)
 
-    def row(x, carry):
-        stack = shifted_ref[pl.ds(x, 3)].reshape(9 * depth, ss)
+    def rows_pair(g, carry):
+        x = 2 * g
+        stack = jnp.concatenate(
+            [
+                shifted_ref[pl.ds(x, 3)].reshape(9 * depth, ss),
+                shifted_ref[pl.ds(x + 1, 3)].reshape(9 * depth, ss),
+            ],
+            axis=1,
+        )
         acc = jnp.dot(band_ref[...], stack, preferred_element_type=jnp.float32)
         act = (acc * jax.nn.sigmoid(acc)).astype(jnp.bfloat16)
-        if head:
-            res = jnp.dot(h_ref[...], act, preferred_element_type=jnp.float32)
-            o_ref[:, x] = res.reshape(res.shape[0] // sv, sv, ss)
-        else:
-            o_ref[x] = act.astype(jnp.float32).reshape(cout, sv, ss)
+        for k in range(2):
+            part = act[:, k * ss : (k + 1) * ss]
+            if head:
+                res = jnp.dot(h_ref[...], part, preferred_element_type=jnp.float32)
+                o_ref[:, x + k] = res.reshape(res.shape[0] // sv, sv, ss)
+            else:
+                o_ref[x + k] = part.astype(jnp.float32).reshape(cout, sv, ss)
         return carry
 
-    lax.fori_loop(0, sx, row, 0)
+    lax.fori_loop(0, sx // 2, rows_pair, 0)
 
 
 def faces(block, axis, dim):
@@ -178,16 +187,25 @@
     lax.fori_loop(0, sx + 2, shift, 0)
     chans = shifted_ref.shape[2]
 
-    def row(x, carry):
-        stack = shifted_ref[pl.ds(x, 3)].reshape(27 * chans, span)
+    def rows_pair(g, carry):
+        x = 2 * g
+        stack = jnp.concatenate(
+            [
+                shifted_ref[pl.ds(x, 3)].reshape(27 * chans, span),
+                shifted_ref[pl.ds(x + 1, 3)].reshape(27 * chans, span),
+            ],
+            axis=1,
+        )
         acc = jnp.dot(w_ref[...], stack, preferred_element_type=jnp.float32)
         act = (acc * jax.nn.sigmoid(acc)).astype(jnp.bfloat16).astype(jnp.float32)
-        for v in range(sv):
-            piece = act if v == 0 else pltpu.roll(act, span - v * pitch, 1)
-            o_ref[x, v] = piece[:, :ss]
+        for k in range(2):
+            part = act[:, k * span : (k + 1) * span]
+            for v in range(sv):
+                piece = part if v == 0 else pltpu.roll(part, span - v * pitch, 1)
+                o_ref[x + k, v] = piece[:, :ss]
         return carry
 
-    lax.fori_loop(0, sx, row, 0)
+    lax.fori_loop(0, sx // 2, rows_pair, 0)
 
 
 def mid_conv(field, weight, sides=MID_SIDES):

time: 229 us -> 221 us (0.965)
  Pallas kernels: 53 us -> 44.7 us
    pallas_call x3, Pallas kernels: 39.1 us -> 32.1 us  [fine_conv(): pl.pallas_call(kernel, out_shape=out_shape, scratch_shapes=[pltpu.VMEM((c...]
where the time goes in v5:
time: 221 us; the launch traced here: 220 us
  starting transfers between devices  46.5 us (21%)
  Pallas kernels  44.7 us (20%)
  local copies, waits for them, and re-layouts  43.1 us (20%)
  waiting for transfers between devices  38.6 us (17%)
  blocking collectives  27.8 us (13%)
  other arithmetic  9.91 us (4%)
  matrix products  8.21 us (4%)
    pallas_call x3, Pallas kernels, fine_conv(): pl.pallas_call(kernel, out_shape=out_shape, scratch_shapes=[pltpu.VMEM((c...  32.1 us
    all_to_all x1, blocking collectives, on_device(): rows = lax.all_to_all(flat, 'gx', split_axis=2, concat_axis=1, tiled=True)  27.8 us
    ppermute x3, starting transfers between devices, extended(): low = lax.ppermute(top, axis, forward)  12.8 us
    ppermute x3, waiting for transfers between devices, faces(): lax.ppermute(bottom, axis, backward)  12.8 us
    pallas_call x2, Pallas kernels, mid_conv(): pl.pallas_call(kernel, out_shape=jax.ShapeDtypeStruct((sx, sv, cout, ss),...  12.5 us
    all_to_all x1, waiting for transfers between devices, on_device(): lax.all_to_all(windows, 'gx', split_axis=1, concat_axis=2, tiled=True)  10.8 us
    ppermute x3, waiting for transfers between devices, extended(): high = lax.ppermute(bottom, axis, backward)  9.9 us
    ppermute x3, starting transfers between devices, faces(): lax.ppermute(top, axis, forward)  9.33 us
  transfers between devices with their start and end apart: 18, of which 13 were waited for; matrix products, arithmetic and copies ran while one was open for 4% of the time, Pallas kernels for 0%

profile of v5, /device:TPU:1, one launch (start us, length us, event | category | flops | bytes accessed | tf_op | source)
XLA Modules:
  0.0 219.7 jit_solution(15590029841135179388)
XLA Ops:
  0.9 3.9 %collective-permute-start = (bf16[8,4,8,128]{3,2,1,0:T(8,128)(2,1)S(1)}, bf16[8,4,8,128]{3,2,1,0:T(8,128)(2,1)S(1)}, u32[]{:S(2)}, u32[]{:S(2)}) collective-permute-start(bf16[8,4,8,128]{3,2,1,0:T(8,128)(2,1)S(1)} %bitcast.175), channel_id=1, source_target_pairs={{0,8},{8,16},{16,24},{24,32},{32,40},{40,48},{48,56},{56,64},{64,7... | collective-permute-start | bytes 196616 | tf_op jit(solution)/shard_map/ppermute | solution.py:33
  6.2 3.7 %collective-permute-done.1 = bf16[8,4,8,128]{3,2,1,0:T(8,128)(2,1)S(1)} collective-permute-done((bf16[8,4,8,128]{3,2,1,0:T(8,128)(2,1)S(1)}, bf16[8,4,8,128]{3,2,1,0:T(8,128)(2,1)S(1)}, u32[]{:S(2)}, u32[]{:S(2)}) %collective-permute-start.1) | collective-permute-done | bytes 65568 | tf_op jit(solution)/shard_map/ppermute | solution.py:34
  10.1 3.5 %collective-permute-start.2 = (bf16[24,8,1,128]{3,2,1,0:T(2,128)(2,1)S(1)}, bf16[24,8,1,128]{3,2,1,0:T(2,128)(2,1)S(1)}, u32[]{:S(2)}, u32[]{:S(2)}) collective-permute-start(bf16[24,8,1,128]{3,2,1,0:T(2,128)(2,1)S(1)} %get-tuple-element.17), channel_id=1, source_target_pairs={{0,1},{1,2},{2,3},{4,5},{5,6},{6,7},{8,9},{9,10},{10,11},{12,13},{... | collective-permute-start | bytes 147464 | tf_op jit(solution)/shard_map/ppermute | solution.py:135
  15.8 3.4 %collective-permute-done.3 = bf16[24,8,1,128]{3,2,1,0:T(2,128)(2,1)S(1)} collective-permute-done((bf16[24,8,1,128]{3,2,1,0:T(2,128)(2,1)S(1)}, bf16[24,8,1,128]{3,2,1,0:T(2,128)(2,1)S(1)}, u32[]{:S(2)}, u32[]{:S(2)}) %collective-permute-start.3) | collective-permute-done | bytes 49184 | tf_op jit(solution)/shard_map/ppermute | solution.py:135
  22.6 3.4 %collective-permute-start.4 = (bf16[24,8,16,1]{0,2,3,1:T(8,128)(2,1)S(1)}, bf16[24,8,16,1]{0,2,3,1:T(8,128)(2,1)S(1)}, u32[]{:S(2)}, u32[]{:S(2)}) collective-permute-start(bf16[24,8,16,1]{0,2,3,1:T(8,128)(2,1)S(1)} %broadcast_select_fusion.11), channel_id=1, source_target_pairs={{0,4},{4,0},{1,5},{5,1},{2,6},{6,2},{3,7},{7,3},{8,12},{12,8},{9,1... | collective-permute-start | bytes 18440 | tf_op jit(solution)/shard_map/ppermute | solution.py:131
  27.9 11.0 %shard_map.145 = f32[22,16,8,128]{3,2,1,0:T(8,128)} custom-call(bf16[24,128,128]{2,1,0:T(8,128)(2,1)} %bitcast.166, bf16[24,8,128]{2,1,0:T(8,128)(2,1)} %pad.33.refs_1_, bf16[27,16,8]{2,1,0:T(8,128)(2,1)} %bitcast.174), custom_call_target="tpu_custom_call" | custom-call | tf_op jit(solution)/shard_map/pallas_call | solution.py:164
  40.7 3.5 %collective-permute-start.5 = (bf16[22,16,1,128]{3,2,1,0:T(2,128)(2,1)S(1)}, bf16[22,16,1,128]{3,2,1,0:T(2,128)(2,1)S(1)}, u32[]{:S(2)}, u32[]{:S(2)}) collective-permute-start(bf16[22,16,1,128]{3,2,1,0:T(2,128)(2,1)S(1)} %get-tuple-element.9), channel_id=1, source_target_pairs={{0,1},{1,2},{2,3},{4,5},{5,6},{6,7},{8,9},{9,10},{10,11},{12,13},{... | collective-permute-start | bytes 270344 | tf_op jit(solution)/shard_map/ppermute | solution.py:135
  47.8 5.7 %collective-permute-done.6 = bf16[22,16,1,128]{3,2,1,0:T(2,128)(2,1)S(1)} collective-permute-done((bf16[22,16,1,128]{3,2,1,0:T(2,128)(2,1)S(1)}, bf16[22,16,1,128]{3,2,1,0:T(2,128)(2,1)S(1)}, u32[]{:S(2)}, u32[]{:S(2)}) %collective-permute-start.6) | collective-permute-done | bytes 90144 | tf_op jit(solution)/shard_map/ppermute | solution.py:135
  61.3 13.0 %shard_map.146 = f32[20,16,8,128]{3,2,1,0:T(8,128)} custom-call(bf16[22,256,128]{2,1,0:T(8,128)(2,1)} %bitcast.165, bf16[22,8,256]{2,1,0:T(8,128)(2,1)} %pad.35.refs_1_, bf16[27,16,16]{2,1,0:T(8,128)(2,1)} %bitcast.180), custom_call_target="tpu_custom_call" | custom-call | tf_op jit(solution)/shard_map/pallas_call | solution.py:164
  75.9 3.5 %copy.161 = bf16[20,16,8,128]{1,3,2,0:T(8,128)(2,1)} copy(bf16[20,16,8,128]{3,2,1,0:T(8,128)(2,1)S(1)} %convert_select_fusion.1) | data formatting | bytes 1310720 | tf_op jit(solution)/shard_map/jit(_where)/select_n | solution.py:46
  79.4 3.8 %multiply_convert_fusion = bf16[64,10,4,64]{0,3,2,1:T(8,128)(2,1)S(1)} fusion(bf16[10,2,16,4,2,64,2]{2,6,5,4,3,1,0:T(2,128)(2,1)} %bitcast.168, bf16[64,16,2,2,2,1,1]{0,4,3,2,1,6,5:T(2,128)(2,1)S(1)} %bitcast.183), kind=kOutput, calls=%fused_computation.8 | convolution fusion | flops 42762240 | bytes 999424 | tf_op jit(solution)/shard_map/xaivbsc,oiabc->oxvs/dot_general | solution.py:246
  88.4 4.0 %collective-permute-start.9 = (bf16[64,10,1,66]{0,3,2,1:T(8,128)(2,1)S(1)}, bf16[64,10,1,66]{0,3,2,1:T(8,128)(2,1)S(1)}, u32[]{:S(2)}, u32[]{:S(2)}) collective-permute-start(bf16[64,10,1,66]{0,3,2,1:T(8,128)(2,1)S(1)} %get-tuple-element.11), channel_id=1, source_target_pairs={{0,1},{1,2},{2,3},{4,5},{5,6},{6,7},{8,9},{9,10},{10,11},{12,13},{... | collective-permute-start | bytes 253448 | tf_op jit(solution)/shard_map/ppermute | solution.py:33
  98.3 6.9 %shard_map.147 = f32[8,4,64,64]{3,2,1,0:T(8,128)} custom-call(bf16[10,64,512]{2,1,0:T(8,128)(2,1)} %pad.36.refs_0_, bf16[64,1728]{1,0:T(8,128)(2,1)} %reshape.153.refs_1_), custom_call_target="tpu_custom_call" | custom-call | tf_op jit(solution)/shard_map/pallas_call | solution.py:224
  108.3 27.8 %all_to_all.24 = bf16[256,2,64]{0,1,2:T(2,128)(2,1)S(1)} all-to-all(bf16[256,2,64]{0,1,2:T(2,128)(2,1)S(1)} %copy.167), channel_id=1, replica_groups=mesh['gx'=32,'gy'=2,'gz'=4] {'gx'}, dimensions={2} | all-to-all | bytes 131072 | tf_op jit(solution)/shard_map/all_to_all | solution.py:321
  139.9 4.1 %all-to-all-start.1 = ((bf16[256,128,2]{0,2,1:T(2,128)(2,1)}), bf16[256,128,2]{0,2,1:T(2,128)(2,1)S(1)}, u32[]{:S(2)}, u32[]{:S(2)}) async-start(bf16[256,128,2]{0,2,1:T(2,128)(2,1)} %bitcast.33), calls=%async_computation.1 | async-start | bytes 262144 | tf_op jit(solution)/shard_map/all_to_all | solution.py:333
  144.6 10.8 %all-to-all-done.1 = bf16[256,128,2]{0,2,1:T(2,128)(2,1)S(1)} async-done(((bf16[256,128,2]{0,2,1:T(2,128)(2,1)}), bf16[256,128,2]{0,2,1:T(2,128)(2,1)S(1)}, u32[]{:S(2)}, u32[]{:S(2)}) %all-to-all-start.1) | async-done | bytes 131104 | tf_op jit(solution)/shard_map/all_to_all | solution.py:333
  159.8 3.9 %collective-permute-start.11 = (bf16[64,8,4,1]{3,0,2,1:T(8,128)(2,1)S(1)}, bf16[64,8,4,1]{3,0,2,1:T(8,128)(2,1)S(1)}, u32[]{:S(2)}, u32[]{:S(2)}) collective-permute-start(bf16[64,8,4,1]{3,0,2,1:T(8,128)(2,1)S(1)} %slice_select_fusion.2), channel_id=1, source_target_pairs={{0,4},{4,0},{1,5},{5,1},{2,6},{6,2},{3,7},{7,3},{8,12},{12,8},{9,1... | collective-permute-start | bytes 12296 | tf_op jit(solution)/shard_map/ppermute | solution.py:27
  166.0 4.9 %collective-permute-start.12 = (bf16[64,8,1,66]{3,0,2,1:T(8,128)(2,1)S(1)}, bf16[64,8,1,66]{3,0,2,1:T(8,128)(2,1)S(1)}, u32[]{:S(2)}, u32[]{:S(2)}) collective-permute-start(bf16[64,8,1,66]{3,0,2,1:T(8,128)(2,1)S(1)} %get-tuple-element.5), channel_id=1, source_target_pairs={{0,1},{1,2},{2,3},{4,5},{5,6},{6,7},{8,9},{9,10},{10,11},{12,13},{... | collective-permute-start | bytes 202760 | tf_op jit(solution)/shard_map/ppermute | solution.py:33
  173.1 3.5 %collective-permute-done.13 = bf16[64,8,1,66]{3,0,2,1:T(8,128)(2,1)S(1)} collective-permute-done((bf16[64,8,1,66]{3,0,2,1:T(8,128)(2,1)S(1)}, bf16[64,8,1,66]{3,0,2,1:T(8,128)(2,1)S(1)}, u32[]{:S(2)}, u32[]{:S(2)}) %collective-permute-start.13) | collective-permute-done | bytes 67616 | tf_op jit(solution)/shard_map/ppermute | solution.py:34
  179.2 5.7 %shard_map.148 = f32[6,4,64,64]{3,2,1,0:T(8,128)} custom-call(bf16[8,64,512]{2,1,0:T(8,128)(2,1)} %pad.38.refs_0_, bf16[64,1728]{1,0:T(8,128)(2,1)} %reshape.167.refs_1_), custom_call_target="tpu_custom_call" | custom-call | tf_op jit(solution)/shard_map/pallas_call | solution.py:224
  186.4 6.4 %copy.184 = f32[6,2,16,4,2,64,2]{2,6,5,4,3,1,0:T(2,128)} copy(f32[6,2,16,4,2,64,2]{5,2,6,4,1,3,0:T(8,128)S(1)} %convolution_bitcast_fusion) | data formatting | bytes 1572864 | tf_op jit(solution)/shard_map/ixvs,ioabc->xaovbsc/transpose | solution.py:250
  192.8 4.4 %copy.185 = f32[12,16,8,128]{3,2,1,0:T(8,128)S(1)} copy(f32[12,16,8,128]{1,3,2,0:T(8,128)} %bitcast.164) | data formatting | bytes 1572864 | tf_op jit(solution)/shard_map/reshape | solution.py:252
  201.1 3.7 %collective-permute-done.15 = bf16[10,16,1,128]{3,2,1,0:T(2,128)(2,1)S(1)} collective-permute-done((bf16[10,16,1,128]{3,2,1,0:T(2,128)(2,1)S(1)}, bf16[10,16,1,128]{3,2,1,0:T(2,128)(2,1)S(1)}, u32[]{:S(2)}, u32[]{:S(2)}) %collective-permute-start.15) | collective-permute-done | bytes 40992 | tf_op jit(solution)/shard_map/ppermute | solution.py:135
  211.5 8.2 %shard_map.149 = f32[4,8,8,128]{3,2,1,0:T(8,128)} custom-call(bf16[10,256,128]{2,1,0:T(8,128)(2,1)} %bitcast.167, bf16[10,8,256]{2,1,0:T(8,128)(2,1)} %pad.39.refs_1_, bf16[27,16,16]{2,1,0:T(8,128)(2,1)} %bitcast.181, bf16[32,128]{1,0:T(8,128)(2,1)} %convert_element_type.137.refs_3_), custom_call_target="tpu_custom_call" | custom-call | tf_op jit(solution)/shard_map/pallas_call | solution.py:164
  (160 shorter events, 66.0 us)
Async XLA Ops:
  0.0 136.7 %copy-start = (bf16[256,256]{1,0:T(8,128)(2,1)S(1)}, bf16[256,256]{1,0:T(8,128)(2,1)}, u32[]{:S(2)}) copy-start(bf16[256,256]{1,0:T(8,128)(2,1)} %param.22) | copy-start | bytes 393220
  0.9 5.3 %collective-permute-start = (bf16[8,4,8,128]{3,2,1,0:T(8,128)(2,1)S(1)}, bf16[8,4,8,128]{3,2,1,0:T(8,128)(2,1)S(1)}, u32[]{:S(2)}, u32[]{:S(2)}) collective-permute-start(bf16[8,4,8,128]{3,2,1,0:T(8,128)(2,1)S(1)} %bitcast.175), channel_id=1, source_target_pairs={{0,8},{8,16},{16,24},{24,32},{32,40},{40,48},{48,56},{56,64},{64,7... | collective-permute-start | bytes 196616 | tf_op jit(solution)/shard_map/ppermute | solution.py:33
  4.8 5.0 %collective-permute-start.1 = (bf16[8,4,8,128]{3,2,1,0:T(8,128)(2,1)S(1)}, bf16[8,4,8,128]{3,2,1,0:T(8,128)(2,1)S(1)}, u32[]{:S(2)}, u32[]{:S(2)}) collective-permute-start(bf16[8,4,8,128]{3,2,1,0:T(8,128)(2,1)S(1)} %bitcast.176), channel_id=1, source_target_pairs={{8,0},{16,8},{24,16},{32,24},{40,32},{48,40},{56,48},{64,56},{72,6... | collective-permute-start | bytes 196616 | tf_op jit(solution)/shard_map/ppermute | solution.py:34
  10.1 5.7 %collective-permute-start.2 = (bf16[24,8,1,128]{3,2,1,0:T(2,128)(2,1)S(1)}, bf16[24,8,1,128]{3,2,1,0:T(2,128)(2,1)S(1)}, u32[]{:S(2)}, u32[]{:S(2)}) collective-permute-start(bf16[24,8,1,128]{3,2,1,0:T(2,128)(2,1)S(1)} %get-tuple-element.17), channel_id=1, source_target_pairs={{0,1},{1,2},{2,3},{4,5},{5,6},{6,7},{8,9},{9,10},{10,11},{12,13},{... | collective-permute-start | bytes 147464 | tf_op jit(solution)/shard_map/ppermute | solution.py:135
  13.6 5.5 %collective-permute-start.3 = (bf16[24,8,1,128]{3,2,1,0:T(2,128)(2,1)S(1)}, bf16[24,8,1,128]{3,2,1,0:T(2,128)(2,1)S(1)}, u32[]{:S(2)}, u32[]{:S(2)}) collective-permute-start(bf16[24,8,1,128]{3,2,1,0:T(2,128)(2,1)S(1)} %get-tuple-element.18), channel_id=1, source_target_pairs={{1,0},{2,1},{3,2},{5,4},{6,5},{7,6},{9,8},{10,9},{11,10},{13,12},{... | collective-permute-start | bytes 147464 | tf_op jit(solution)/shard_map/ppermute | solution.py:135
  22.6 4.3 %collective-permute-start.4 = (bf16[24,8,16,1]{0,2,3,1:T(8,128)(2,1)S(1)}, bf16[24,8,16,1]{0,2,3,1:T(8,128)(2,1)S(1)}, u32[]{:S(2)}, u32[]{:S(2)}) collective-permute-start(bf16[24,8,16,1]{0,2,3,1:T(8,128)(2,1)S(1)} %broadcast_select_fusion.11), channel_id=1, source_target_pairs={{0,4},{4,0},{1,5},{5,1},{2,6},{6,2},{3,7},{7,3},{8,12},{12,8},{9,1... | collective-permute-start | bytes 18440 | tf_op jit(solution)/shard_map/ppermute | solution.py:131
  40.7 7.1 %collective-permute-start.5 = (bf16[22,16,1,128]{3,2,1,0:T(2,128)(2,1)S(1)}, bf16[22,16,1,128]{3,2,1,0:T(2,128)(2,1)S(1)}, u32[]{:S(2)}, u32[]{:S(2)}) collective-permute-start(bf16[22,16,1,128]{3,2,1,0:T(2,128)(2,1)S(1)} %get-tuple-element.9), channel_id=1, source_target_pairs={{0,1},{1,2},{2,3},{4,5},{5,6},{6,7},{8,9},{9,10},{10,11},{12,13},{... | collective-permute-start | bytes 270344 | tf_op jit(solution)/shard_map/ppermute | solution.py:135
  44.2 9.2 %collective-permute-start.6 = (bf16[22,16,1,128]{3,2,1,0:T(2,128)(2,1)S(1)}, bf16[22,16,1,128]{3,2,1,0:T(2,128)(2,1)S(1)}, u32[]{:S(2)}, u32[]{:S(2)}) collective-permute-start(bf16[22,16,1,128]{3,2,1,0:T(2,128)(2,1)S(1)} %get-tuple-element.10), channel_id=1, source_target_pairs={{1,0},{2,1},{3,2},{5,4},{6,5},{7,6},{9,8},{10,9},{11,10},{13,12},{... | collective-permute-start | bytes 270344 | tf_op jit(solution)/shard_map/ppermute | solution.py:135
  57.7 2.3 %collective-permute-start.7 = (bf16[22,16,16,1]{0,2,3,1:T(8,128)(2,1)S(1)}, bf16[22,16,16,1]{0,2,3,1:T(8,128)(2,1)S(1)}, u32[]{:S(2)}, u32[]{:S(2)}) collective-permute-start(bf16[22,16,16,1]{0,2,3,1:T(8,128)(2,1)S(1)} %copy.157), channel_id=1, source_target_pairs={{0,4},{4,0},{1,5},{5,1},{2,6},{6,2},{3,7},{7,3},{8,12},{12,8},{9,1... | collective-permute-start | bytes 33800 | tf_op jit(solution)/shard_map/ppermute | solution.py:131
  83.3 3.6 %collective-permute-start.8 = (bf16[64,10,4,1]{0,3,2,1:T(2,128)(2,1)S(1)}, bf16[64,10,4,1]{0,3,2,1:T(2,128)(2,1)S(1)}, u32[]{:S(2)}, u32[]{:S(2)}) collective-permute-start(bf16[64,10,4,1]{0,3,2,1:T(2,128)(2,1)S(1)} %broadcast_select_fusion.8), channel_id=1, source_target_pairs={{0,4},{4,0},{1,5},{5,1},{2,6},{6,2},{3,7},{7,3},{8,12},{12,8},{9,1... | collective-permute-start | bytes 15368 | tf_op jit(solution)/shard_map/ppermute | solution.py:27
  87.1 8.0 %collective-permute-start.10 = (bf16[64,10,1,66]{0,3,2,1:T(8,128)(2,1)S(1)}, bf16[64,10,1,66]{0,3,2,1:T(8,128)(2,1)S(1)}, u32[]{:S(2)}, u32[]{:S(2)}) collective-permute-start(bf16[64,10,1,66]{0,3,2,1:T(8,128)(2,1)S(1)} %get-tuple-element.12), channel_id=1, source_target_pairs={{1,0},{2,1},{3,2},{5,4},{6,5},{7,6},{9,8},{10,9},{11,10},{13,12},{... | collective-permute-start | bytes 253448 | tf_op jit(solution)/shard_map/ppermute | solution.py:34
  88.4 7.6 %collective-permute-start.9 = (bf16[64,10,1,66]{0,3,2,1:T(8,128)(2,1)S(1)}, bf16[64,10,1,66]{0,3,2,1:T(8,128)(2,1)S(1)}, u32[]{:S(2)}, u32[]{:S(2)}) collective-permute-start(bf16[64,10,1,66]{0,3,2,1:T(8,128)(2,1)S(1)} %get-tuple-element.11), channel_id=1, source_target_pairs={{0,1},{1,2},{2,3},{4,5},{5,6},{6,7},{8,9},{9,10},{10,11},{12,13},{... | collective-permute-start | bytes 253448 | tf_op jit(solution)/shard_map/ppermute | solution.py:33
  108.1 28.9 %copy-start.11 = (bf16[256,256]{1,0:T(8,128)(2,1)S(1)}, bf16[256,256]{1,0:T(8,128)(2,1)}, u32[]{:S(2)}) copy-start(bf16[256,256]{1,0:T(8,128)(2,1)} %param.21) | copy-start | bytes 393220
  108.3 29.5 %copy-start.12 = (bf16[256,256]{1,0:T(8,128)(2,1)S(1)}, bf16[256,256]{1,0:T(8,128)(2,1)}, u32[]{:S(2)}) copy-start(bf16[256,256]{1,0:T(8,128)(2,1)} %param.23) | copy-start | bytes 393220
  138.1 5.9 %copy-start.7 = (bf16[8,16384]{1,0:T(8,128)(2,1)S(1)}, bf16[8,16384]{1,0:T(8,128)(2,1)}, u32[]{:S(2)}) copy-start(bf16[8,16384]{1,0:T(8,128)(2,1)} %param.25) | copy-start | bytes 786436
  139.9 15.5 %all-to-all-start.1 = ((bf16[256,128,2]{0,2,1:T(2,128)(2,1)}), bf16[256,128,2]{0,2,1:T(2,128)(2,1)S(1)}, u32[]{:S(2)}, u32[]{:S(2)}) async-start(bf16[256,128,2]{0,2,1:T(2,128)(2,1)} %bitcast.33), calls=%async_computation.1 | async-start | bytes 262144 | tf_op jit(solution)/shard_map/all_to_all | solution.py:333
  159.8 5.8 %collective-permute-start.11 = (bf16[64,8,4,1]{3,0,2,1:T(8,128)(2,1)S(1)}, bf16[64,8,4,1]{3,0,2,1:T(8,128)(2,1)S(1)}, u32[]{:S(2)}, u32[]{:S(2)}) collective-permute-start(bf16[64,8,4,1]{3,0,2,1:T(8,128)(2,1)S(1)} %slice_select_fusion.2), channel_id=1, source_target_pairs={{0,4},{4,0},{1,5},{5,1},{2,6},{6,2},{3,7},{7,3},{8,12},{12,8},{9,1... | collective-permute-start | bytes 12296 | tf_op jit(solution)/shard_map/ppermute | solution.py:27
  166.0 7.1 %collective-permute-start.12 = (bf16[64,8,1,66]{3,0,2,1:T(8,128)(2,1)S(1)}, bf16[64,8,1,66]{3,0,2,1:T(8,128)(2,1)S(1)}, u32[]{:S(2)}, u32[]{:S(2)}) collective-permute-start(bf16[64,8,1,66]{3,0,2,1:T(8,128)(2,1)S(1)} %get-tuple-element.5), channel_id=1, source_target_pairs={{0,1},{1,2},{2,3},{4,5},{5,6},{6,7},{8,9},{9,10},{10,11},{12,13},{... | collective-permute-start | bytes 202760 | tf_op jit(solution)/shard_map/ppermute | solution.py:33
  170.9 5.7 %collective-permute-start.13 = (bf16[64,8,1,66]{3,0,2,1:T(8,128)(2,1)S(1)}, bf16[64,8,1,66]{3,0,2,1:T(8,128)(2,1)S(1)}, u32[]{:S(2)}, u32[]{:S(2)}) collective-permute-start(bf16[64,8,1,66]{3,0,2,1:T(8,128)(2,1)S(1)} %get-tuple-element.6), channel_id=1, source_target_pairs={{1,0},{2,1},{3,2},{5,4},{6,5},{7,6},{9,8},{10,9},{11,10},{13,12},{... | collective-permute-start | bytes 202760 | tf_op jit(solution)/shard_map/ppermute | solution.py:34
  178.3 6.5 %copy-start.13 = (bf16[64,16,2,2,2]{0,4,3,2,1:T(2,128)(2,1)S(1)}, bf16[64,16,2,2,2]{0,4,3,2,1:T(2,128)(2,1)}, u32[]{:S(2)}) copy-start(bf16[64,16,2,2,2]{0,4,3,2,1:T(2,128)(2,1)} %param.27) | copy-start | bytes 49156
  197.4 3.7 %collective-permute-start.14 = (bf16[10,16,1,128]{3,2,1,0:T(2,128)(2,1)S(1)}, bf16[10,16,1,128]{3,2,1,0:T(2,128)(2,1)S(1)}, u32[]{:S(2)}, u32[]{:S(2)}) collective-permute-start(bf16[10,16,1,128]{3,2,1,0:T(2,128)(2,1)S(1)} %get-tuple-element.15), channel_id=1, source_target_pairs={{0,1},{1,2},{2,3},{4,5},{5,6},{6,7},{8,9},{9,10},{10,11},{12,13},{... | collective-permute-start | bytes 122888 | tf_op jit(solution)/shard_map/ppermute | solution.py:135
  199.6 5.2 %collective-permute-start.15 = (bf16[10,16,1,128]{3,2,1,0:T(2,128)(2,1)S(1)}, bf16[10,16,1,128]{3,2,1,0:T(2,128)(2,1)S(1)}, u32[]{:S(2)}, u32[]{:S(2)}) collective-permute-start(bf16[10,16,1,128]{3,2,1,0:T(2,128)(2,1)S(1)} %get-tuple-element.16), channel_id=1, source_target_pairs={{1,0},{2,1},{3,2},{5,4},{6,5},{7,6},{9,8},{10,9},{11,10},{13,12},{... | collective-permute-start | bytes 122888 | tf_op jit(solution)/shard_map/ppermute | solution.py:135
  205.3 5.5 %copy-start.3 = (bf16[10,16,16,128]{3,2,1,0:T(8,128)(2,1)}, bf16[10,16,16,128]{3,2,1,0:T(8,128)(2,1)S(1)}, u32[]{:S(2)}) copy-start(bf16[10,16,16,128]{3,2,1,0:T(8,128)(2,1)S(1)} %maximum_maximum_fusion.2) | copy-start | bytes 1966084
  206.5 4.1 %collective-permute-start.16 = (bf16[10,16,16,1]{2,1,3,0:T(8,128)(2,1)S(1)}, bf16[10,16,16,1]{2,1,3,0:T(8,128)(2,1)S(1)}, u32[]{:S(2)}, u32[]{:S(2)}) collective-permute-start(bf16[10,16,16,1]{2,1,3,0:T(8,128)(2,1)S(1)} %copy.186), channel_id=1, source_target_pairs={{0,4},{4,0},{1,5},{5,1},{2,6},{6,2},{3,7},{7,3},{8,12},{12,8},{9,1... | collective-permute-start | bytes 15368 | tf_op jit(solution)/shard_map/ppermute | solution.py:131
  (10 other events, 25.1 us)

commit v6 on v5

--- a/solution.py
+++ b/solution.py
@@ -99,18 +99,16 @@
 
     lax.fori_loop(0, sx + 2, shift, 0)
 
+    group = 4 if sx % 4 == 0 else 2
+
     def rows_pair(g, carry):
-        x = 2 * g
+        x = group * g
         stack = jnp.concatenate(
-            [
-                shifted_ref[pl.ds(x, 3)].reshape(9 * depth, ss),
-                shifted_ref[pl.ds(x + 1, 3)].reshape(9 * depth, ss),
-            ],
-            axis=1,
+            [shifted_ref[pl.ds(x + k, 3)].reshape(9 * depth, ss) for k in range(group)], axis=1
         )
         acc = jnp.dot(band_ref[...], stack, preferred_element_type=jnp.float32)
         act = (acc * jax.nn.sigmoid(acc)).astype(jnp.bfloat16)
-        for k in range(2):
+        for k in range(group):
             part = act[:, k * ss : (k + 1) * ss]
             if head:
                 res = jnp.dot(h_ref[...], part, preferred_element_type=jnp.float32)
@@ -119,7 +117,7 @@
                 o_ref[x + k] = part.astype(jnp.float32).reshape(cout, sv, ss)
         return carry
 
-    lax.fori_loop(0, sx // 2, rows_pair, 0)
+    lax.fori_loop(0, sx // group, rows_pair, 0)
 
 
 def faces(block, axis, dim):
@@ -187,25 +185,23 @@
     lax.fori_loop(0, sx + 2, shift, 0)
     chans = shifted_ref.shape[2]
 
+    group = 4 if sx % 4 == 0 else 2
+
     def rows_pair(g, carry):
-        x = 2 * g
+        x = group * g
         stack = jnp.concatenate(
-            [
-                shifted_ref[pl.ds(x, 3)].reshape(27 * chans, span),
-                shifted_ref[pl.ds(x + 1, 3)].reshape(27 * chans, span),
-            ],
-            axis=1,
+            [shifted_ref[pl.ds(x + k, 3)].reshape(27 * chans, span) for k in range(group)], axis=1
         )
         acc = jnp.dot(w_ref[...], stack, preferred_element_type=jnp.float32)
         act = (acc * jax.nn.sigmoid(acc)).astype(jnp.bfloat16).astype(jnp.float32)
-        for k in range(2):
+        for k in range(group):
             part = act[:, k * span : (k + 1) * span]
             for v in range(sv):
                 piece = part if v == 0 else pltpu.roll(part, span - v * pitch, 1)
                 o_ref[x + k, v] = piece[:, :ss]
         return carry
 
-    lax.fori_loop(0, sx // 2, rows_pair, 0)
+    lax.fori_loop(0, sx // group, rows_pair, 0)
 
 
 def mid_conv(field, weight, sides=MID_SIDES):

time: 221 us -> 218 us (0.986)
  no operation moved by 1% of the time
where the time goes in v6:
time: 218 us; the launch traced here: 217 us
  starting transfers between devices  46.3 us (21%)
  local copies, waits for them, and re-layouts  43.1 us (20%)
  Pallas kernels  42.6 us (20%)
  waiting for transfers between devices  38.6 us (18%)
  blocking collectives  27.8 us (13%)
  other arithmetic  9.91 us (5%)
  matrix products  8.21 us (4%)
    pallas_call x3, Pallas kernels, fine_conv(): pl.pallas_call(kernel, out_shape=out_shape, scratch_shapes=[pltpu.VMEM((c...  30.5 us
    all_to_all x1, blocking collectives, on_device(): rows = lax.all_to_all(flat, 'gx', split_axis=2, concat_axis=1, tiled=True)  27.8 us
    ppermute x3, starting transfers between devices, extended(): low = lax.ppermute(top, axis, forward)  12.8 us
    ppermute x3, waiting for transfers between devices, faces(): lax.ppermute(bottom, axis, backward)  12.8 us
    pallas_call x2, Pallas kernels, mid_conv(): pl.pallas_call(kernel, out_shape=jax.ShapeDtypeStruct((sx, sv, cout, ss),...  12.1 us
    all_to_all x1, waiting for transfers between devices, on_device(): lax.all_to_all(windows, 'gx', split_axis=1, concat_axis=2, tiled=True)  10.8 us
    ppermute x3, waiting for transfers between devices, extended(): high = lax.ppermute(bottom, axis, backward)  9.9 us
    ppermute x3, starting transfers between devices, faces(): lax.ppermute(top, axis, forward)  9.32 us
  transfers between devices with their start and end apart: 18, of which 13 were waited for; matrix products, arithmetic and copies ran while one was open for 4% of the time, Pallas kernels for 0%

profile of v6, /device:TPU:1, one launch (start us, length us, event | category | flops | bytes accessed | tf_op | source)
XLA Modules:
  0.0 217.4 jit_solution(100353617189040415)
XLA Ops:
  0.9 3.9 %collective-permute-start = (bf16[8,4,8,128]{3,2,1,0:T(8,128)(2,1)S(1)}, bf16[8,4,8,128]{3,2,1,0:T(8,128)(2,1)S(1)}, u32[]{:S(2)}, u32[]{:S(2)}) collective-permute-start(bf16[8,4,8,128]{3,2,1,0:T(8,128)(2,1)S(1)} %bitcast.175), channel_id=1, source_target_pairs={{0,8},{8,16},{16,24},{24,32},{32,40},{40,48},{48,56},{56,64},{64,7... | collective-permute-start | bytes 196616 | tf_op jit(solution)/shard_map/ppermute | solution.py:33
  6.2 3.7 %collective-permute-done.1 = bf16[8,4,8,128]{3,2,1,0:T(8,128)(2,1)S(1)} collective-permute-done((bf16[8,4,8,128]{3,2,1,0:T(8,128)(2,1)S(1)}, bf16[8,4,8,128]{3,2,1,0:T(8,128)(2,1)S(1)}, u32[]{:S(2)}, u32[]{:S(2)}) %collective-permute-start.1) | collective-permute-done | bytes 65568 | tf_op jit(solution)/shard_map/ppermute | solution.py:34
  10.1 3.5 %collective-permute-start.2 = (bf16[24,8,1,128]{3,2,1,0:T(2,128)(2,1)S(1)}, bf16[24,8,1,128]{3,2,1,0:T(2,128)(2,1)S(1)}, u32[]{:S(2)}, u32[]{:S(2)}) collective-permute-start(bf16[24,8,1,128]{3,2,1,0:T(2,128)(2,1)S(1)} %get-tuple-element.17), channel_id=1, source_target_pairs={{0,1},{1,2},{2,3},{4,5},{5,6},{6,7},{8,9},{9,10},{10,11},{12,13},{... | collective-permute-start | bytes 147464 | tf_op jit(solution)/shard_map/ppermute | solution.py:133
  15.8 3.4 %collective-permute-done.3 = bf16[24,8,1,128]{3,2,1,0:T(2,128)(2,1)S(1)} collective-permute-done((bf16[24,8,1,128]{3,2,1,0:T(2,128)(2,1)S(1)}, bf16[24,8,1,128]{3,2,1,0:T(2,128)(2,1)S(1)}, u32[]{:S(2)}, u32[]{:S(2)}) %collective-permute-start.3) | collective-permute-done | bytes 49184 | tf_op jit(solution)/shard_map/ppermute | solution.py:133
  22.6 3.4 %collective-permute-start.4 = (bf16[24,8,16,1]{0,2,3,1:T(8,128)(2,1)S(1)}, bf16[24,8,16,1]{0,2,3,1:T(8,128)(2,1)S(1)}, u32[]{:S(2)}, u32[]{:S(2)}) collective-permute-start(bf16[24,8,16,1]{0,2,3,1:T(8,128)(2,1)S(1)} %broadcast_select_fusion.11), channel_id=1, source_target_pairs={{0,4},{4,0},{1,5},{5,1},{2,6},{6,2},{3,7},{7,3},{8,12},{12,8},{9,1... | collective-permute-start | bytes 18440 | tf_op jit(solution)/shard_map/ppermute | solution.py:129
  27.9 11.0 %shard_map.145 = f32[22,16,8,128]{3,2,1,0:T(8,128)} custom-call(bf16[24,128,128]{2,1,0:T(8,128)(2,1)} %bitcast.166, bf16[24,8,128]{2,1,0:T(8,128)(2,1)} %pad.33.refs_1_, bf16[27,16,8]{2,1,0:T(8,128)(2,1)} %bitcast.174), custom_call_target="tpu_custom_call" | custom-call | tf_op jit(solution)/shard_map/pallas_call | solution.py:162
  40.7 3.5 %collective-permute-start.5 = (bf16[22,16,1,128]{3,2,1,0:T(2,128)(2,1)S(1)}, bf16[22,16,1,128]{3,2,1,0:T(2,128)(2,1)S(1)}, u32[]{:S(2)}, u32[]{:S(2)}) collective-permute-start(bf16[22,16,1,128]{3,2,1,0:T(2,128)(2,1)S(1)} %get-tuple-element.9), channel_id=1, source_target_pairs={{0,1},{1,2},{2,3},{4,5},{5,6},{6,7},{8,9},{9,10},{10,11},{12,13},{... | collective-permute-start | bytes 270344 | tf_op jit(solution)/shard_map/ppermute | solution.py:133
  47.8 5.7 %collective-permute-done.6 = bf16[22,16,1,128]{3,2,1,0:T(2,128)(2,1)S(1)} collective-permute-done((bf16[22,16,1,128]{3,2,1,0:T(2,128)(2,1)S(1)}, bf16[22,16,1,128]{3,2,1,0:T(2,128)(2,1)S(1)}, u32[]{:S(2)}, u32[]{:S(2)}) %collective-permute-start.6) | collective-permute-done | bytes 90144 | tf_op jit(solution)/shard_map/ppermute | solution.py:133
  61.3 12.0 %shard_map.146 = f32[20,16,8,128]{3,2,1,0:T(8,128)} custom-call(bf16[22,256,128]{2,1,0:T(8,128)(2,1)} %bitcast.165, bf16[22,8,256]{2,1,0:T(8,128)(2,1)} %pad.35.refs_1_, bf16[27,16,16]{2,1,0:T(8,128)(2,1)} %bitcast.180), custom_call_target="tpu_custom_call" | custom-call | tf_op jit(solution)/shard_map/pallas_call | solution.py:162
  74.9 3.5 %copy.161 = bf16[20,16,8,128]{1,3,2,0:T(8,128)(2,1)} copy(bf16[20,16,8,128]{3,2,1,0:T(8,128)(2,1)S(1)} %convert_select_fusion.1) | data formatting | bytes 1310720 | tf_op jit(solution)/shard_map/jit(_where)/select_n | solution.py:46
  78.4 3.8 %multiply_convert_fusion = bf16[64,10,4,64]{0,3,2,1:T(8,128)(2,1)S(1)} fusion(bf16[10,2,16,4,2,64,2]{2,6,5,4,3,1,0:T(2,128)(2,1)} %bitcast.168, bf16[64,16,2,2,2,1,1]{0,4,3,2,1,6,5:T(2,128)(2,1)S(1)} %bitcast.183), kind=kOutput, calls=%fused_computation.8 | convolution fusion | flops 42762240 | bytes 999424 | tf_op jit(solution)/shard_map/xaivbsc,oiabc->oxvs/dot_general | solution.py:242
  87.5 4.0 %collective-permute-start.9 = (bf16[64,10,1,66]{0,3,2,1:T(8,128)(2,1)S(1)}, bf16[64,10,1,66]{0,3,2,1:T(8,128)(2,1)S(1)}, u32[]{:S(2)}, u32[]{:S(2)}) collective-permute-start(bf16[64,10,1,66]{0,3,2,1:T(8,128)(2,1)S(1)} %get-tuple-element.11), channel_id=1, source_target_pairs={{0,1},{1,2},{2,3},{4,5},{5,6},{6,7},{8,9},{9,10},{10,11},{12,13},{... | collective-permute-start | bytes 253448 | tf_op jit(solution)/shard_map/ppermute | solution.py:33
  97.3 6.5 %shard_map.147 = f32[8,4,64,64]{3,2,1,0:T(8,128)} custom-call(bf16[10,64,512]{2,1,0:T(8,128)(2,1)} %pad.36.refs_0_, bf16[64,1728]{1,0:T(8,128)(2,1)} %reshape.153.refs_1_), custom_call_target="tpu_custom_call" | custom-call | tf_op jit(solution)/shard_map/pallas_call | solution.py:220
  106.9 27.8 %all_to_all.24 = bf16[256,2,64]{0,1,2:T(2,128)(2,1)S(1)} all-to-all(bf16[256,2,64]{0,1,2:T(2,128)(2,1)S(1)} %copy.167), channel_id=1, replica_groups=mesh['gx'=32,'gy'=2,'gz'=4] {'gx'}, dimensions={2} | all-to-all | bytes 131072 | tf_op jit(solution)/shard_map/all_to_all | solution.py:317
  138.6 3.9 %all-to-all-start.1 = ((bf16[256,128,2]{0,2,1:T(2,128)(2,1)}), bf16[256,128,2]{0,2,1:T(2,128)(2,1)S(1)}, u32[]{:S(2)}, u32[]{:S(2)}) async-start(bf16[256,128,2]{0,2,1:T(2,128)(2,1)} %bitcast.33), calls=%async_computation.1 | async-start | bytes 262144 | tf_op jit(solution)/shard_map/all_to_all | solution.py:329
  143.0 10.8 %all-to-all-done.1 = bf16[256,128,2]{0,2,1:T(2,128)(2,1)S(1)} async-done(((bf16[256,128,2]{0,2,1:T(2,128)(2,1)}), bf16[256,128,2]{0,2,1:T(2,128)(2,1)S(1)}, u32[]{:S(2)}, u32[]{:S(2)}) %all-to-all-start.1) | async-done | bytes 131104 | tf_op jit(solution)/shard_map/all_to_all | solution.py:329
  158.3 3.9 %collective-permute-start.11 = (bf16[64,8,4,1]{3,0,2,1:T(8,128)(2,1)S(1)}, bf16[64,8,4,1]{3,0,2,1:T(8,128)(2,1)S(1)}, u32[]{:S(2)}, u32[]{:S(2)}) collective-permute-start(bf16[64,8,4,1]{3,0,2,1:T(8,128)(2,1)S(1)} %slice_select_fusion.2), channel_id=1, source_target_pairs={{0,4},{4,0},{1,5},{5,1},{2,6},{6,2},{3,7},{7,3},{8,12},{12,8},{9,1... | collective-permute-start | bytes 12296 | tf_op jit(solution)/shard_map/ppermute | solution.py:27
  164.4 4.9 %collective-permute-start.12 = (bf16[64,8,1,66]{3,0,2,1:T(8,128)(2,1)S(1)}, bf16[64,8,1,66]{3,0,2,1:T(8,128)(2,1)S(1)}, u32[]{:S(2)}, u32[]{:S(2)}) collective-permute-start(bf16[64,8,1,66]{3,0,2,1:T(8,128)(2,1)S(1)} %get-tuple-element.5), channel_id=1, source_target_pairs={{0,1},{1,2},{2,3},{4,5},{5,6},{6,7},{8,9},{9,10},{10,11},{12,13},{... | collective-permute-start | bytes 202760 | tf_op jit(solution)/shard_map/ppermute | solution.py:33
  171.5 3.5 %collective-permute-done.13 = bf16[64,8,1,66]{3,0,2,1:T(8,128)(2,1)S(1)} collective-permute-done((bf16[64,8,1,66]{3,0,2,1:T(8,128)(2,1)S(1)}, bf16[64,8,1,66]{3,0,2,1:T(8,128)(2,1)S(1)}, u32[]{:S(2)}, u32[]{:S(2)}) %collective-permute-start.13) | collective-permute-done | bytes 67616 | tf_op jit(solution)/shard_map/ppermute | solution.py:34
  177.6 5.7 %shard_map.148 = f32[6,4,64,64]{3,2,1,0:T(8,128)} custom-call(bf16[8,64,512]{2,1,0:T(8,128)(2,1)} %pad.38.refs_0_, bf16[64,1728]{1,0:T(8,128)(2,1)} %reshape.167.refs_1_), custom_call_target="tpu_custom_call" | custom-call | tf_op jit(solution)/shard_map/pallas_call | solution.py:220
  184.8 6.4 %copy.184 = f32[6,2,16,4,2,64,2]{2,6,5,4,3,1,0:T(2,128)} copy(f32[6,2,16,4,2,64,2]{5,2,6,4,1,3,0:T(8,128)S(1)} %convolution_bitcast_fusion) | data formatting | bytes 1572864 | tf_op jit(solution)/shard_map/ixvs,ioabc->xaovbsc/transpose | solution.py:246
  191.2 4.4 %copy.185 = f32[12,16,8,128]{3,2,1,0:T(8,128)S(1)} copy(f32[12,16,8,128]{1,3,2,0:T(8,128)} %bitcast.164) | data formatting | bytes 1572864 | tf_op jit(solution)/shard_map/reshape | solution.py:248
  199.5 3.7 %collective-permute-done.15 = bf16[10,16,1,128]{3,2,1,0:T(2,128)(2,1)S(1)} collective-permute-done((bf16[10,16,1,128]{3,2,1,0:T(2,128)(2,1)S(1)}, bf16[10,16,1,128]{3,2,1,0:T(2,128)(2,1)S(1)}, u32[]{:S(2)}, u32[]{:S(2)}) %collective-permute-start.15) | collective-permute-done | bytes 40992 | tf_op jit(solution)/shard_map/ppermute | solution.py:133
  209.9 7.5 %shard_map.149 = f32[4,8,8,128]{3,2,1,0:T(8,128)} custom-call(bf16[10,256,128]{2,1,0:T(8,128)(2,1)} %bitcast.167, bf16[10,8,256]{2,1,0:T(8,128)(2,1)} %pad.39.refs_1_, bf16[27,16,16]{2,1,0:T(8,128)(2,1)} %bitcast.181, bf16[32,128]{1,0:T(8,128)(2,1)} %convert_element_type.137.refs_3_), custom_call_target="tpu_custom_call" | custom-call | tf_op jit(solution)/shard_map/pallas_call | solution.py:162
  (160 shorter events, 66.0 us)
Async XLA Ops:
  0.0 135.3 %copy-start = (bf16[256,256]{1,0:T(8,128)(2,1)S(1)}, bf16[256,256]{1,0:T(8,128)(2,1)}, u32[]{:S(2)}) copy-start(bf16[256,256]{1,0:T(8,128)(2,1)} %param.22) | copy-start | bytes 393220
  0.9 5.3 %collective-permute-start = (bf16[8,4,8,128]{3,2,1,0:T(8,128)(2,1)S(1)}, bf16[8,4,8,128]{3,2,1,0:T(8,128)(2,1)S(1)}, u32[]{:S(2)}, u32[]{:S(2)}) collective-permute-start(bf16[8,4,8,128]{3,2,1,0:T(8,128)(2,1)S(1)} %bitcast.175), channel_id=1, source_target_pairs={{0,8},{8,16},{16,24},{24,32},{32,40},{40,48},{48,56},{56,64},{64,7... | collective-permute-start | bytes 196616 | tf_op jit(solution)/shard_map/ppermute | solution.py:33
  4.8 5.0 %collective-permute-start.1 = (bf16[8,4,8,128]{3,2,1,0:T(8,128)(2,1)S(1)}, bf16[8,4,8,128]{3,2,1,0:T(8,128)(2,1)S(1)}, u32[]{:S(2)}, u32[]{:S(2)}) collective-permute-start(bf16[8,4,8,128]{3,2,1,0:T(8,128)(2,1)S(1)} %bitcast.176), channel_id=1, source_target_pairs={{8,0},{16,8},{24,16},{32,24},{40,32},{48,40},{56,48},{64,56},{72,6... | collective-permute-start | bytes 196616 | tf_op jit(solution)/shard_map/ppermute | solution.py:34
  10.1 5.7 %collective-permute-start.2 = (bf16[24,8,1,128]{3,2,1,0:T(2,128)(2,1)S(1)}, bf16[24,8,1,128]{3,2,1,0:T(2,128)(2,1)S(1)}, u32[]{:S(2)}, u32[]{:S(2)}) collective-permute-start(bf16[24,8,1,128]{3,2,1,0:T(2,128)(2,1)S(1)} %get-tuple-element.17), channel_id=1, source_target_pairs={{0,1},{1,2},{2,3},{4,5},{5,6},{6,7},{8,9},{9,10},{10,11},{12,13},{... | collective-permute-start | bytes 147464 | tf_op jit(solution)/shard_map/ppermute | solution.py:133
  13.6 5.5 %collective-permute-start.3 = (bf16[24,8,1,128]{3,2,1,0:T(2,128)(2,1)S(1)}, bf16[24,8,1,128]{3,2,1,0:T(2,128)(2,1)S(1)}, u32[]{:S(2)}, u32[]{:S(2)}) collective-permute-start(bf16[24,8,1,128]{3,2,1,0:T(2,128)(2,1)S(1)} %get-tuple-element.18), channel_id=1, source_target_pairs={{1,0},{2,1},{3,2},{5,4},{6,5},{7,6},{9,8},{10,9},{11,10},{13,12},{... | collective-permute-start | bytes 147464 | tf_op jit(solution)/shard_map/ppermute | solution.py:133
  22.6 4.3 %collective-permute-start.4 = (bf16[24,8,16,1]{0,2,3,1:T(8,128)(2,1)S(1)}, bf16[24,8,16,1]{0,2,3,1:T(8,128)(2,1)S(1)}, u32[]{:S(2)}, u32[]{:S(2)}) collective-permute-start(bf16[24,8,16,1]{0,2,3,1:T(8,128)(2,1)S(1)} %broadcast_select_fusion.11), channel_id=1, source_target_pairs={{0,4},{4,0},{1,5},{5,1},{2,6},{6,2},{3,7},{7,3},{8,12},{12,8},{9,1... | collective-permute-start | bytes 18440 | tf_op jit(solution)/shard_map/ppermute | solution.py:129
  40.7 7.1 %collective-permute-start.5 = (bf16[22,16,1,128]{3,2,1,0:T(2,128)(2,1)S(1)}, bf16[22,16,1,128]{3,2,1,0:T(2,128)(2,1)S(1)}, u32[]{:S(2)}, u32[]{:S(2)}) collective-permute-start(bf16[22,16,1,128]{3,2,1,0:T(2,128)(2,1)S(1)} %get-tuple-element.9), channel_id=1, source_target_pairs={{0,1},{1,2},{2,3},{4,5},{5,6},{6,7},{8,9},{9,10},{10,11},{12,13},{... | collective-permute-start | bytes 270344 | tf_op jit(solution)/shard_map/ppermute | solution.py:133
  44.2 9.2 %collective-permute-start.6 = (bf16[22,16,1,128]{3,2,1,0:T(2,128)(2,1)S(1)}, bf16[22,16,1,128]{3,2,1,0:T(2,128)(2,1)S(1)}, u32[]{:S(2)}, u32[]{:S(2)}) collective-permute-start(bf16[22,16,1,128]{3,2,1,0:T(2,128)(2,1)S(1)} %get-tuple-element.10), channel_id=1, source_target_pairs={{1,0},{2,1},{3,2},{5,4},{6,5},{7,6},{9,8},{10,9},{11,10},{13,12},{... | collective-permute-start | bytes 270344 | tf_op jit(solution)/shard_map/ppermute | solution.py:133
  57.7 2.3 %collective-permute-start.7 = (bf16[22,16,16,1]{0,2,3,1:T(8,128)(2,1)S(1)}, bf16[22,16,16,1]{0,2,3,1:T(8,128)(2,1)S(1)}, u32[]{:S(2)}, u32[]{:S(2)}) collective-permute-start(bf16[22,16,16,1]{0,2,3,1:T(8,128)(2,1)S(1)} %copy.157), channel_id=1, source_target_pairs={{0,4},{4,0},{1,5},{5,1},{2,6},{6,2},{3,7},{7,3},{8,12},{12,8},{9,1... | collective-permute-start | bytes 33800 | tf_op jit(solution)/shard_map/ppermute | solution.py:129
  82.3 3.6 %collective-permute-start.8 = (bf16[64,10,4,1]{0,3,2,1:T(2,128)(2,1)S(1)}, bf16[64,10,4,1]{0,3,2,1:T(2,128)(2,1)S(1)}, u32[]{:S(2)}, u32[]{:S(2)}) collective-permute-start(bf16[64,10,4,1]{0,3,2,1:T(2,128)(2,1)S(1)} %broadcast_select_fusion.8), channel_id=1, source_target_pairs={{0,4},{4,0},{1,5},{5,1},{2,6},{6,2},{3,7},{7,3},{8,12},{12,8},{9,1... | collective-permute-start | bytes 15368 | tf_op jit(solution)/shard_map/ppermute | solution.py:27
  86.2 8.0 %collective-permute-start.10 = (bf16[64,10,1,66]{0,3,2,1:T(8,128)(2,1)S(1)}, bf16[64,10,1,66]{0,3,2,1:T(8,128)(2,1)S(1)}, u32[]{:S(2)}, u32[]{:S(2)}) collective-permute-start(bf16[64,10,1,66]{0,3,2,1:T(8,128)(2,1)S(1)} %get-tuple-element.12), channel_id=1, source_target_pairs={{1,0},{2,1},{3,2},{5,4},{6,5},{7,6},{9,8},{10,9},{11,10},{13,12},{... | collective-permute-start | bytes 253448 | tf_op jit(solution)/shard_map/ppermute | solution.py:34
  87.5 7.6 %collective-permute-start.9 = (bf16[64,10,1,66]{0,3,2,1:T(8,128)(2,1)S(1)}, bf16[64,10,1,66]{0,3,2,1:T(8,128)(2,1)S(1)}, u32[]{:S(2)}, u32[]{:S(2)}) collective-permute-start(bf16[64,10,1,66]{0,3,2,1:T(8,128)(2,1)S(1)} %get-tuple-element.11), channel_id=1, source_target_pairs={{0,1},{1,2},{2,3},{4,5},{5,6},{6,7},{8,9},{9,10},{10,11},{12,13},{... | collective-permute-start | bytes 253448 | tf_op jit(solution)/shard_map/ppermute | solution.py:33
  106.8 28.9 %copy-start.11 = (bf16[256,256]{1,0:T(8,128)(2,1)S(1)}, bf16[256,256]{1,0:T(8,128)(2,1)}, u32[]{:S(2)}) copy-start(bf16[256,256]{1,0:T(8,128)(2,1)} %param.21) | copy-start | bytes 393220
  106.9 29.5 %copy-start.12 = (bf16[256,256]{1,0:T(8,128)(2,1)S(1)}, bf16[256,256]{1,0:T(8,128)(2,1)}, u32[]{:S(2)}) copy-start(bf16[256,256]{1,0:T(8,128)(2,1)} %param.23) | copy-start | bytes 393220
  136.8 5.7 %copy-start.7 = (bf16[8,16384]{1,0:T(8,128)(2,1)S(1)}, bf16[8,16384]{1,0:T(8,128)(2,1)}, u32[]{:S(2)}) copy-start(bf16[8,16384]{1,0:T(8,128)(2,1)} %param.25) | copy-start | bytes 786436
  138.6 15.3 %all-to-all-start.1 = ((bf16[256,128,2]{0,2,1:T(2,128)(2,1)}), bf16[256,128,2]{0,2,1:T(2,128)(2,1)S(1)}, u32[]{:S(2)}, u32[]{:S(2)}) async-start(bf16[256,128,2]{0,2,1:T(2,128)(2,1)} %bitcast.33), calls=%async_computation.1 | async-start | bytes 262144 | tf_op jit(solution)/shard_map/all_to_all | solution.py:329
  158.3 5.8 %collective-permute-start.11 = (bf16[64,8,4,1]{3,0,2,1:T(8,128)(2,1)S(1)}, bf16[64,8,4,1]{3,0,2,1:T(8,128)(2,1)S(1)}, u32[]{:S(2)}, u32[]{:S(2)}) collective-permute-start(bf16[64,8,4,1]{3,0,2,1:T(8,128)(2,1)S(1)} %slice_select_fusion.2), channel_id=1, source_target_pairs={{0,4},{4,0},{1,5},{5,1},{2,6},{6,2},{3,7},{7,3},{8,12},{12,8},{9,1... | collective-permute-start | bytes 12296 | tf_op jit(solution)/shard_map/ppermute | solution.py:27
  164.4 7.1 %collective-permute-start.12 = (bf16[64,8,1,66]{3,0,2,1:T(8,128)(2,1)S(1)}, bf16[64,8,1,66]{3,0,2,1:T(8,128)(2,1)S(1)}, u32[]{:S(2)}, u32[]{:S(2)}) collective-permute-start(bf16[64,8,1,66]{3,0,2,1:T(8,128)(2,1)S(1)} %get-tuple-element.5), channel_id=1, source_target_pairs={{0,1},{1,2},{2,3},{4,5},{5,6},{6,7},{8,9},{9,10},{10,11},{12,13},{... | collective-permute-start | bytes 202760 | tf_op jit(solution)/shard_map/ppermute | solution.py:33
  169.3 5.7 %collective-permute-start.13 = (bf16[64,8,1,66]{3,0,2,1:T(8,128)(2,1)S(1)}, bf16[64,8,1,66]{3,0,2,1:T(8,128)(2,1)S(1)}, u32[]{:S(2)}, u32[]{:S(2)}) collective-permute-start(bf16[64,8,1,66]{3,0,2,1:T(8,128)(2,1)S(1)} %get-tuple-element.6), channel_id=1, source_target_pairs={{1,0},{2,1},{3,2},{5,4},{6,5},{7,6},{9,8},{10,9},{11,10},{13,12},{... | collective-permute-start | bytes 202760 | tf_op jit(solution)/shard_map/ppermute | solution.py:34
  176.7 6.5 %copy-start.13 = (bf16[64,16,2,2,2]{0,4,3,2,1:T(2,128)(2,1)S(1)}, bf16[64,16,2,2,2]{0,4,3,2,1:T(2,128)(2,1)}, u32[]{:S(2)}) copy-start(bf16[64,16,2,2,2]{0,4,3,2,1:T(2,128)(2,1)} %param.27) | copy-start | bytes 49156
  195.8 3.7 %collective-permute-start.14 = (bf16[10,16,1,128]{3,2,1,0:T(2,128)(2,1)S(1)}, bf16[10,16,1,128]{3,2,1,0:T(2,128)(2,1)S(1)}, u32[]{:S(2)}, u32[]{:S(2)}) collective-permute-start(bf16[10,16,1,128]{3,2,1,0:T(2,128)(2,1)S(1)} %get-tuple-element.15), channel_id=1, source_target_pairs={{0,1},{1,2},{2,3},{4,5},{5,6},{6,7},{8,9},{9,10},{10,11},{12,13},{... | collective-permute-start | bytes 122888 | tf_op jit(solution)/shard_map/ppermute | solution.py:133
  198.0 5.2 %collective-permute-start.15 = (bf16[10,16,1,128]{3,2,1,0:T(2,128)(2,1)S(1)}, bf16[10,16,1,128]{3,2,1,0:T(2,128)(2,1)S(1)}, u32[]{:S(2)}, u32[]{:S(2)}) collective-permute-start(bf16[10,16,1,128]{3,2,1,0:T(2,128)(2,1)S(1)} %get-tuple-element.16), channel_id=1, source_target_pairs={{1,0},{2,1},{3,2},{5,4},{6,5},{7,6},{9,8},{10,9},{11,10},{13,12},{... | collective-permute-start | bytes 122888 | tf_op jit(solution)/shard_map/ppermute | solution.py:133
  203.7 5.5 %copy-start.3 = (bf16[10,16,16,128]{3,2,1,0:T(8,128)(2,1)}, bf16[10,16,16,128]{3,2,1,0:T(8,128)(2,1)S(1)}, u32[]{:S(2)}) copy-start(bf16[10,16,16,128]{3,2,1,0:T(8,128)(2,1)S(1)} %maximum_maximum_fusion.2) | copy-start | bytes 1966084
  205.0 4.1 %collective-permute-start.16 = (bf16[10,16,16,1]{2,1,3,0:T(8,128)(2,1)S(1)}, bf16[10,16,16,1]{2,1,3,0:T(8,128)(2,1)S(1)}, u32[]{:S(2)}, u32[]{:S(2)}) collective-permute-start(bf16[10,16,16,1]{2,1,3,0:T(8,128)(2,1)S(1)} %copy.186), channel_id=1, source_target_pairs={{0,4},{4,0},{1,5},{5,1},{2,6},{6,2},{3,7},{7,3},{8,12},{12,8},{9,1... | collective-permute-start | bytes 15368 | tf_op jit(solution)/shard_map/ppermute | solution.py:129
  (10 other events, 25.1 us)

commit v7 on v6

--- a/solution.py
+++ b/solution.py
@@ -89,7 +89,7 @@
 
     def shift(x, carry):
         slab = p_ref[x].astype(jnp.float32)
-        edges = jnp.transpose(e_ref[x].astype(jnp.float32))
+        edges = e_ref[x].astype(jnp.float32)
         low = jnp.where(lane == 0, edges[:, 0:1], pltpu.roll(slab, 1, 1))
         high = jnp.where(lane == ss - 1, edges[:, 1:2], pltpu.roll(slab, ss - 1, 1))
         shifted_ref[x, 0] = low.astype(jnp.bfloat16)
@@ -144,8 +144,7 @@
     spare = jnp.zeros((rows_x, wide, rows - sv - 2, ss), block.dtype)
     padded = jnp.concatenate([block, below, above, spare], axis=2)
     left, right = faces(padded, "gy", 3)
-    edges = jnp.concatenate([left, right], axis=3).transpose(0, 3, 1, 2)
-    edges = jnp.pad(edges.reshape(rows_x, 2, wide * rows), ((0, 0), (0, 6), (0, 0)))
+    edges = jnp.concatenate([left, right], axis=3).reshape(rows_x, wide * rows, 2)
     padded = padded.reshape(rows_x, wide * rows, ss)
     taps = jnp.pad(weight, ((0, 0), (0, wide - cin), (0, 0), (0, 0), (0, 0)))
     operands = [padded, edges, taps.transpose(2, 3, 4, 0, 1).reshape(27, cout, wide)]

time: 218 us -> 232 us (1.064); the launches traced: 217 us -> 229 us
  blocking collectives: 27.8 us -> 37.8 us
  local copies, waits for them, and re-layouts: 43.1 us -> 48 us
  Pallas kernels: 42.6 us -> 38.7 us
    all_to_all x1, blocking collectives: 27.8 us -> 37.8 us  [on_device(): rows = lax.all_to_all(flat, 'gx', split_axis=2, concat_axis=1, tiled=True)]
    concatenate x0 -> x3, local copies, waits for them, and re-layouts: none -> 7.9 us  [fine_conv(): jnp.concatenate([left, right], axis=3).reshape(rows_x, wide * rows, 2)]
    pallas_call x3, Pallas kernels: 30.5 us -> 26.5 us  [fine_conv(): pl.pallas_call(kernel, out_shape=out_shape, scratch_shapes=[pltpu.VMEM((c...]
where the time goes in v7:
time: 232 us; the launch traced here: 229 us
  local copies, waits for them, and re-layouts  48 us (21%)
  starting transfers between devices  46.4 us (20%)
  Pallas kernels  38.7 us (17%)
  waiting for transfers between devices  38.6 us (17%)
  blocking collectives  37.8 us (16%)
  other arithmetic  9.91 us (4%)
  matrix products  8.21 us (4%)
    all_to_all x1, blocking collectives, on_device(): rows = lax.all_to_all(flat, 'gx', split_axis=2, concat_axis=1, tiled=True)  37.8 us
    pallas_call x3, Pallas kernels, fine_conv(): pl.pallas_call(kernel, out_shape=out_shape, scratch_shapes=[pltpu.VMEM((c...  26.5 us
    ppermute x3, starting transfers between devices, extended(): low = lax.ppermute(top, axis, forward)  12.8 us
    ppermute x3, waiting for transfers between devices, faces(): lax.ppermute(bottom, axis, backward)  12.8 us
    pallas_call x2, Pallas kernels, mid_conv(): pl.pallas_call(kernel, out_shape=jax.ShapeDtypeStruct((sx, sv, cout, ss),...  12.1 us
    all_to_all x1, waiting for transfers between devices, on_device(): lax.all_to_all(windows, 'gx', split_axis=1, concat_axis=2, tiled=True)  10.8 us
    ppermute x3, waiting for transfers between devices, extended(): high = lax.ppermute(bottom, axis, backward)  9.9 us
    ppermute x3, starting transfers between devices, faces(): lax.ppermute(top, axis, forward)  9.02 us
  transfers between devices with their start and end apart: 18, of which 13 were waited for; matrix products, arithmetic and copies ran while one was open for 4% of the time, Pallas kernels for 0%

profile of v7, /device:TPU:1, one launch (start us, length us, event | category | flops | bytes accessed | tf_op | source)
XLA Modules:
  0.0 228.6 jit_solution(7032184210069852430)
XLA Ops:
  0.9 3.9 %collective-permute-start = (bf16[8,4,8,128]{3,2,1,0:T(8,128)(2,1)S(1)}, bf16[8,4,8,128]{3,2,1,0:T(8,128)(2,1)S(1)}, u32[]{:S(2)}, u32[]{:S(2)}) collective-permute-start(bf16[8,4,8,128]{3,2,1,0:T(8,128)(2,1)S(1)} %bitcast.169), channel_id=1, source_target_pairs={{0,8},{8,16},{16,24},{24,32},{32,40},{40,48},{48,56},{56,64},{64,7... | collective-permute-start | bytes 196616 | tf_op jit(solution)/shard_map/ppermute | solution.py:33
  6.2 3.7 %collective-permute-done.1 = bf16[8,4,8,128]{3,2,1,0:T(8,128)(2,1)S(1)} collective-permute-done((bf16[8,4,8,128]{3,2,1,0:T(8,128)(2,1)S(1)}, bf16[8,4,8,128]{3,2,1,0:T(8,128)(2,1)S(1)}, u32[]{:S(2)}, u32[]{:S(2)}) %collective-permute-start.1) | collective-permute-done | bytes 65568 | tf_op jit(solution)/shard_map/ppermute | solution.py:34
  10.1 3.5 %collective-permute-start.2 = (bf16[24,8,1,128]{3,2,1,0:T(2,128)(2,1)S(1)}, bf16[24,8,1,128]{3,2,1,0:T(2,128)(2,1)S(1)}, u32[]{:S(2)}, u32[]{:S(2)}) collective-permute-start(bf16[24,8,1,128]{3,2,1,0:T(2,128)(2,1)S(1)} %get-tuple-element.17), channel_id=1, source_target_pairs={{0,1},{1,2},{2,3},{4,5},{5,6},{6,7},{8,9},{9,10},{10,11},{12,13},{... | collective-permute-start | bytes 147464 | tf_op jit(solution)/shard_map/ppermute | solution.py:133
  29.2 8.8 %shard_map.145 = f32[22,16,8,128]{3,2,1,0:T(8,128)} custom-call(bf16[24,128,128]{2,1,0:T(8,128)(2,1)} %bitcast.157, bf16[24,128,2]{2,1,0:T(8,128)(2,1)} %bitcast.162, bf16[27,16,8]{2,1,0:T(8,128)(2,1)} %bitcast.168), custom_call_target="tpu_custom_call" | custom-call | tf_op jit(solution)/shard_map/pallas_call | solution.py:161
  39.8 3.6 %collective-permute-start.5 = (bf16[22,16,1,128]{3,2,1,0:T(2,128)(2,1)S(1)}, bf16[22,16,1,128]{3,2,1,0:T(2,128)(2,1)S(1)}, u32[]{:S(2)}, u32[]{:S(2)}) collective-permute-start(bf16[22,16,1,128]{3,2,1,0:T(2,128)(2,1)S(1)} %get-tuple-element.9), channel_id=1, source_target_pairs={{0,1},{1,2},{2,3},{4,5},{5,6},{6,7},{8,9},{9,10},{10,11},{12,13},{... | collective-permute-start | bytes 270344 | tf_op jit(solution)/shard_map/ppermute | solution.py:133
  47.0 5.7 %collective-permute-done.6 = bf16[22,16,1,128]{3,2,1,0:T(2,128)(2,1)S(1)} collective-permute-done((bf16[22,16,1,128]{3,2,1,0:T(2,128)(2,1)S(1)}, bf16[22,16,1,128]{3,2,1,0:T(2,128)(2,1)S(1)}, u32[]{:S(2)}, u32[]{:S(2)}) %collective-permute-start.6) | collective-permute-done | bytes 90144 | tf_op jit(solution)/shard_map/ppermute | solution.py:133
  59.3 3.8 %copy.154 = bf16[22,16,16,2]{3,2,1,0:T(8,128)(2,1)} copy(bf16[22,16,16,2]{0,2,3,1:T(8,128)(2,1)S(1)} %pad_maximum_fusion.6) | data formatting | bytes 45056 | tf_op jit(solution)/shard_map/concatenate | solution.py:147
  63.1 10.8 %shard_map.146 = f32[20,16,8,128]{3,2,1,0:T(8,128)} custom-call(bf16[22,256,128]{2,1,0:T(8,128)(2,1)} %bitcast.156, bf16[22,256,2]{2,1,0:T(8,128)(2,1)} %bitcast.159, bf16[27,16,16]{2,1,0:T(8,128)(2,1)} %bitcast.174), custom_call_target="tpu_custom_call" | custom-call | tf_op jit(solution)/shard_map/pallas_call | solution.py:161
  75.4 3.5 %copy.155 = bf16[20,16,8,128]{1,3,2,0:T(8,128)(2,1)} copy(bf16[20,16,8,128]{3,2,1,0:T(8,128)(2,1)S(1)} %convert_select_fusion.1) | data formatting | bytes 1310720 | tf_op jit(solution)/shard_map/jit(_where)/select_n | solution.py:46
  78.9 3.8 %multiply_convert_fusion = bf16[64,10,4,64]{0,3,2,1:T(8,128)(2,1)S(1)} fusion(bf16[10,2,16,4,2,64,2]{2,6,5,4,3,1,0:T(2,128)(2,1)} %bitcast.160, bf16[64,16,2,2,2,1,1]{0,4,3,2,1,6,5:T(2,128)(2,1)S(1)} %bitcast.177), kind=kOutput, calls=%fused_computation.8 | convolution fusion | flops 42762240 | bytes 999424 | tf_op jit(solution)/shard_map/xaivbsc,oiabc->oxvs/dot_general | solution.py:241
  88.0 4.0 %collective-permute-start.9 = (bf16[64,10,1,66]{0,3,2,1:T(8,128)(2,1)S(1)}, bf16[64,10,1,66]{0,3,2,1:T(8,128)(2,1)S(1)}, u32[]{:S(2)}, u32[]{:S(2)}) collective-permute-start(bf16[64,10,1,66]{0,3,2,1:T(8,128)(2,1)S(1)} %get-tuple-element.11), channel_id=1, source_target_pairs={{0,1},{1,2},{2,3},{4,5},{5,6},{6,7},{8,9},{9,10},{10,11},{12,13},{... | collective-permute-start | bytes 253448 | tf_op jit(solution)/shard_map/ppermute | solution.py:33
  97.8 6.5 %shard_map.147 = f32[8,4,64,64]{3,2,1,0:T(8,128)} custom-call(bf16[10,64,512]{2,1,0:T(8,128)(2,1)} %pad.22.refs_0_, bf16[64,1728]{1,0:T(8,128)(2,1)} %reshape.153.refs_1_), custom_call_target="tpu_custom_call" | custom-call | tf_op jit(solution)/shard_map/pallas_call | solution.py:219
  107.5 37.8 %all_to_all.24 = bf16[256,2,64]{0,1,2:T(2,128)(2,1)S(1)} all-to-all(bf16[256,2,64]{0,1,2:T(2,128)(2,1)S(1)} %copy.161), channel_id=1, replica_groups=mesh['gx'=32,'gy'=2,'gz'=4] {'gx'}, dimensions={2} | all-to-all | bytes 131072 | tf_op jit(solution)/shard_map/all_to_all | solution.py:316
  149.1 3.9 %all-to-all-start.1 = ((bf16[256,128,2]{0,2,1:T(2,128)(2,1)}), bf16[256,128,2]{0,2,1:T(2,128)(2,1)S(1)}, u32[]{:S(2)}, u32[]{:S(2)}) async-start(bf16[256,128,2]{0,2,1:T(2,128)(2,1)} %bitcast.33), calls=%async_computation.1 | async-start | bytes 262144 | tf_op jit(solution)/shard_map/all_to_all | solution.py:328
  153.5 10.8 %all-to-all-done.1 = bf16[256,128,2]{0,2,1:T(2,128)(2,1)S(1)} async-done(((bf16[256,128,2]{0,2,1:T(2,128)(2,1)}), bf16[256,128,2]{0,2,1:T(2,128)(2,1)S(1)}, u32[]{:S(2)}, u32[]{:S(2)}) %all-to-all-start.1) | async-done | bytes 131104 | tf_op jit(solution)/shard_map/all_to_all | solution.py:328
  168.8 3.9 %collective-permute-start.11 = (bf16[64,8,4,1]{3,0,2,1:T(8,128)(2,1)S(1)}, bf16[64,8,4,1]{3,0,2,1:T(8,128)(2,1)S(1)}, u32[]{:S(2)}, u32[]{:S(2)}) collective-permute-start(bf16[64,8,4,1]{3,0,2,1:T(8,128)(2,1)S(1)} %slice_select_fusion.2), channel_id=1, source_target_pairs={{0,4},{4,0},{1,5},{5,1},{2,6},{6,2},{3,7},{7,3},{8,12},{12,8},{9,1... | collective-permute-start | bytes 12296 | tf_op jit(solution)/shard_map/ppermute | solution.py:27
  174.9 4.9 %collective-permute-start.12 = (bf16[64,8,1,66]{3,0,2,1:T(8,128)(2,1)S(1)}, bf16[64,8,1,66]{3,0,2,1:T(8,128)(2,1)S(1)}, u32[]{:S(2)}, u32[]{:S(2)}) collective-permute-start(bf16[64,8,1,66]{3,0,2,1:T(8,128)(2,1)S(1)} %get-tuple-element.5), channel_id=1, source_target_pairs={{0,1},{1,2},{2,3},{4,5},{5,6},{6,7},{8,9},{9,10},{10,11},{12,13},{... | collective-permute-start | bytes 202760 | tf_op jit(solution)/shard_map/ppermute | solution.py:33
  182.0 3.5 %collective-permute-done.13 = bf16[64,8,1,66]{3,0,2,1:T(8,128)(2,1)S(1)} collective-permute-done((bf16[64,8,1,66]{3,0,2,1:T(8,128)(2,1)S(1)}, bf16[64,8,1,66]{3,0,2,1:T(8,128)(2,1)S(1)}, u32[]{:S(2)}, u32[]{:S(2)}) %collective-permute-start.13) | collective-permute-done | bytes 67616 | tf_op jit(solution)/shard_map/ppermute | solution.py:34
  188.1 5.7 %shard_map.148 = f32[6,4,64,64]{3,2,1,0:T(8,128)} custom-call(bf16[8,64,512]{2,1,0:T(8,128)(2,1)} %pad.24.refs_0_, bf16[64,1728]{1,0:T(8,128)(2,1)} %reshape.167.refs_1_), custom_call_target="tpu_custom_call" | custom-call | tf_op jit(solution)/shard_map/pallas_call | solution.py:219
  195.3 6.4 %copy.178 = f32[6,2,16,4,2,64,2]{2,6,5,4,3,1,0:T(2,128)} copy(f32[6,2,16,4,2,64,2]{5,2,6,4,1,3,0:T(8,128)S(1)} %convolution_bitcast_fusion) | data formatting | bytes 1572864 | tf_op jit(solution)/shard_map/ixvs,ioabc->xaovbsc/transpose | solution.py:245
  201.7 4.4 %copy.179 = f32[12,16,8,128]{3,2,1,0:T(8,128)S(1)} copy(f32[12,16,8,128]{1,3,2,0:T(8,128)} %bitcast.155) | data formatting | bytes 1572864 | tf_op jit(solution)/shard_map/reshape | solution.py:247
  209.7 3.7 %collective-permute-done.15 = bf16[10,16,1,128]{3,2,1,0:T(2,128)(2,1)S(1)} collective-permute-done((bf16[10,16,1,128]{3,2,1,0:T(2,128)(2,1)S(1)}, bf16[10,16,1,128]{3,2,1,0:T(2,128)(2,1)S(1)}, u32[]{:S(2)}, u32[]{:S(2)}) %collective-permute-start.15) | collective-permute-done | bytes 40992 | tf_op jit(solution)/shard_map/ppermute | solution.py:133
  215.2 3.6 %collective-permute-start.16 = (bf16[10,16,16,1]{2,1,3,0:T(8,128)(2,1)S(1)}, bf16[10,16,16,1]{2,1,3,0:T(8,128)(2,1)S(1)}, u32[]{:S(2)}, u32[]{:S(2)}) collective-permute-start(bf16[10,16,16,1]{2,1,3,0:T(8,128)(2,1)S(1)} %copy.180), channel_id=1, source_target_pairs={{0,4},{4,0},{1,5},{5,1},{2,6},{6,2},{3,7},{7,3},{8,12},{12,8},{9,1... | collective-permute-start | bytes 15368 | tf_op jit(solution)/shard_map/ppermute | solution.py:129
  221.5 6.9 %shard_map.149 = f32[4,8,8,128]{3,2,1,0:T(8,128)} custom-call(bf16[10,256,128]{2,1,0:T(8,128)(2,1)} %bitcast.158, bf16[10,256,2]{2,1,0:T(8,128)(2,1)} %bitcast.163, bf16[27,16,16]{2,1,0:T(8,128)(2,1)} %bitcast.175, bf16[32,128]{1,0:T(8,128)(2,1)} %convert_element_type.131.refs_3_), custom_call_target="tpu_custom_call" | custom-call | tf_op jit(solution)/shard_map/pallas_call | solution.py:161
  (155 shorter events, 70.5 us)
Async XLA Ops:
  0.0 145.8 %copy-start = (bf16[256,256]{1,0:T(8,128)(2,1)S(1)}, bf16[256,256]{1,0:T(8,128)(2,1)}, u32[]{:S(2)}) copy-start(bf16[256,256]{1,0:T(8,128)(2,1)} %param.22) | copy-start | bytes 393220
  0.9 5.3 %collective-permute-start = (bf16[8,4,8,128]{3,2,1,0:T(8,128)(2,1)S(1)}, bf16[8,4,8,128]{3,2,1,0:T(8,128)(2,1)S(1)}, u32[]{:S(2)}, u32[]{:S(2)}) collective-permute-start(bf16[8,4,8,128]{3,2,1,0:T(8,128)(2,1)S(1)} %bitcast.169), channel_id=1, source_target_pairs={{0,8},{8,16},{16,24},{24,32},{32,40},{40,48},{48,56},{56,64},{64,7... | collective-permute-start | bytes 196616 | tf_op jit(solution)/shard_map/ppermute | solution.py:33
  4.8 5.0 %collective-permute-start.1 = (bf16[8,4,8,128]{3,2,1,0:T(8,128)(2,1)S(1)}, bf16[8,4,8,128]{3,2,1,0:T(8,128)(2,1)S(1)}, u32[]{:S(2)}, u32[]{:S(2)}) collective-permute-start(bf16[8,4,8,128]{3,2,1,0:T(8,128)(2,1)S(1)} %bitcast.170), channel_id=1, source_target_pairs={{8,0},{16,8},{24,16},{32,24},{40,32},{48,40},{56,48},{64,56},{72,6... | collective-permute-start | bytes 196616 | tf_op jit(solution)/shard_map/ppermute | solution.py:34
  10.1 5.7 %collective-permute-start.2 = (bf16[24,8,1,128]{3,2,1,0:T(2,128)(2,1)S(1)}, bf16[24,8,1,128]{3,2,1,0:T(2,128)(2,1)S(1)}, u32[]{:S(2)}, u32[]{:S(2)}) collective-permute-start(bf16[24,8,1,128]{3,2,1,0:T(2,128)(2,1)S(1)} %get-tuple-element.17), channel_id=1, source_target_pairs={{0,1},{1,2},{2,3},{4,5},{5,6},{6,7},{8,9},{9,10},{10,11},{12,13},{... | collective-permute-start | bytes 147464 | tf_op jit(solution)/shard_map/ppermute | solution.py:133
  13.6 5.5 %collective-permute-start.3 = (bf16[24,8,1,128]{3,2,1,0:T(2,128)(2,1)S(1)}, bf16[24,8,1,128]{3,2,1,0:T(2,128)(2,1)S(1)}, u32[]{:S(2)}, u32[]{:S(2)}) collective-permute-start(bf16[24,8,1,128]{3,2,1,0:T(2,128)(2,1)S(1)} %get-tuple-element.18), channel_id=1, source_target_pairs={{1,0},{2,1},{3,2},{5,4},{6,5},{7,6},{9,8},{10,9},{11,10},{13,12},{... | collective-permute-start | bytes 147464 | tf_op jit(solution)/shard_map/ppermute | solution.py:133
  22.6 4.3 %collective-permute-start.4 = (bf16[24,8,16,1]{0,2,3,1:T(8,128)(2,1)S(1)}, bf16[24,8,16,1]{0,2,3,1:T(8,128)(2,1)S(1)}, u32[]{:S(2)}, u32[]{:S(2)}) collective-permute-start(bf16[24,8,16,1]{0,2,3,1:T(8,128)(2,1)S(1)} %broadcast_select_fusion.11), channel_id=1, source_target_pairs={{0,4},{4,0},{1,5},{5,1},{2,6},{6,2},{3,7},{7,3},{8,12},{12,8},{9,1... | collective-permute-start | bytes 18440 | tf_op jit(solution)/shard_map/ppermute | solution.py:129
  39.8 7.1 %collective-permute-start.5 = (bf16[22,16,1,128]{3,2,1,0:T(2,128)(2,1)S(1)}, bf16[22,16,1,128]{3,2,1,0:T(2,128)(2,1)S(1)}, u32[]{:S(2)}, u32[]{:S(2)}) collective-permute-start(bf16[22,16,1,128]{3,2,1,0:T(2,128)(2,1)S(1)} %get-tuple-element.9), channel_id=1, source_target_pairs={{0,1},{1,2},{2,3},{4,5},{5,6},{6,7},{8,9},{9,10},{10,11},{12,13},{... | collective-permute-start | bytes 270344 | tf_op jit(solution)/shard_map/ppermute | solution.py:133
  43.4 9.2 %collective-permute-start.6 = (bf16[22,16,1,128]{3,2,1,0:T(2,128)(2,1)S(1)}, bf16[22,16,1,128]{3,2,1,0:T(2,128)(2,1)S(1)}, u32[]{:S(2)}, u32[]{:S(2)}) collective-permute-start(bf16[22,16,1,128]{3,2,1,0:T(2,128)(2,1)S(1)} %get-tuple-element.10), channel_id=1, source_target_pairs={{1,0},{2,1},{3,2},{5,4},{6,5},{7,6},{9,8},{10,9},{11,10},{13,12},{... | collective-permute-start | bytes 270344 | tf_op jit(solution)/shard_map/ppermute | solution.py:133
  56.8 2.4 %collective-permute-start.7 = (bf16[22,16,16,1]{0,2,3,1:T(8,128)(2,1)S(1)}, bf16[22,16,16,1]{0,2,3,1:T(8,128)(2,1)S(1)}, u32[]{:S(2)}, u32[]{:S(2)}) collective-permute-start(bf16[22,16,16,1]{0,2,3,1:T(8,128)(2,1)S(1)} %copy.151), channel_id=1, source_target_pairs={{0,4},{4,0},{1,5},{5,1},{2,6},{6,2},{3,7},{7,3},{8,12},{12,8},{9,1... | collective-permute-start | bytes 33800 | tf_op jit(solution)/shard_map/ppermute | solution.py:129
  82.8 3.6 %collective-permute-start.8 = (bf16[64,10,4,1]{0,3,2,1:T(2,128)(2,1)S(1)}, bf16[64,10,4,1]{0,3,2,1:T(2,128)(2,1)S(1)}, u32[]{:S(2)}, u32[]{:S(2)}) collective-permute-start(bf16[64,10,4,1]{0,3,2,1:T(2,128)(2,1)S(1)} %broadcast_select_fusion.8), channel_id=1, source_target_pairs={{0,4},{4,0},{1,5},{5,1},{2,6},{6,2},{3,7},{7,3},{8,12},{12,8},{9,1... | collective-permute-start | bytes 15368 | tf_op jit(solution)/shard_map/ppermute | solution.py:27
  86.7 8.0 %collective-permute-start.10 = (bf16[64,10,1,66]{0,3,2,1:T(8,128)(2,1)S(1)}, bf16[64,10,1,66]{0,3,2,1:T(8,128)(2,1)S(1)}, u32[]{:S(2)}, u32[]{:S(2)}) collective-permute-start(bf16[64,10,1,66]{0,3,2,1:T(8,128)(2,1)S(1)} %get-tuple-element.12), channel_id=1, source_target_pairs={{1,0},{2,1},{3,2},{5,4},{6,5},{7,6},{9,8},{10,9},{11,10},{13,12},{... | collective-permute-start | bytes 253448 | tf_op jit(solution)/shard_map/ppermute | solution.py:34
  88.0 7.6 %collective-permute-start.9 = (bf16[64,10,1,66]{0,3,2,1:T(8,128)(2,1)S(1)}, bf16[64,10,1,66]{0,3,2,1:T(8,128)(2,1)S(1)}, u32[]{:S(2)}, u32[]{:S(2)}) collective-permute-start(bf16[64,10,1,66]{0,3,2,1:T(8,128)(2,1)S(1)} %get-tuple-element.11), channel_id=1, source_target_pairs={{0,1},{1,2},{2,3},{4,5},{5,6},{6,7},{8,9},{9,10},{10,11},{12,13},{... | collective-permute-start | bytes 253448 | tf_op jit(solution)/shard_map/ppermute | solution.py:33
  107.3 38.9 %copy-start.11 = (bf16[256,256]{1,0:T(8,128)(2,1)S(1)}, bf16[256,256]{1,0:T(8,128)(2,1)}, u32[]{:S(2)}) copy-start(bf16[256,256]{1,0:T(8,128)(2,1)} %param.21) | copy-start | bytes 393220
  107.4 39.5 %copy-start.12 = (bf16[256,256]{1,0:T(8,128)(2,1)S(1)}, bf16[256,256]{1,0:T(8,128)(2,1)}, u32[]{:S(2)}) copy-start(bf16[256,256]{1,0:T(8,128)(2,1)} %param.23) | copy-start | bytes 393220
  147.3 5.7 %copy-start.7 = (bf16[8,16384]{1,0:T(8,128)(2,1)S(1)}, bf16[8,16384]{1,0:T(8,128)(2,1)}, u32[]{:S(2)}) copy-start(bf16[8,16384]{1,0:T(8,128)(2,1)} %param.25) | copy-start | bytes 786436
  149.1 15.3 %all-to-all-start.1 = ((bf16[256,128,2]{0,2,1:T(2,128)(2,1)}), bf16[256,128,2]{0,2,1:T(2,128)(2,1)S(1)}, u32[]{:S(2)}, u32[]{:S(2)}) async-start(bf16[256,128,2]{0,2,1:T(2,128)(2,1)} %bitcast.33), calls=%async_computation.1 | async-start | bytes 262144 | tf_op jit(solution)/shard_map/all_to_all | solution.py:328
  168.8 5.8 %collective-permute-start.11 = (bf16[64,8,4,1]{3,0,2,1:T(8,128)(2,1)S(1)}, bf16[64,8,4,1]{3,0,2,1:T(8,128)(2,1)S(1)}, u32[]{:S(2)}, u32[]{:S(2)}) collective-permute-start(bf16[64,8,4,1]{3,0,2,1:T(8,128)(2,1)S(1)} %slice_select_fusion.2), channel_id=1, source_target_pairs={{0,4},{4,0},{1,5},{5,1},{2,6},{6,2},{3,7},{7,3},{8,12},{12,8},{9,1... | collective-permute-start | bytes 12296 | tf_op jit(solution)/shard_map/ppermute | solution.py:27
  174.9 7.1 %collective-permute-start.12 = (bf16[64,8,1,66]{3,0,2,1:T(8,128)(2,1)S(1)}, bf16[64,8,1,66]{3,0,2,1:T(8,128)(2,1)S(1)}, u32[]{:S(2)}, u32[]{:S(2)}) collective-permute-start(bf16[64,8,1,66]{3,0,2,1:T(8,128)(2,1)S(1)} %get-tuple-element.5), channel_id=1, source_target_pairs={{0,1},{1,2},{2,3},{4,5},{5,6},{6,7},{8,9},{9,10},{10,11},{12,13},{... | collective-permute-start | bytes 202760 | tf_op jit(solution)/shard_map/ppermute | solution.py:33
  179.8 5.7 %collective-permute-start.13 = (bf16[64,8,1,66]{3,0,2,1:T(8,128)(2,1)S(1)}, bf16[64,8,1,66]{3,0,2,1:T(8,128)(2,1)S(1)}, u32[]{:S(2)}, u32[]{:S(2)}) collective-permute-start(bf16[64,8,1,66]{3,0,2,1:T(8,128)(2,1)S(1)} %get-tuple-element.6), channel_id=1, source_target_pairs={{1,0},{2,1},{3,2},{5,4},{6,5},{7,6},{9,8},{10,9},{11,10},{13,12},{... | collective-permute-start | bytes 202760 | tf_op jit(solution)/shard_map/ppermute | solution.py:34
  187.2 6.5 %copy-start.13 = (bf16[64,16,2,2,2]{0,4,3,2,1:T(2,128)(2,1)S(1)}, bf16[64,16,2,2,2]{0,4,3,2,1:T(2,128)(2,1)}, u32[]{:S(2)}) copy-start(bf16[64,16,2,2,2]{0,4,3,2,1:T(2,128)(2,1)} %param.27) | copy-start | bytes 49156
  206.3 3.4 %collective-permute-start.14 = (bf16[10,16,1,128]{3,2,1,0:T(2,128)(2,1)S(1)}, bf16[10,16,1,128]{3,2,1,0:T(2,128)(2,1)S(1)}, u32[]{:S(2)}, u32[]{:S(2)}) collective-permute-start(bf16[10,16,1,128]{3,2,1,0:T(2,128)(2,1)S(1)} %get-tuple-element.15), channel_id=1, source_target_pairs={{0,1},{1,2},{2,3},{4,5},{5,6},{6,7},{8,9},{9,10},{10,11},{12,13},{... | collective-permute-start | bytes 122888 | tf_op jit(solution)/shard_map/ppermute | solution.py:133
  208.2 5.2 %collective-permute-start.15 = (bf16[10,16,1,128]{3,2,1,0:T(2,128)(2,1)S(1)}, bf16[10,16,1,128]{3,2,1,0:T(2,128)(2,1)S(1)}, u32[]{:S(2)}, u32[]{:S(2)}) collective-permute-start(bf16[10,16,1,128]{3,2,1,0:T(2,128)(2,1)S(1)} %get-tuple-element.16), channel_id=1, source_target_pairs={{1,0},{2,1},{3,2},{5,4},{6,5},{7,6},{9,8},{10,9},{11,10},{13,12},{... | collective-permute-start | bytes 122888 | tf_op jit(solution)/shard_map/ppermute | solution.py:133
  213.9 5.8 %copy-start.3 = (bf16[10,16,16,128]{3,2,1,0:T(8,128)(2,1)}, bf16[10,16,16,128]{3,2,1,0:T(8,128)(2,1)S(1)}, u32[]{:S(2)}) copy-start(bf16[10,16,16,128]{3,2,1,0:T(8,128)(2,1)S(1)} %maximum_maximum_fusion.2) | copy-start | bytes 1966084
  215.2 4.4 %collective-permute-start.16 = (bf16[10,16,16,1]{2,1,3,0:T(8,128)(2,1)S(1)}, bf16[10,16,16,1]{2,1,3,0:T(8,128)(2,1)S(1)}, u32[]{:S(2)}, u32[]{:S(2)}) collective-permute-start(bf16[10,16,16,1]{2,1,3,0:T(8,128)(2,1)S(1)} %copy.180), channel_id=1, source_target_pairs={{0,4},{4,0},{1,5},{5,1},{2,6},{6,2},{3,7},{7,3},{8,12},{12,8},{9,1... | collective-permute-start | bytes 15368 | tf_op jit(solution)/shard_map/ppermute | solution.py:129
  (10 other events, 24.8 us)

commit v8 on v6

--- a/solution.py
+++ b/solution.py
@@ -75,14 +75,16 @@
     offset = place - (r & (sv - 1))
     for a in range(3):
         for c in range(3):
-            band = jnp.zeros((cout * sv, depth), jnp.float32)
-            for b in range(3):
+
+            def add_tap(b, band):
                 tap = w_ref[(a * 3 + b) * 3 + c]
                 grown = jnp.dot(widen_rows, tap, preferred_element_type=jnp.float32)
                 grown = jnp.dot(
                     grown.astype(jnp.bfloat16), widen_cols, preferred_element_type=jnp.float32
                 )
-                band = band + jnp.where(offset == b, grown, 0.0)
+                return band + jnp.where(offset == b, grown, 0.0)
+
+            band = lax.fori_loop(0, 3, add_tap, jnp.zeros((cout * sv, depth), jnp.float32))
             band_ref[:, pl.ds((a * 3 + c) * depth, depth)] = band.astype(jnp.bfloat16)
 
     lane = lax.broadcasted_iota(jnp.int32, (depth, ss), 1)

time: 218 us -> 235 us (1.078)
  Pallas kernels: 42.6 us -> 58.8 us
    pallas_call x3, Pallas kernels: 30.5 us -> 46.7 us  [fine_conv(): pl.pallas_call(kernel, out_shape=out_shape, scratch_shapes=[pltpu.VMEM((c...]
  transfers between devices with their start and end apart: 18 -> 18, of which waited for: 13 -> 13; matrix products, arithmetic and copies ran while one was open for 4% -> 3% of each run, Pallas kernels for 0% -> 0%
where the time goes in v8:
time: 235 us; the launch traced here: 234 us
  Pallas kernels  58.8 us (25%)
  starting transfers between devices  46.5 us (20%)
  local copies, waits for them, and re-layouts  43.1 us (18%)
  waiting for transfers between devices  38.6 us (16%)
  blocking collectives  27.9 us (12%)
  other arithmetic  9.91 us (4%)
  matrix products  8.21 us (3%)
    pallas_call x3, Pallas kernels, fine_conv(): pl.pallas_call(kernel, out_shape=out_shape, scratch_shapes=[pltpu.VMEM((c...  46.7 us
    all_to_all x1, blocking collectives, on_device(): rows = lax.all_to_all(flat, 'gx', split_axis=2, concat_axis=1, tiled=True)  27.9 us
    ppermute x3, starting transfers between devices, extended(): low = lax.ppermute(top, axis, forward)  12.8 us
    ppermute x3, waiting for transfers between devices, faces(): lax.ppermute(bottom, axis, backward)  12.8 us
    pallas_call x2, Pallas kernels, mid_conv(): pl.pallas_call(kernel, out_shape=jax.ShapeDtypeStruct((sx, sv, cout, ss),...  12.1 us
    all_to_all x1, waiting for transfers between devices, on_device(): lax.all_to_all(windows, 'gx', split_axis=1, concat_axis=2, tiled=True)  10.8 us
    ppermute x3, waiting for transfers between devices, extended(): high = lax.ppermute(bottom, axis, backward)  9.9 us
    ppermute x3, starting transfers between devices, faces(): lax.ppermute(top, axis, forward)  9.02 us
  transfers between devices with their start and end apart: 18, of which 13 were waited for; matrix products, arithmetic and copies ran while one was open for 3% of the time, Pallas kernels for 0%

profile of v8, /device:TPU:1, one launch (start us, length us, event | category | flops | bytes accessed | tf_op | source)
XLA Modules:
  0.0 233.9 jit_solution(12578958646293525186)
XLA Ops:
  0.9 3.9 %collective-permute-start = (bf16[8,4,8,128]{3,2,1,0:T(8,128)(2,1)S(1)}, bf16[8,4,8,128]{3,2,1,0:T(8,128)(2,1)S(1)}, u32[]{:S(2)}, u32[]{:S(2)}) collective-permute-start(bf16[8,4,8,128]{3,2,1,0:T(8,128)(2,1)S(1)} %bitcast.175), channel_id=1, source_target_pairs={{0,8},{8,16},{16,24},{24,32},{32,40},{40,48},{48,56},{56,64},{64,7... | collective-permute-start | bytes 196616 | tf_op jit(solution)/shard_map/ppermute | solution.py:33
  6.2 3.7 %collective-permute-done.1 = bf16[8,4,8,128]{3,2,1,0:T(8,128)(2,1)S(1)} collective-permute-done((bf16[8,4,8,128]{3,2,1,0:T(8,128)(2,1)S(1)}, bf16[8,4,8,128]{3,2,1,0:T(8,128)(2,1)S(1)}, u32[]{:S(2)}, u32[]{:S(2)}) %collective-permute-start.1) | collective-permute-done | bytes 65568 | tf_op jit(solution)/shard_map/ppermute | solution.py:34
  10.1 3.5 %collective-permute-start.2 = (bf16[24,8,1,128]{3,2,1,0:T(2,128)(2,1)S(1)}, bf16[24,8,1,128]{3,2,1,0:T(2,128)(2,1)S(1)}, u32[]{:S(2)}, u32[]{:S(2)}) collective-permute-start(bf16[24,8,1,128]{3,2,1,0:T(2,128)(2,1)S(1)} %get-tuple-element.17), channel_id=1, source_target_pairs={{0,1},{1,2},{2,3},{4,5},{5,6},{6,7},{8,9},{9,10},{10,11},{12,13},{... | collective-permute-start | bytes 147464 | tf_op jit(solution)/shard_map/ppermute | solution.py:135
  22.6 3.4 %collective-permute-start.4 = (bf16[24,8,16,1]{0,2,3,1:T(8,128)(2,1)S(1)}, bf16[24,8,16,1]{0,2,3,1:T(8,128)(2,1)S(1)}, u32[]{:S(2)}, u32[]{:S(2)}) collective-permute-start(bf16[24,8,16,1]{0,2,3,1:T(8,128)(2,1)S(1)} %broadcast_select_fusion.11), channel_id=1, source_target_pairs={{0,4},{4,0},{1,5},{5,1},{2,6},{6,2},{3,7},{7,3},{8,12},{12,8},{9,1... | collective-permute-start | bytes 18440 | tf_op jit(solution)/shard_map/ppermute | solution.py:131
  27.9 17.1 %shard_map.145 = f32[22,16,8,128]{3,2,1,0:T(8,128)} custom-call(bf16[24,128,128]{2,1,0:T(8,128)(2,1)} %bitcast.166, bf16[24,8,128]{2,1,0:T(8,128)(2,1)} %pad.33.refs_1_, bf16[27,16,8]{2,1,0:T(8,128)(2,1)} %bitcast.174), custom_call_target="tpu_custom_call" | custom-call | tf_op jit(solution)/shard_map/pallas_call | solution.py:164
  46.7 3.6 %collective-permute-start.5 = (bf16[22,16,1,128]{3,2,1,0:T(2,128)(2,1)S(1)}, bf16[22,16,1,128]{3,2,1,0:T(2,128)(2,1)S(1)}, u32[]{:S(2)}, u32[]{:S(2)}) collective-permute-start(bf16[22,16,1,128]{3,2,1,0:T(2,128)(2,1)S(1)} %get-tuple-element.9), channel_id=1, source_target_pairs={{0,1},{1,2},{2,3},{4,5},{5,6},{6,7},{8,9},{9,10},{10,11},{12,13},{... | collective-permute-start | bytes 270344 | tf_op jit(solution)/shard_map/ppermute | solution.py:135
  53.9 5.7 %collective-permute-done.6 = bf16[22,16,1,128]{3,2,1,0:T(2,128)(2,1)S(1)} collective-permute-done((bf16[22,16,1,128]{3,2,1,0:T(2,128)(2,1)S(1)}, bf16[22,16,1,128]{3,2,1,0:T(2,128)(2,1)S(1)}, u32[]{:S(2)}, u32[]{:S(2)}) %collective-permute-start.6) | collective-permute-done | bytes 90144 | tf_op jit(solution)/shard_map/ppermute | solution.py:135
  67.4 17.1 %shard_map.146 = f32[20,16,8,128]{3,2,1,0:T(8,128)} custom-call(bf16[22,256,128]{2,1,0:T(8,128)(2,1)} %bitcast.165, bf16[22,8,256]{2,1,0:T(8,128)(2,1)} %pad.35.refs_1_, bf16[27,16,16]{2,1,0:T(8,128)(2,1)} %bitcast.180), custom_call_target="tpu_custom_call" | custom-call | tf_op jit(solution)/shard_map/pallas_call | solution.py:164
  86.0 3.5 %copy.161 = bf16[20,16,8,128]{1,3,2,0:T(8,128)(2,1)} copy(bf16[20,16,8,128]{3,2,1,0:T(8,128)(2,1)S(1)} %convert_select_fusion.1) | data formatting | bytes 1310720 | tf_op jit(solution)/shard_map/jit(_where)/select_n | solution.py:46
  89.6 3.8 %multiply_convert_fusion = bf16[64,10,4,64]{0,3,2,1:T(8,128)(2,1)S(1)} fusion(bf16[10,2,16,4,2,64,2]{2,6,5,4,3,1,0:T(2,128)(2,1)} %bitcast.168, bf16[64,16,2,2,2,1,1]{0,4,3,2,1,6,5:T(2,128)(2,1)S(1)} %bitcast.183), kind=kOutput, calls=%fused_computation.8 | convolution fusion | flops 42762240 | bytes 999424 | tf_op jit(solution)/shard_map/xaivbsc,oiabc->oxvs/dot_general | solution.py:244
  98.6 4.0 %collective-permute-start.9 = (bf16[64,10,1,66]{0,3,2,1:T(8,128)(2,1)S(1)}, bf16[64,10,1,66]{0,3,2,1:T(8,128)(2,1)S(1)}, u32[]{:S(2)}, u32[]{:S(2)}) collective-permute-start(bf16[64,10,1,66]{0,3,2,1:T(8,128)(2,1)S(1)} %get-tuple-element.11), channel_id=1, source_target_pairs={{0,1},{1,2},{2,3},{4,5},{5,6},{6,7},{8,9},{9,10},{10,11},{12,13},{... | collective-permute-start | bytes 253448 | tf_op jit(solution)/shard_map/ppermute | solution.py:33
  108.5 6.5 %shard_map.147 = f32[8,4,64,64]{3,2,1,0:T(8,128)} custom-call(bf16[10,64,512]{2,1,0:T(8,128)(2,1)} %pad.36.refs_0_, bf16[64,1728]{1,0:T(8,128)(2,1)} %reshape.153.refs_1_), custom_call_target="tpu_custom_call" | custom-call | tf_op jit(solution)/shard_map/pallas_call | solution.py:222
  118.1 27.9 %all_to_all.24 = bf16[256,2,64]{0,1,2:T(2,128)(2,1)S(1)} all-to-all(bf16[256,2,64]{0,1,2:T(2,128)(2,1)S(1)} %copy.167), channel_id=1, replica_groups=mesh['gx'=32,'gy'=2,'gz'=4] {'gx'}, dimensions={2} | all-to-all | bytes 131072 | tf_op jit(solution)/shard_map/all_to_all | solution.py:319
  149.8 4.1 %all-to-all-start.1 = ((bf16[256,128,2]{0,2,1:T(2,128)(2,1)}), bf16[256,128,2]{0,2,1:T(2,128)(2,1)S(1)}, u32[]{:S(2)}, u32[]{:S(2)}) async-start(bf16[256,128,2]{0,2,1:T(2,128)(2,1)} %bitcast.33), calls=%async_computation.1 | async-start | bytes 262144 | tf_op jit(solution)/shard_map/all_to_all | solution.py:331
  154.4 10.8 %all-to-all-done.1 = bf16[256,128,2]{0,2,1:T(2,128)(2,1)S(1)} async-done(((bf16[256,128,2]{0,2,1:T(2,128)(2,1)}), bf16[256,128,2]{0,2,1:T(2,128)(2,1)S(1)}, u32[]{:S(2)}, u32[]{:S(2)}) %all-to-all-start.1) | async-done | bytes 131104 | tf_op jit(solution)/shard_map/all_to_all | solution.py:331
  169.7 3.9 %collective-permute-start.11 = (bf16[64,8,4,1]{3,0,2,1:T(8,128)(2,1)S(1)}, bf16[64,8,4,1]{3,0,2,1:T(8,128)(2,1)S(1)}, u32[]{:S(2)}, u32[]{:S(2)}) collective-permute-start(bf16[64,8,4,1]{3,0,2,1:T(8,128)(2,1)S(1)} %slice_select_fusion.2), channel_id=1, source_target_pairs={{0,4},{4,0},{1,5},{5,1},{2,6},{6,2},{3,7},{7,3},{8,12},{12,8},{9,1... | collective-permute-start | bytes 12296 | tf_op jit(solution)/shard_map/ppermute | solution.py:27
  175.8 4.9 %collective-permute-start.12 = (bf16[64,8,1,66]{3,0,2,1:T(8,128)(2,1)S(1)}, bf16[64,8,1,66]{3,0,2,1:T(8,128)(2,1)S(1)}, u32[]{:S(2)}, u32[]{:S(2)}) collective-permute-start(bf16[64,8,1,66]{3,0,2,1:T(8,128)(2,1)S(1)} %get-tuple-element.5), channel_id=1, source_target_pairs={{0,1},{1,2},{2,3},{4,5},{5,6},{6,7},{8,9},{9,10},{10,11},{12,13},{... | collective-permute-start | bytes 202760 | tf_op jit(solution)/shard_map/ppermute | solution.py:33
  182.9 3.5 %collective-permute-done.13 = bf16[64,8,1,66]{3,0,2,1:T(8,128)(2,1)S(1)} collective-permute-done((bf16[64,8,1,66]{3,0,2,1:T(8,128)(2,1)S(1)}, bf16[64,8,1,66]{3,0,2,1:T(8,128)(2,1)S(1)}, u32[]{:S(2)}, u32[]{:S(2)}) %collective-permute-start.13) | collective-permute-done | bytes 67616 | tf_op jit(solution)/shard_map/ppermute | solution.py:34
  189.0 5.7 %shard_map.148 = f32[6,4,64,64]{3,2,1,0:T(8,128)} custom-call(bf16[8,64,512]{2,1,0:T(8,128)(2,1)} %pad.38.refs_0_, bf16[64,1728]{1,0:T(8,128)(2,1)} %reshape.167.refs_1_), custom_call_target="tpu_custom_call" | custom-call | tf_op jit(solution)/shard_map/pallas_call | solution.py:222
  196.2 6.4 %copy.184 = f32[6,2,16,4,2,64,2]{2,6,5,4,3,1,0:T(2,128)} copy(f32[6,2,16,4,2,64,2]{5,2,6,4,1,3,0:T(8,128)S(1)} %convolution_bitcast_fusion) | data formatting | bytes 1572864 | tf_op jit(solution)/shard_map/ixvs,ioabc->xaovbsc/transpose | solution.py:248
  202.6 4.4 %copy.185 = f32[12,16,8,128]{3,2,1,0:T(8,128)S(1)} copy(f32[12,16,8,128]{1,3,2,0:T(8,128)} %bitcast.164) | data formatting | bytes 1572864 | tf_op jit(solution)/shard_map/reshape | solution.py:250
  210.5 3.7 %collective-permute-done.15 = bf16[10,16,1,128]{3,2,1,0:T(2,128)(2,1)S(1)} collective-permute-done((bf16[10,16,1,128]{3,2,1,0:T(2,128)(2,1)S(1)}, bf16[10,16,1,128]{3,2,1,0:T(2,128)(2,1)S(1)}, u32[]{:S(2)}, u32[]{:S(2)}) %collective-permute-start.15) | collective-permute-done | bytes 40992 | tf_op jit(solution)/shard_map/ppermute | solution.py:135
  216.0 3.6 %collective-permute-start.16 = (bf16[10,16,16,1]{2,1,3,0:T(8,128)(2,1)S(1)}, bf16[10,16,16,1]{2,1,3,0:T(8,128)(2,1)S(1)}, u32[]{:S(2)}, u32[]{:S(2)}) collective-permute-start(bf16[10,16,16,1]{2,1,3,0:T(8,128)(2,1)S(1)} %copy.186), channel_id=1, source_target_pairs={{0,4},{4,0},{1,5},{5,1},{2,6},{6,2},{3,7},{7,3},{8,12},{12,8},{9,1... | collective-permute-start | bytes 15368 | tf_op jit(solution)/shard_map/ppermute | solution.py:131
  221.3 12.5 %shard_map.149 = f32[4,8,8,128]{3,2,1,0:T(8,128)} custom-call(bf16[10,256,128]{2,1,0:T(8,128)(2,1)} %bitcast.167, bf16[10,8,256]{2,1,0:T(8,128)(2,1)} %pad.39.refs_1_, bf16[27,16,16]{2,1,0:T(8,128)(2,1)} %bitcast.181, bf16[32,128]{1,0:T(8,128)(2,1)} %convert_element_type.137.refs_3_), custom_call_target="tpu_custom_call" | custom-call | tf_op jit(solution)/shard_map/pallas_call | solution.py:164
  (160 shorter events, 65.8 us)
Async XLA Ops:
  0.0 146.5 %copy-start = (bf16[256,256]{1,0:T(8,128)(2,1)S(1)}, bf16[256,256]{1,0:T(8,128)(2,1)}, u32[]{:S(2)}) copy-start(bf16[256,256]{1,0:T(8,128)(2,1)} %param.22) | copy-start | bytes 393220
  0.9 5.3 %collective-permute-start = (bf16[8,4,8,128]{3,2,1,0:T(8,128)(2,1)S(1)}, bf16[8,4,8,128]{3,2,1,0:T(8,128)(2,1)S(1)}, u32[]{:S(2)}, u32[]{:S(2)}) collective-permute-start(bf16[8,4,8,128]{3,2,1,0:T(8,128)(2,1)S(1)} %bitcast.175), channel_id=1, source_target_pairs={{0,8},{8,16},{16,24},{24,32},{32,40},{40,48},{48,56},{56,64},{64,7... | collective-permute-start | bytes 196616 | tf_op jit(solution)/shard_map/ppermute | solution.py:33
  4.8 5.0 %collective-permute-start.1 = (bf16[8,4,8,128]{3,2,1,0:T(8,128)(2,1)S(1)}, bf16[8,4,8,128]{3,2,1,0:T(8,128)(2,1)S(1)}, u32[]{:S(2)}, u32[]{:S(2)}) collective-permute-start(bf16[8,4,8,128]{3,2,1,0:T(8,128)(2,1)S(1)} %bitcast.176), channel_id=1, source_target_pairs={{8,0},{16,8},{24,16},{32,24},{40,32},{48,40},{56,48},{64,56},{72,6... | collective-permute-start | bytes 196616 | tf_op jit(solution)/shard_map/ppermute | solution.py:34
  10.1 5.7 %collective-permute-start.2 = (bf16[24,8,1,128]{3,2,1,0:T(2,128)(2,1)S(1)}, bf16[24,8,1,128]{3,2,1,0:T(2,128)(2,1)S(1)}, u32[]{:S(2)}, u32[]{:S(2)}) collective-permute-start(bf16[24,8,1,128]{3,2,1,0:T(2,128)(2,1)S(1)} %get-tuple-element.17), channel_id=1, source_target_pairs={{0,1},{1,2},{2,3},{4,5},{5,6},{6,7},{8,9},{9,10},{10,11},{12,13},{... | collective-permute-start | bytes 147464 | tf_op jit(solution)/shard_map/ppermute | solution.py:135
  13.6 5.5 %collective-permute-start.3 = (bf16[24,8,1,128]{3,2,1,0:T(2,128)(2,1)S(1)}, bf16[24,8,1,128]{3,2,1,0:T(2,128)(2,1)S(1)}, u32[]{:S(2)}, u32[]{:S(2)}) collective-permute-start(bf16[24,8,1,128]{3,2,1,0:T(2,128)(2,1)S(1)} %get-tuple-element.18), channel_id=1, source_target_pairs={{1,0},{2,1},{3,2},{5,4},{6,5},{7,6},{9,8},{10,9},{11,10},{13,12},{... | collective-permute-start | bytes 147464 | tf_op jit(solution)/shard_map/ppermute | solution.py:135
  22.6 4.3 %collective-permute-start.4 = (bf16[24,8,16,1]{0,2,3,1:T(8,128)(2,1)S(1)}, bf16[24,8,16,1]{0,2,3,1:T(8,128)(2,1)S(1)}, u32[]{:S(2)}, u32[]{:S(2)}) collective-permute-start(bf16[24,8,16,1]{0,2,3,1:T(8,128)(2,1)S(1)} %broadcast_select_fusion.11), channel_id=1, source_target_pairs={{0,4},{4,0},{1,5},{5,1},{2,6},{6,2},{3,7},{7,3},{8,12},{12,8},{9,1... | collective-permute-start | bytes 18440 | tf_op jit(solution)/shard_map/ppermute | solution.py:131
  46.7 7.1 %collective-permute-start.5 = (bf16[22,16,1,128]{3,2,1,0:T(2,128)(2,1)S(1)}, bf16[22,16,1,128]{3,2,1,0:T(2,128)(2,1)S(1)}, u32[]{:S(2)}, u32[]{:S(2)}) collective-permute-start(bf16[22,16,1,128]{3,2,1,0:T(2,128)(2,1)S(1)} %get-tuple-element.9), channel_id=1, source_target_pairs={{0,1},{1,2},{2,3},{4,5},{5,6},{6,7},{8,9},{9,10},{10,11},{12,13},{... | collective-permute-start | bytes 270344 | tf_op jit(solution)/shard_map/ppermute | solution.py:135
  50.3 9.2 %collective-permute-start.6 = (bf16[22,16,1,128]{3,2,1,0:T(2,128)(2,1)S(1)}, bf16[22,16,1,128]{3,2,1,0:T(2,128)(2,1)S(1)}, u32[]{:S(2)}, u32[]{:S(2)}) collective-permute-start(bf16[22,16,1,128]{3,2,1,0:T(2,128)(2,1)S(1)} %get-tuple-element.10), channel_id=1, source_target_pairs={{1,0},{2,1},{3,2},{5,4},{6,5},{7,6},{9,8},{10,9},{11,10},{13,12},{... | collective-permute-start | bytes 270344 | tf_op jit(solution)/shard_map/ppermute | solution.py:135
  63.7 2.3 collective-permute-start.7
  93.5 3.6 %collective-permute-start.8 = (bf16[64,10,4,1]{0,3,2,1:T(2,128)(2,1)S(1)}, bf16[64,10,4,1]{0,3,2,1:T(2,128)(2,1)S(1)}, u32[]{:S(2)}, u32[]{:S(2)}) collective-permute-start(bf16[64,10,4,1]{0,3,2,1:T(2,128)(2,1)S(1)} %broadcast_select_fusion.8), channel_id=1, source_target_pairs={{0,4},{4,0},{1,5},{5,1},{2,6},{6,2},{3,7},{7,3},{8,12},{12,8},{9,1... | collective-permute-start | bytes 15368 | tf_op jit(solution)/shard_map/ppermute | solution.py:27
  97.3 8.0 %collective-permute-start.10 = (bf16[64,10,1,66]{0,3,2,1:T(8,128)(2,1)S(1)}, bf16[64,10,1,66]{0,3,2,1:T(8,128)(2,1)S(1)}, u32[]{:S(2)}, u32[]{:S(2)}) collective-permute-start(bf16[64,10,1,66]{0,3,2,1:T(8,128)(2,1)S(1)} %get-tuple-element.12), channel_id=1, source_target_pairs={{1,0},{2,1},{3,2},{5,4},{6,5},{7,6},{9,8},{10,9},{11,10},{13,12},{... | collective-permute-start | bytes 253448 | tf_op jit(solution)/shard_map/ppermute | solution.py:34
  98.6 7.6 %collective-permute-start.9 = (bf16[64,10,1,66]{0,3,2,1:T(8,128)(2,1)S(1)}, bf16[64,10,1,66]{0,3,2,1:T(8,128)(2,1)S(1)}, u32[]{:S(2)}, u32[]{:S(2)}) collective-permute-start(bf16[64,10,1,66]{0,3,2,1:T(8,128)(2,1)S(1)} %get-tuple-element.11), channel_id=1, source_target_pairs={{0,1},{1,2},{2,3},{4,5},{5,6},{6,7},{8,9},{9,10},{10,11},{12,13},{... | collective-permute-start | bytes 253448 | tf_op jit(solution)/shard_map/ppermute | solution.py:33
  117.9 28.9 %copy-start.11 = (bf16[256,256]{1,0:T(8,128)(2,1)S(1)}, bf16[256,256]{1,0:T(8,128)(2,1)}, u32[]{:S(2)}) copy-start(bf16[256,256]{1,0:T(8,128)(2,1)} %param.21) | copy-start | bytes 393220
  118.1 29.5 %copy-start.12 = (bf16[256,256]{1,0:T(8,128)(2,1)S(1)}, bf16[256,256]{1,0:T(8,128)(2,1)}, u32[]{:S(2)}) copy-start(bf16[256,256]{1,0:T(8,128)(2,1)} %param.23) | copy-start | bytes 393220
  148.0 5.9 %copy-start.7 = (bf16[8,16384]{1,0:T(8,128)(2,1)S(1)}, bf16[8,16384]{1,0:T(8,128)(2,1)}, u32[]{:S(2)}) copy-start(bf16[8,16384]{1,0:T(8,128)(2,1)} %param.25) | copy-start | bytes 786436
  149.8 15.5 %all-to-all-start.1 = ((bf16[256,128,2]{0,2,1:T(2,128)(2,1)}), bf16[256,128,2]{0,2,1:T(2,128)(2,1)S(1)}, u32[]{:S(2)}, u32[]{:S(2)}) async-start(bf16[256,128,2]{0,2,1:T(2,128)(2,1)} %bitcast.33), calls=%async_computation.1 | async-start | bytes 262144 | tf_op jit(solution)/shard_map/all_to_all | solution.py:331
  169.7 5.8 %collective-permute-start.11 = (bf16[64,8,4,1]{3,0,2,1:T(8,128)(2,1)S(1)}, bf16[64,8,4,1]{3,0,2,1:T(8,128)(2,1)S(1)}, u32[]{:S(2)}, u32[]{:S(2)}) collective-permute-start(bf16[64,8,4,1]{3,0,2,1:T(8,128)(2,1)S(1)} %slice_select_fusion.2), channel_id=1, source_target_pairs={{0,4},{4,0},{1,5},{5,1},{2,6},{6,2},{3,7},{7,3},{8,12},{12,8},{9,1... | collective-permute-start | bytes 12296 | tf_op jit(solution)/shard_map/ppermute | solution.py:27
  175.8 7.1 %collective-permute-start.12 = (bf16[64,8,1,66]{3,0,2,1:T(8,128)(2,1)S(1)}, bf16[64,8,1,66]{3,0,2,1:T(8,128)(2,1)S(1)}, u32[]{:S(2)}, u32[]{:S(2)}) collective-permute-start(bf16[64,8,1,66]{3,0,2,1:T(8,128)(2,1)S(1)} %get-tuple-element.5), channel_id=1, source_target_pairs={{0,1},{1,2},{2,3},{4,5},{5,6},{6,7},{8,9},{9,10},{10,11},{12,13},{... | collective-permute-start | bytes 202760 | tf_op jit(solution)/shard_map/ppermute | solution.py:33
  180.7 5.7 %collective-permute-start.13 = (bf16[64,8,1,66]{3,0,2,1:T(8,128)(2,1)S(1)}, bf16[64,8,1,66]{3,0,2,1:T(8,128)(2,1)S(1)}, u32[]{:S(2)}, u32[]{:S(2)}) collective-permute-start(bf16[64,8,1,66]{3,0,2,1:T(8,128)(2,1)S(1)} %get-tuple-element.6), channel_id=1, source_target_pairs={{1,0},{2,1},{3,2},{5,4},{6,5},{7,6},{9,8},{10,9},{11,10},{13,12},{... | collective-permute-start | bytes 202760 | tf_op jit(solution)/shard_map/ppermute | solution.py:34
  188.1 6.5 %copy-start.13 = (bf16[64,16,2,2,2]{0,4,3,2,1:T(2,128)(2,1)S(1)}, bf16[64,16,2,2,2]{0,4,3,2,1:T(2,128)(2,1)}, u32[]{:S(2)}) copy-start(bf16[64,16,2,2,2]{0,4,3,2,1:T(2,128)(2,1)} %param.27) | copy-start | bytes 49156
  207.2 3.4 %collective-permute-start.14 = (bf16[10,16,1,128]{3,2,1,0:T(2,128)(2,1)S(1)}, bf16[10,16,1,128]{3,2,1,0:T(2,128)(2,1)S(1)}, u32[]{:S(2)}, u32[]{:S(2)}) collective-permute-start(bf16[10,16,1,128]{3,2,1,0:T(2,128)(2,1)S(1)} %get-tuple-element.15), channel_id=1, source_target_pairs={{0,1},{1,2},{2,3},{4,5},{5,6},{6,7},{8,9},{9,10},{10,11},{12,13},{... | collective-permute-start | bytes 122888 | tf_op jit(solution)/shard_map/ppermute | solution.py:135
  209.1 5.2 %collective-permute-start.15 = (bf16[10,16,1,128]{3,2,1,0:T(2,128)(2,1)S(1)}, bf16[10,16,1,128]{3,2,1,0:T(2,128)(2,1)S(1)}, u32[]{:S(2)}, u32[]{:S(2)}) collective-permute-start(bf16[10,16,1,128]{3,2,1,0:T(2,128)(2,1)S(1)} %get-tuple-element.16), channel_id=1, source_target_pairs={{1,0},{2,1},{3,2},{5,4},{6,5},{7,6},{9,8},{10,9},{11,10},{13,12},{... | collective-permute-start | bytes 122888 | tf_op jit(solution)/shard_map/ppermute | solution.py:135
  214.8 5.8 %copy-start.3 = (bf16[10,16,16,128]{3,2,1,0:T(8,128)(2,1)}, bf16[10,16,16,128]{3,2,1,0:T(8,128)(2,1)S(1)}, u32[]{:S(2)}) copy-start(bf16[10,16,16,128]{3,2,1,0:T(8,128)(2,1)S(1)} %maximum_maximum_fusion.2) | copy-start | bytes 1966084
  216.0 4.5 %collective-permute-start.16 = (bf16[10,16,16,1]{2,1,3,0:T(8,128)(2,1)S(1)}, bf16[10,16,16,1]{2,1,3,0:T(8,128)(2,1)S(1)}, u32[]{:S(2)}, u32[]{:S(2)}) collective-permute-start(bf16[10,16,16,1]{2,1,3,0:T(8,128)(2,1)S(1)} %copy.186), channel_id=1, source_target_pairs={{0,4},{4,0},{1,5},{5,1},{2,6},{6,2},{3,7},{7,3},{8,12},{12,8},{9,1... | collective-permute-start | bytes 15368 | tf_op jit(solution)/shard_map/ppermute | solution.py:131
  (10 other events, 24.8 us)

commit v9 on v6

--- a/solution.py
+++ b/solution.py
@@ -185,7 +185,7 @@
     lax.fori_loop(0, sx + 2, shift, 0)
     chans = shifted_ref.shape[2]
 
-    group = 4 if sx % 4 == 0 else 2
+    group = sx if sx <= 8 else (4 if sx % 4 == 0 else 2)
 
     def rows_pair(g, carry):
         x = group * g

time: 218 us -> 218 us (level)
  transfers between devices with their start and end apart: 18 -> 18, of which waited for: 13 -> 12; matrix products, arithmetic and copies ran while one was open for 4% -> 4% of each run, Pallas kernels for 0% -> 0%
where the time goes in v9:
time: 218 us; the launch traced here: 217 us
  starting transfers between devices  46.5 us (21%)
  local copies, waits for them, and re-layouts  43.1 us (20%)
  Pallas kernels  41.9 us (19%)
  waiting for transfers between devices  38.4 us (18%)
  blocking collectives  27.8 us (13%)
  other arithmetic  9.91 us (5%)
  matrix products  8.21 us (4%)
    pallas_call x3, Pallas kernels, fine_conv(): pl.pallas_call(kernel, out_shape=out_shape, scratch_shapes=[pltpu.VMEM((c...  30.5 us
    all_to_all x1, blocking collectives, on_device(): rows = lax.all_to_all(flat, 'gx', split_axis=2, concat_axis=1, tiled=True)  27.8 us
    ppermute x3, starting transfers between devices, extended(): low = lax.ppermute(top, axis, forward)  12.8 us
    ppermute x3, waiting for transfers between devices, faces(): lax.ppermute(bottom, axis, backward)  12.6 us
    pallas_call x2, Pallas kernels, mid_conv(): pl.pallas_call(kernel, out_shape=jax.ShapeDtypeStruct((sx, sv, cout, ss),...  11.4 us
    all_to_all x1, waiting for transfers between devices, on_device(): lax.all_to_all(windows, 'gx', split_axis=1, concat_axis=2, tiled=True)  10.8 us
    ppermute x3, waiting for transfers between devices, extended(): high = lax.ppermute(bottom, axis, backward)  9.9 us
    ppermute x3, starting transfers between devices, faces(): lax.ppermute(top, axis, forward)  9.32 us
  transfers between devices with their start and end apart: 18, of which 12 were waited for; matrix products, arithmetic and copies ran while one was open for 4% of the time, Pallas kernels for 0%

profile of v9, /device:TPU:1, one launch (start us, length us, event | category | flops | bytes accessed | tf_op | source)
XLA Modules:
  0.0 216.7 jit_solution(15499599751371548753)
XLA Ops:
  0.9 3.9 %collective-permute-start = (bf16[8,4,8,128]{3,2,1,0:T(8,128)(2,1)S(1)}, bf16[8,4,8,128]{3,2,1,0:T(8,128)(2,1)S(1)}, u32[]{:S(2)}, u32[]{:S(2)}) collective-permute-start(bf16[8,4,8,128]{3,2,1,0:T(8,128)(2,1)S(1)} %bitcast.175), channel_id=1, source_target_pairs={{0,8},{8,16},{16,24},{24,32},{32,40},{40,48},{48,56},{56,64},{64,7... | collective-permute-start | bytes 196616 | tf_op jit(solution)/shard_map/ppermute | solution.py:33
  6.2 3.7 %collective-permute-done.1 = bf16[8,4,8,128]{3,2,1,0:T(8,128)(2,1)S(1)} collective-permute-done((bf16[8,4,8,128]{3,2,1,0:T(8,128)(2,1)S(1)}, bf16[8,4,8,128]{3,2,1,0:T(8,128)(2,1)S(1)}, u32[]{:S(2)}, u32[]{:S(2)}) %collective-permute-start.1) | collective-permute-done | bytes 65568 | tf_op jit(solution)/shard_map/ppermute | solution.py:34
  10.1 3.5 %collective-permute-start.2 = (bf16[24,8,1,128]{3,2,1,0:T(2,128)(2,1)S(1)}, bf16[24,8,1,128]{3,2,1,0:T(2,128)(2,1)S(1)}, u32[]{:S(2)}, u32[]{:S(2)}) collective-permute-start(bf16[24,8,1,128]{3,2,1,0:T(2,128)(2,1)S(1)} %get-tuple-element.17), channel_id=1, source_target_pairs={{0,1},{1,2},{2,3},{4,5},{5,6},{6,7},{8,9},{9,10},{10,11},{12,13},{... | collective-permute-start | bytes 147464 | tf_op jit(solution)/shard_map/ppermute | solution.py:133
  15.8 3.4 %collective-permute-done.3 = bf16[24,8,1,128]{3,2,1,0:T(2,128)(2,1)S(1)} collective-permute-done((bf16[24,8,1,128]{3,2,1,0:T(2,128)(2,1)S(1)}, bf16[24,8,1,128]{3,2,1,0:T(2,128)(2,1)S(1)}, u32[]{:S(2)}, u32[]{:S(2)}) %collective-permute-start.3) | collective-permute-done | bytes 49184 | tf_op jit(solution)/shard_map/ppermute | solution.py:133
  22.6 3.4 %collective-permute-start.4 = (bf16[24,8,16,1]{0,2,3,1:T(8,128)(2,1)S(1)}, bf16[24,8,16,1]{0,2,3,1:T(8,128)(2,1)S(1)}, u32[]{:S(2)}, u32[]{:S(2)}) collective-permute-start(bf16[24,8,16,1]{0,2,3,1:T(8,128)(2,1)S(1)} %broadcast_select_fusion.11), channel_id=1, source_target_pairs={{0,4},{4,0},{1,5},{5,1},{2,6},{6,2},{3,7},{7,3},{8,12},{12,8},{9,1... | collective-permute-start | bytes 18440 | tf_op jit(solution)/shard_map/ppermute | solution.py:129
  27.9 11.0 %shard_map.145 = f32[22,16,8,128]{3,2,1,0:T(8,128)} custom-call(bf16[24,128,128]{2,1,0:T(8,128)(2,1)} %bitcast.166, bf16[24,8,128]{2,1,0:T(8,128)(2,1)} %pad.33.refs_1_, bf16[27,16,8]{2,1,0:T(8,128)(2,1)} %bitcast.174), custom_call_target="tpu_custom_call" | custom-call | tf_op jit(solution)/shard_map/pallas_call | solution.py:162
  40.7 3.5 %collective-permute-start.5 = (bf16[22,16,1,128]{3,2,1,0:T(2,128)(2,1)S(1)}, bf16[22,16,1,128]{3,2,1,0:T(2,128)(2,1)S(1)}, u32[]{:S(2)}, u32[]{:S(2)}) collective-permute-start(bf16[22,16,1,128]{3,2,1,0:T(2,128)(2,1)S(1)} %get-tuple-element.9), channel_id=1, source_target_pairs={{0,1},{1,2},{2,3},{4,5},{5,6},{6,7},{8,9},{9,10},{10,11},{12,13},{... | collective-permute-start | bytes 270344 | tf_op jit(solution)/shard_map/ppermute | solution.py:133
  47.8 5.7 %collective-permute-done.6 = bf16[22,16,1,128]{3,2,1,0:T(2,128)(2,1)S(1)} collective-permute-done((bf16[22,16,1,128]{3,2,1,0:T(2,128)(2,1)S(1)}, bf16[22,16,1,128]{3,2,1,0:T(2,128)(2,1)S(1)}, u32[]{:S(2)}, u32[]{:S(2)}) %collective-permute-start.6) | collective-permute-done | bytes 90144 | tf_op jit(solution)/shard_map/ppermute | solution.py:133
  61.3 12.0 %shard_map.146 = f32[20,16,8,128]{3,2,1,0:T(8,128)} custom-call(bf16[22,256,128]{2,1,0:T(8,128)(2,1)} %bitcast.165, bf16[22,8,256]{2,1,0:T(8,128)(2,1)} %pad.35.refs_1_, bf16[27,16,16]{2,1,0:T(8,128)(2,1)} %bitcast.180), custom_call_target="tpu_custom_call" | custom-call | tf_op jit(solution)/shard_map/pallas_call | solution.py:162
  74.9 3.5 %copy.161 = bf16[20,16,8,128]{1,3,2,0:T(8,128)(2,1)} copy(bf16[20,16,8,128]{3,2,1,0:T(8,128)(2,1)S(1)} %convert_select_fusion.1) | data formatting | bytes 1310720 | tf_op jit(solution)/shard_map/jit(_where)/select_n | solution.py:46
  78.4 3.8 %multiply_convert_fusion = bf16[64,10,4,64]{0,3,2,1:T(8,128)(2,1)S(1)} fusion(bf16[10,2,16,4,2,64,2]{2,6,5,4,3,1,0:T(2,128)(2,1)} %bitcast.168, bf16[64,16,2,2,2,1,1]{0,4,3,2,1,6,5:T(2,128)(2,1)S(1)} %bitcast.183), kind=kOutput, calls=%fused_computation.8 | convolution fusion | flops 42762240 | bytes 999424 | tf_op jit(solution)/shard_map/xaivbsc,oiabc->oxvs/dot_general | solution.py:242
  87.5 4.0 %collective-permute-start.9 = (bf16[64,10,1,66]{0,3,2,1:T(8,128)(2,1)S(1)}, bf16[64,10,1,66]{0,3,2,1:T(8,128)(2,1)S(1)}, u32[]{:S(2)}, u32[]{:S(2)}) collective-permute-start(bf16[64,10,1,66]{0,3,2,1:T(8,128)(2,1)S(1)} %get-tuple-element.11), channel_id=1, source_target_pairs={{0,1},{1,2},{2,3},{4,5},{5,6},{6,7},{8,9},{9,10},{10,11},{12,13},{... | collective-permute-start | bytes 253448 | tf_op jit(solution)/shard_map/ppermute | solution.py:33
  97.3 6.3 %shard_map.147 = f32[8,4,64,64]{3,2,1,0:T(8,128)} custom-call(bf16[10,64,512]{2,1,0:T(8,128)(2,1)} %pad.36.refs_0_, bf16[64,1728]{1,0:T(8,128)(2,1)} %reshape.153.refs_1_), custom_call_target="tpu_custom_call" | custom-call | tf_op jit(solution)/shard_map/pallas_call | solution.py:220
  106.7 27.8 %all_to_all.24 = bf16[256,2,64]{0,1,2:T(2,128)(2,1)S(1)} all-to-all(bf16[256,2,64]{0,1,2:T(2,128)(2,1)S(1)} %copy.167), channel_id=1, replica_groups=mesh['gx'=32,'gy'=2,'gz'=4] {'gx'}, dimensions={2} | all-to-all | bytes 131072 | tf_op jit(solution)/shard_map/all_to_all | solution.py:317
  138.4 3.9 %all-to-all-start.1 = ((bf16[256,128,2]{0,2,1:T(2,128)(2,1)}), bf16[256,128,2]{0,2,1:T(2,128)(2,1)S(1)}, u32[]{:S(2)}, u32[]{:S(2)}) async-start(bf16[256,128,2]{0,2,1:T(2,128)(2,1)} %bitcast.33), calls=%async_computation.1 | async-start | bytes 262144 | tf_op jit(solution)/shard_map/all_to_all | solution.py:329
  142.8 10.8 %all-to-all-done.1 = bf16[256,128,2]{0,2,1:T(2,128)(2,1)S(1)} async-done(((bf16[256,128,2]{0,2,1:T(2,128)(2,1)}), bf16[256,128,2]{0,2,1:T(2,128)(2,1)S(1)}, u32[]{:S(2)}, u32[]{:S(2)}) %all-to-all-start.1) | async-done | bytes 131104 | tf_op jit(solution)/shard_map/all_to_all | solution.py:329
  158.1 3.9 %collective-permute-start.11 = (bf16[64,8,4,1]{3,0,2,1:T(8,128)(2,1)S(1)}, bf16[64,8,4,1]{3,0,2,1:T(8,128)(2,1)S(1)}, u32[]{:S(2)}, u32[]{:S(2)}) collective-permute-start(bf16[64,8,4,1]{3,0,2,1:T(8,128)(2,1)S(1)} %slice_select_fusion.2), channel_id=1, source_target_pairs={{0,4},{4,0},{1,5},{5,1},{2,6},{6,2},{3,7},{7,3},{8,12},{12,8},{9,1... | collective-permute-start | bytes 12296 | tf_op jit(solution)/shard_map/ppermute | solution.py:27
  164.2 4.9 %collective-permute-start.12 = (bf16[64,8,1,66]{3,0,2,1:T(8,128)(2,1)S(1)}, bf16[64,8,1,66]{3,0,2,1:T(8,128)(2,1)S(1)}, u32[]{:S(2)}, u32[]{:S(2)}) collective-permute-start(bf16[64,8,1,66]{3,0,2,1:T(8,128)(2,1)S(1)} %get-tuple-element.5), channel_id=1, source_target_pairs={{0,1},{1,2},{2,3},{4,5},{5,6},{6,7},{8,9},{9,10},{10,11},{12,13},{... | collective-permute-start | bytes 202760 | tf_op jit(solution)/shard_map/ppermute | solution.py:33
  171.3 3.5 %collective-permute-done.13 = bf16[64,8,1,66]{3,0,2,1:T(8,128)(2,1)S(1)} collective-permute-done((bf16[64,8,1,66]{3,0,2,1:T(8,128)(2,1)S(1)}, bf16[64,8,1,66]{3,0,2,1:T(8,128)(2,1)S(1)}, u32[]{:S(2)}, u32[]{:S(2)}) %collective-permute-start.13) | collective-permute-done | bytes 67616 | tf_op jit(solution)/shard_map/ppermute | solution.py:34
  177.4 5.2 %shard_map.148 = f32[6,4,64,64]{3,2,1,0:T(8,128)} custom-call(bf16[8,64,512]{2,1,0:T(8,128)(2,1)} %pad.38.refs_0_, bf16[64,1728]{1,0:T(8,128)(2,1)} %reshape.167.refs_1_), custom_call_target="tpu_custom_call" | custom-call | tf_op jit(solution)/shard_map/pallas_call | solution.py:220
  184.1 6.4 %copy.184 = f32[6,2,16,4,2,64,2]{2,6,5,4,3,1,0:T(2,128)} copy(f32[6,2,16,4,2,64,2]{5,2,6,4,1,3,0:T(8,128)S(1)} %convolution_bitcast_fusion) | data formatting | bytes 1572864 | tf_op jit(solution)/shard_map/ixvs,ioabc->xaovbsc/transpose | solution.py:246
  190.5 4.4 %copy.185 = f32[12,16,8,128]{3,2,1,0:T(8,128)S(1)} copy(f32[12,16,8,128]{1,3,2,0:T(8,128)} %bitcast.164) | data formatting | bytes 1572864 | tf_op jit(solution)/shard_map/reshape | solution.py:248
  198.9 3.6 %collective-permute-done.15 = bf16[10,16,1,128]{3,2,1,0:T(2,128)(2,1)S(1)} collective-permute-done((bf16[10,16,1,128]{3,2,1,0:T(2,128)(2,1)S(1)}, bf16[10,16,1,128]{3,2,1,0:T(2,128)(2,1)S(1)}, u32[]{:S(2)}, u32[]{:S(2)}) %collective-permute-start.15) | collective-permute-done | bytes 40992 | tf_op jit(solution)/shard_map/ppermute | solution.py:133
  209.2 7.5 %shard_map.149 = f32[4,8,8,128]{3,2,1,0:T(8,128)} custom-call(bf16[10,256,128]{2,1,0:T(8,128)(2,1)} %bitcast.167, bf16[10,8,256]{2,1,0:T(8,128)(2,1)} %pad.39.refs_1_, bf16[27,16,16]{2,1,0:T(8,128)(2,1)} %bitcast.181, bf16[32,128]{1,0:T(8,128)(2,1)} %convert_element_type.137.refs_3_), custom_call_target="tpu_custom_call" | custom-call | tf_op jit(solution)/shard_map/pallas_call | solution.py:162
  (160 shorter events, 66.2 us)
Async XLA Ops:
  0.0 135.1 %copy-start = (bf16[256,256]{1,0:T(8,128)(2,1)S(1)}, bf16[256,256]{1,0:T(8,128)(2,1)}, u32[]{:S(2)}) copy-start(bf16[256,256]{1,0:T(8,128)(2,1)} %param.22) | copy-start | bytes 393220
  0.9 5.3 %collective-permute-start = (bf16[8,4,8,128]{3,2,1,0:T(8,128)(2,1)S(1)}, bf16[8,4,8,128]{3,2,1,0:T(8,128)(2,1)S(1)}, u32[]{:S(2)}, u32[]{:S(2)}) collective-permute-start(bf16[8,4,8,128]{3,2,1,0:T(8,128)(2,1)S(1)} %bitcast.175), channel_id=1, source_target_pairs={{0,8},{8,16},{16,24},{24,32},{32,40},{40,48},{48,56},{56,64},{64,7... | collective-permute-start | bytes 196616 | tf_op jit(solution)/shard_map/ppermute | solution.py:33
  4.8 5.0 %collective-permute-start.1 = (bf16[8,4,8,128]{3,2,1,0:T(8,128)(2,1)S(1)}, bf16[8,4,8,128]{3,2,1,0:T(8,128)(2,1)S(1)}, u32[]{:S(2)}, u32[]{:S(2)}) collective-permute-start(bf16[8,4,8,128]{3,2,1,0:T(8,128)(2,1)S(1)} %bitcast.176), channel_id=1, source_target_pairs={{8,0},{16,8},{24,16},{32,24},{40,32},{48,40},{56,48},{64,56},{72,6... | collective-permute-start | bytes 196616 | tf_op jit(solution)/shard_map/ppermute | solution.py:34
  10.1 5.7 %collective-permute-start.2 = (bf16[24,8,1,128]{3,2,1,0:T(2,128)(2,1)S(1)}, bf16[24,8,1,128]{3,2,1,0:T(2,128)(2,1)S(1)}, u32[]{:S(2)}, u32[]{:S(2)}) collective-permute-start(bf16[24,8,1,128]{3,2,1,0:T(2,128)(2,1)S(1)} %get-tuple-element.17), channel_id=1, source_target_pairs={{0,1},{1,2},{2,3},{4,5},{5,6},{6,7},{8,9},{9,10},{10,11},{12,13},{... | collective-permute-start | bytes 147464 | tf_op jit(solution)/shard_map/ppermute | solution.py:133
  13.6 5.5 %collective-permute-start.3 = (bf16[24,8,1,128]{3,2,1,0:T(2,128)(2,1)S(1)}, bf16[24,8,1,128]{3,2,1,0:T(2,128)(2,1)S(1)}, u32[]{:S(2)}, u32[]{:S(2)}) collective-permute-start(bf16[24,8,1,128]{3,2,1,0:T(2,128)(2,1)S(1)} %get-tuple-element.18), channel_id=1, source_target_pairs={{1,0},{2,1},{3,2},{5,4},{6,5},{7,6},{9,8},{10,9},{11,10},{13,12},{... | collective-permute-start | bytes 147464 | tf_op jit(solution)/shard_map/ppermute | solution.py:133
  22.6 4.3 %collective-permute-start.4 = (bf16[24,8,16,1]{0,2,3,1:T(8,128)(2,1)S(1)}, bf16[24,8,16,1]{0,2,3,1:T(8,128)(2,1)S(1)}, u32[]{:S(2)}, u32[]{:S(2)}) collective-permute-start(bf16[24,8,16,1]{0,2,3,1:T(8,128)(2,1)S(1)} %broadcast_select_fusion.11), channel_id=1, source_target_pairs={{0,4},{4,0},{1,5},{5,1},{2,6},{6,2},{3,7},{7,3},{8,12},{12,8},{9,1... | collective-permute-start | bytes 18440 | tf_op jit(solution)/shard_map/ppermute | solution.py:129
  40.7 7.1 %collective-permute-start.5 = (bf16[22,16,1,128]{3,2,1,0:T(2,128)(2,1)S(1)}, bf16[22,16,1,128]{3,2,1,0:T(2,128)(2,1)S(1)}, u32[]{:S(2)}, u32[]{:S(2)}) collective-permute-start(bf16[22,16,1,128]{3,2,1,0:T(2,128)(2,1)S(1)} %get-tuple-element.9), channel_id=1, source_target_pairs={{0,1},{1,2},{2,3},{4,5},{5,6},{6,7},{8,9},{9,10},{10,11},{12,13},{... | collective-permute-start | bytes 270344 | tf_op jit(solution)/shard_map/ppermute | solution.py:133
  44.2 9.2 %collective-permute-start.6 = (bf16[22,16,1,128]{3,2,1,0:T(2,128)(2,1)S(1)}, bf16[22,16,1,128]{3,2,1,0:T(2,128)(2,1)S(1)}, u32[]{:S(2)}, u32[]{:S(2)}) collective-permute-start(bf16[22,16,1,128]{3,2,1,0:T(2,128)(2,1)S(1)} %get-tuple-element.10), channel_id=1, source_target_pairs={{1,0},{2,1},{3,2},{5,4},{6,5},{7,6},{9,8},{10,9},{11,10},{13,12},{... | collective-permute-start | bytes 270344 | tf_op jit(solution)/shard_map/ppermute | solution.py:133
  57.7 2.3 %collective-permute-start.7 = (bf16[22,16,16,1]{0,2,3,1:T(8,128)(2,1)S(1)}, bf16[22,16,16,1]{0,2,3,1:T(8,128)(2,1)S(1)}, u32[]{:S(2)}, u32[]{:S(2)}) collective-permute-start(bf16[22,16,16,1]{0,2,3,1:T(8,128)(2,1)S(1)} %copy.157), channel_id=1, source_target_pairs={{0,4},{4,0},{1,5},{5,1},{2,6},{6,2},{3,7},{7,3},{8,12},{12,8},{9,1... | collective-permute-start | bytes 33800 | tf_op jit(solution)/shard_map/ppermute | solution.py:129
  82.3 3.6 %collective-permute-start.8 = (bf16[64,10,4,1]{0,3,2,1:T(2,128)(2,1)S(1)}, bf16[64,10,4,1]{0,3,2,1:T(2,128)(2,1)S(1)}, u32[]{:S(2)}, u32[]{:S(2)}) collective-permute-start(bf16[64,10,4,1]{0,3,2,1:T(2,128)(2,1)S(1)} %broadcast_select_fusion.8), channel_id=1, source_target_pairs={{0,4},{4,0},{1,5},{5,1},{2,6},{6,2},{3,7},{7,3},{8,12},{12,8},{9,1... | collective-permute-start | bytes 15368 | tf_op jit(solution)/shard_map/ppermute | solution.py:27
  86.2 8.0 %collective-permute-start.10 = (bf16[64,10,1,66]{0,3,2,1:T(8,128)(2,1)S(1)}, bf16[64,10,1,66]{0,3,2,1:T(8,128)(2,1)S(1)}, u32[]{:S(2)}, u32[]{:S(2)}) collective-permute-start(bf16[64,10,1,66]{0,3,2,1:T(8,128)(2,1)S(1)} %get-tuple-element.12), channel_id=1, source_target_pairs={{1,0},{2,1},{3,2},{5,4},{6,5},{7,6},{9,8},{10,9},{11,10},{13,12},{... | collective-permute-start | bytes 253448 | tf_op jit(solution)/shard_map/ppermute | solution.py:34
  87.5 7.6 %collective-permute-start.9 = (bf16[64,10,1,66]{0,3,2,1:T(8,128)(2,1)S(1)}, bf16[64,10,1,66]{0,3,2,1:T(8,128)(2,1)S(1)}, u32[]{:S(2)}, u32[]{:S(2)}) collective-permute-start(bf16[64,10,1,66]{0,3,2,1:T(8,128)(2,1)S(1)} %get-tuple-element.11), channel_id=1, source_target_pairs={{0,1},{1,2},{2,3},{4,5},{5,6},{6,7},{8,9},{9,10},{10,11},{12,13},{... | collective-permute-start | bytes 253448 | tf_op jit(solution)/shard_map/ppermute | solution.py:33
  106.5 28.9 %copy-start.11 = (bf16[256,256]{1,0:T(8,128)(2,1)S(1)}, bf16[256,256]{1,0:T(8,128)(2,1)}, u32[]{:S(2)}) copy-start(bf16[256,256]{1,0:T(8,128)(2,1)} %param.21) | copy-start | bytes 393220
  106.7 29.5 %copy-start.12 = (bf16[256,256]{1,0:T(8,128)(2,1)S(1)}, bf16[256,256]{1,0:T(8,128)(2,1)}, u32[]{:S(2)}) copy-start(bf16[256,256]{1,0:T(8,128)(2,1)} %param.23) | copy-start | bytes 393220
  136.6 5.7 %copy-start.7 = (bf16[8,16384]{1,0:T(8,128)(2,1)S(1)}, bf16[8,16384]{1,0:T(8,128)(2,1)}, u32[]{:S(2)}) copy-start(bf16[8,16384]{1,0:T(8,128)(2,1)} %param.25) | copy-start | bytes 786436
  138.4 15.3 %all-to-all-start.1 = ((bf16[256,128,2]{0,2,1:T(2,128)(2,1)}), bf16[256,128,2]{0,2,1:T(2,128)(2,1)S(1)}, u32[]{:S(2)}, u32[]{:S(2)}) async-start(bf16[256,128,2]{0,2,1:T(2,128)(2,1)} %bitcast.33), calls=%async_computation.1 | async-start | bytes 262144 | tf_op jit(solution)/shard_map/all_to_all | solution.py:329
  158.1 5.8 %collective-permute-start.11 = (bf16[64,8,4,1]{3,0,2,1:T(8,128)(2,1)S(1)}, bf16[64,8,4,1]{3,0,2,1:T(8,128)(2,1)S(1)}, u32[]{:S(2)}, u32[]{:S(2)}) collective-permute-start(bf16[64,8,4,1]{3,0,2,1:T(8,128)(2,1)S(1)} %slice_select_fusion.2), channel_id=1, source_target_pairs={{0,4},{4,0},{1,5},{5,1},{2,6},{6,2},{3,7},{7,3},{8,12},{12,8},{9,1... | collective-permute-start | bytes 12296 | tf_op jit(solution)/shard_map/ppermute | solution.py:27
  164.2 7.1 %collective-permute-start.12 = (bf16[64,8,1,66]{3,0,2,1:T(8,128)(2,1)S(1)}, bf16[64,8,1,66]{3,0,2,1:T(8,128)(2,1)S(1)}, u32[]{:S(2)}, u32[]{:S(2)}) collective-permute-start(bf16[64,8,1,66]{3,0,2,1:T(8,128)(2,1)S(1)} %get-tuple-element.5), channel_id=1, source_target_pairs={{0,1},{1,2},{2,3},{4,5},{5,6},{6,7},{8,9},{9,10},{10,11},{12,13},{... | collective-permute-start | bytes 202760 | tf_op jit(solution)/shard_map/ppermute | solution.py:33
  169.1 5.7 %collective-permute-start.13 = (bf16[64,8,1,66]{3,0,2,1:T(8,128)(2,1)S(1)}, bf16[64,8,1,66]{3,0,2,1:T(8,128)(2,1)S(1)}, u32[]{:S(2)}, u32[]{:S(2)}) collective-permute-start(bf16[64,8,1,66]{3,0,2,1:T(8,128)(2,1)S(1)} %get-tuple-element.6), channel_id=1, source_target_pairs={{1,0},{2,1},{3,2},{5,4},{6,5},{7,6},{9,8},{10,9},{11,10},{13,12},{... | collective-permute-start | bytes 202760 | tf_op jit(solution)/shard_map/ppermute | solution.py:34
  176.5 6.1 %copy-start.13 = (bf16[64,16,2,2,2]{0,4,3,2,1:T(2,128)(2,1)S(1)}, bf16[64,16,2,2,2]{0,4,3,2,1:T(2,128)(2,1)}, u32[]{:S(2)}) copy-start(bf16[64,16,2,2,2]{0,4,3,2,1:T(2,128)(2,1)} %param.27) | copy-start | bytes 49156
  195.1 3.9 %collective-permute-start.14 = (bf16[10,16,1,128]{3,2,1,0:T(2,128)(2,1)S(1)}, bf16[10,16,1,128]{3,2,1,0:T(2,128)(2,1)S(1)}, u32[]{:S(2)}, u32[]{:S(2)}) collective-permute-start(bf16[10,16,1,128]{3,2,1,0:T(2,128)(2,1)S(1)} %get-tuple-element.15), channel_id=1, source_target_pairs={{0,1},{1,2},{2,3},{4,5},{5,6},{6,7},{8,9},{9,10},{10,11},{12,13},{... | collective-permute-start | bytes 122888 | tf_op jit(solution)/shard_map/ppermute | solution.py:133
  197.3 5.2 %collective-permute-start.15 = (bf16[10,16,1,128]{3,2,1,0:T(2,128)(2,1)S(1)}, bf16[10,16,1,128]{3,2,1,0:T(2,128)(2,1)S(1)}, u32[]{:S(2)}, u32[]{:S(2)}) collective-permute-start(bf16[10,16,1,128]{3,2,1,0:T(2,128)(2,1)S(1)} %get-tuple-element.16), channel_id=1, source_target_pairs={{1,0},{2,1},{3,2},{5,4},{6,5},{7,6},{9,8},{10,9},{11,10},{13,12},{... | collective-permute-start | bytes 122888 | tf_op jit(solution)/shard_map/ppermute | solution.py:133
  203.0 5.5 %copy-start.3 = (bf16[10,16,16,128]{3,2,1,0:T(8,128)(2,1)}, bf16[10,16,16,128]{3,2,1,0:T(8,128)(2,1)S(1)}, u32[]{:S(2)}) copy-start(bf16[10,16,16,128]{3,2,1,0:T(8,128)(2,1)S(1)} %maximum_maximum_fusion.2) | copy-start | bytes 1966084
  204.3 4.2 %collective-permute-start.16 = (bf16[10,16,16,1]{2,1,3,0:T(8,128)(2,1)S(1)}, bf16[10,16,16,1]{2,1,3,0:T(8,128)(2,1)S(1)}, u32[]{:S(2)}, u32[]{:S(2)}) collective-permute-start(bf16[10,16,16,1]{2,1,3,0:T(8,128)(2,1)S(1)} %copy.186), channel_id=1, source_target_pairs={{0,4},{4,0},{1,5},{5,1},{2,6},{6,2},{3,7},{7,3},{8,12},{12,8},{9,1... | collective-permute-start | bytes 15368 | tf_op jit(solution)/shard_map/ppermute | solution.py:129
  (10 other events, 25.3 us)

commit v10 on v6

--- a/solution.py
+++ b/solution.py
@@ -99,7 +99,7 @@
 
     lax.fori_loop(0, sx + 2, shift, 0)
 
-    group = 4 if sx % 4 == 0 else 2
+    group = sx if sx <= 8 else (4 if sx % 4 == 0 else 2)
 
     def rows_pair(g, carry):
         x = group * g

time: 218 us -> 218 us (level)
  no operation moved by 1% of the time
where the time goes in v10:
time: 218 us; the launch traced here: 217 us
  starting transfers between devices  46.3 us (21%)
  local copies, waits for them, and re-layouts  43.1 us (20%)
  Pallas kernels  42.5 us (19%)
  waiting for transfers between devices  38.6 us (18%)
  blocking collectives  27.8 us (13%)
  other arithmetic  9.91 us (5%)
  matrix products  8.21 us (4%)
    pallas_call x3, Pallas kernels, fine_conv(): pl.pallas_call(kernel, out_shape=out_shape, scratch_shapes=[pltpu.VMEM((c...  30.3 us
    all_to_all x1, blocking collectives, on_device(): rows = lax.all_to_all(flat, 'gx', split_axis=2, concat_axis=1, tiled=True)  27.8 us
    ppermute x3, starting transfers between devices, extended(): low = lax.ppermute(top, axis, forward)  12.8 us
    ppermute x3, waiting for transfers between devices, faces(): lax.ppermute(bottom, axis, backward)  12.8 us
    pallas_call x2, Pallas kernels, mid_conv(): pl.pallas_call(kernel, out_shape=jax.ShapeDtypeStruct((sx, sv, cout, ss),...  12.1 us
    all_to_all x1, waiting for transfers between devices, on_device(): lax.all_to_all(windows, 'gx', split_axis=1, concat_axis=2, tiled=True)  10.8 us
    ppermute x3, waiting for transfers between devices, extended(): high = lax.ppermute(bottom, axis, backward)  9.9 us
    ppermute x3, starting transfers between devices, faces(): lax.ppermute(top, axis, forward)  9.32 us
  transfers between devices with their start and end apart: 18, of which 13 were waited for; matrix products, arithmetic and copies ran while one was open for 4% of the time, Pallas kernels for 0%

profile of v10, /device:TPU:1, one launch (start us, length us, event | category | flops | bytes accessed | tf_op | source)
XLA Modules:
  0.0 217.2 jit_solution(2369978716514370358)
XLA Ops:
  0.9 3.9 %collective-permute-start = (bf16[8,4,8,128]{3,2,1,0:T(8,128)(2,1)S(1)}, bf16[8,4,8,128]{3,2,1,0:T(8,128)(2,1)S(1)}, u32[]{:S(2)}, u32[]{:S(2)}) collective-permute-start(bf16[8,4,8,128]{3,2,1,0:T(8,128)(2,1)S(1)} %bitcast.175), channel_id=1, source_target_pairs={{0,8},{8,16},{16,24},{24,32},{32,40},{40,48},{48,56},{56,64},{64,7... | collective-permute-start | bytes 196616 | tf_op jit(solution)/shard_map/ppermute | solution.py:33
  6.2 3.7 %collective-permute-done.1 = bf16[8,4,8,128]{3,2,1,0:T(8,128)(2,1)S(1)} collective-permute-done((bf16[8,4,8,128]{3,2,1,0:T(8,128)(2,1)S(1)}, bf16[8,4,8,128]{3,2,1,0:T(8,128)(2,1)S(1)}, u32[]{:S(2)}, u32[]{:S(2)}) %collective-permute-start.1) | collective-permute-done | bytes 65568 | tf_op jit(solution)/shard_map/ppermute | solution.py:34
  10.1 3.5 %collective-permute-start.2 = (bf16[24,8,1,128]{3,2,1,0:T(2,128)(2,1)S(1)}, bf16[24,8,1,128]{3,2,1,0:T(2,128)(2,1)S(1)}, u32[]{:S(2)}, u32[]{:S(2)}) collective-permute-start(bf16[24,8,1,128]{3,2,1,0:T(2,128)(2,1)S(1)} %get-tuple-element.17), channel_id=1, source_target_pairs={{0,1},{1,2},{2,3},{4,5},{5,6},{6,7},{8,9},{9,10},{10,11},{12,13},{... | collective-permute-start | bytes 147464 | tf_op jit(solution)/shard_map/ppermute | solution.py:133
  15.8 3.4 %collective-permute-done.3 = bf16[24,8,1,128]{3,2,1,0:T(2,128)(2,1)S(1)} collective-permute-done((bf16[24,8,1,128]{3,2,1,0:T(2,128)(2,1)S(1)}, bf16[24,8,1,128]{3,2,1,0:T(2,128)(2,1)S(1)}, u32[]{:S(2)}, u32[]{:S(2)}) %collective-permute-start.3) | collective-permute-done | bytes 49184 | tf_op jit(solution)/shard_map/ppermute | solution.py:133
  22.6 3.4 %collective-permute-start.4 = (bf16[24,8,16,1]{0,2,3,1:T(8,128)(2,1)S(1)}, bf16[24,8,16,1]{0,2,3,1:T(8,128)(2,1)S(1)}, u32[]{:S(2)}, u32[]{:S(2)}) collective-permute-start(bf16[24,8,16,1]{0,2,3,1:T(8,128)(2,1)S(1)} %broadcast_select_fusion.11), channel_id=1, source_target_pairs={{0,4},{4,0},{1,5},{5,1},{2,6},{6,2},{3,7},{7,3},{8,12},{12,8},{9,1... | collective-permute-start | bytes 18440 | tf_op jit(solution)/shard_map/ppermute | solution.py:129
  27.9 11.0 %shard_map.145 = f32[22,16,8,128]{3,2,1,0:T(8,128)} custom-call(bf16[24,128,128]{2,1,0:T(8,128)(2,1)} %bitcast.166, bf16[24,8,128]{2,1,0:T(8,128)(2,1)} %pad.33.refs_1_, bf16[27,16,8]{2,1,0:T(8,128)(2,1)} %bitcast.174), custom_call_target="tpu_custom_call" | custom-call | tf_op jit(solution)/shard_map/pallas_call | solution.py:162
  40.7 3.5 %collective-permute-start.5 = (bf16[22,16,1,128]{3,2,1,0:T(2,128)(2,1)S(1)}, bf16[22,16,1,128]{3,2,1,0:T(2,128)(2,1)S(1)}, u32[]{:S(2)}, u32[]{:S(2)}) collective-permute-start(bf16[22,16,1,128]{3,2,1,0:T(2,128)(2,1)S(1)} %get-tuple-element.9), channel_id=1, source_target_pairs={{0,1},{1,2},{2,3},{4,5},{5,6},{6,7},{8,9},{9,10},{10,11},{12,13},{... | collective-permute-start | bytes 270344 | tf_op jit(solution)/shard_map/ppermute | solution.py:133
  47.8 5.7 %collective-permute-done.6 = bf16[22,16,1,128]{3,2,1,0:T(2,128)(2,1)S(1)} collective-permute-done((bf16[22,16,1,128]{3,2,1,0:T(2,128)(2,1)S(1)}, bf16[22,16,1,128]{3,2,1,0:T(2,128)(2,1)S(1)}, u32[]{:S(2)}, u32[]{:S(2)}) %collective-permute-start.6) | collective-permute-done | bytes 90144 | tf_op jit(solution)/shard_map/ppermute | solution.py:133
  61.3 12.0 %shard_map.146 = f32[20,16,8,128]{3,2,1,0:T(8,128)} custom-call(bf16[22,256,128]{2,1,0:T(8,128)(2,1)} %bitcast.165, bf16[22,8,256]{2,1,0:T(8,128)(2,1)} %pad.35.refs_1_, bf16[27,16,16]{2,1,0:T(8,128)(2,1)} %bitcast.180), custom_call_target="tpu_custom_call" | custom-call | tf_op jit(solution)/shard_map/pallas_call | solution.py:162
  74.9 3.5 %copy.161 = bf16[20,16,8,128]{1,3,2,0:T(8,128)(2,1)} copy(bf16[20,16,8,128]{3,2,1,0:T(8,128)(2,1)S(1)} %convert_select_fusion.1) | data formatting | bytes 1310720 | tf_op jit(solution)/shard_map/jit(_where)/select_n | solution.py:46
  78.4 3.8 %multiply_convert_fusion = bf16[64,10,4,64]{0,3,2,1:T(8,128)(2,1)S(1)} fusion(bf16[10,2,16,4,2,64,2]{2,6,5,4,3,1,0:T(2,128)(2,1)} %bitcast.168, bf16[64,16,2,2,2,1,1]{0,4,3,2,1,6,5:T(2,128)(2,1)S(1)} %bitcast.183), kind=kOutput, calls=%fused_computation.8 | convolution fusion | flops 42762240 | bytes 999424 | tf_op jit(solution)/shard_map/xaivbsc,oiabc->oxvs/dot_general | solution.py:242
  87.5 4.0 %collective-permute-start.9 = (bf16[64,10,1,66]{0,3,2,1:T(8,128)(2,1)S(1)}, bf16[64,10,1,66]{0,3,2,1:T(8,128)(2,1)S(1)}, u32[]{:S(2)}, u32[]{:S(2)}) collective-permute-start(bf16[64,10,1,66]{0,3,2,1:T(8,128)(2,1)S(1)} %get-tuple-element.11), channel_id=1, source_target_pairs={{0,1},{1,2},{2,3},{4,5},{5,6},{6,7},{8,9},{9,10},{10,11},{12,13},{... | collective-permute-start | bytes 253448 | tf_op jit(solution)/shard_map/ppermute | solution.py:33
  97.3 6.5 %shard_map.147 = f32[8,4,64,64]{3,2,1,0:T(8,128)} custom-call(bf16[10,64,512]{2,1,0:T(8,128)(2,1)} %pad.36.refs_0_, bf16[64,1728]{1,0:T(8,128)(2,1)} %reshape.153.refs_1_), custom_call_target="tpu_custom_call" | custom-call | tf_op jit(solution)/shard_map/pallas_call | solution.py:220
  106.9 27.8 %all_to_all.24 = bf16[256,2,64]{0,1,2:T(2,128)(2,1)S(1)} all-to-all(bf16[256,2,64]{0,1,2:T(2,128)(2,1)S(1)} %copy.167), channel_id=1, replica_groups=mesh['gx'=32,'gy'=2,'gz'=4] {'gx'}, dimensions={2} | all-to-all | bytes 131072 | tf_op jit(solution)/shard_map/all_to_all | solution.py:317
  138.6 3.9 %all-to-all-start.1 = ((bf16[256,128,2]{0,2,1:T(2,128)(2,1)}), bf16[256,128,2]{0,2,1:T(2,128)(2,1)S(1)}, u32[]{:S(2)}, u32[]{:S(2)}) async-start(bf16[256,128,2]{0,2,1:T(2,128)(2,1)} %bitcast.33), calls=%async_computation.1 | async-start | bytes 262144 | tf_op jit(solution)/shard_map/all_to_all | solution.py:329
  143.0 10.8 %all-to-all-done.1 = bf16[256,128,2]{0,2,1:T(2,128)(2,1)S(1)} async-done(((bf16[256,128,2]{0,2,1:T(2,128)(2,1)}), bf16[256,128,2]{0,2,1:T(2,128)(2,1)S(1)}, u32[]{:S(2)}, u32[]{:S(2)}) %all-to-all-start.1) | async-done | bytes 131104 | tf_op jit(solution)/shard_map/all_to_all | solution.py:329
  158.3 3.9 %collective-permute-start.11 = (bf16[64,8,4,1]{3,0,2,1:T(8,128)(2,1)S(1)}, bf16[64,8,4,1]{3,0,2,1:T(8,128)(2,1)S(1)}, u32[]{:S(2)}, u32[]{:S(2)}) collective-permute-start(bf16[64,8,4,1]{3,0,2,1:T(8,128)(2,1)S(1)} %slice_select_fusion.2), channel_id=1, source_target_pairs={{0,4},{4,0},{1,5},{5,1},{2,6},{6,2},{3,7},{7,3},{8,12},{12,8},{9,1... | collective-permute-start | bytes 12296 | tf_op jit(solution)/shard_map/ppermute | solution.py:27
  164.4 4.9 %collective-permute-start.12 = (bf16[64,8,1,66]{3,0,2,1:T(8,128)(2,1)S(1)}, bf16[64,8,1,66]{3,0,2,1:T(8,128)(2,1)S(1)}, u32[]{:S(2)}, u32[]{:S(2)}) collective-permute-start(bf16[64,8,1,66]{3,0,2,1:T(8,128)(2,1)S(1)} %get-tuple-element.5), channel_id=1, source_target_pairs={{0,1},{1,2},{2,3},{4,5},{5,6},{6,7},{8,9},{9,10},{10,11},{12,13},{... | collective-permute-start | bytes 202760 | tf_op jit(solution)/shard_map/ppermute | solution.py:33
  171.5 3.5 %collective-permute-done.13 = bf16[64,8,1,66]{3,0,2,1:T(8,128)(2,1)S(1)} collective-permute-done((bf16[64,8,1,66]{3,0,2,1:T(8,128)(2,1)S(1)}, bf16[64,8,1,66]{3,0,2,1:T(8,128)(2,1)S(1)}, u32[]{:S(2)}, u32[]{:S(2)}) %collective-permute-start.13) | collective-permute-done | bytes 67616 | tf_op jit(solution)/shard_map/ppermute | solution.py:34
  177.6 5.7 %shard_map.148 = f32[6,4,64,64]{3,2,1,0:T(8,128)} custom-call(bf16[8,64,512]{2,1,0:T(8,128)(2,1)} %pad.38.refs_0_, bf16[64,1728]{1,0:T(8,128)(2,1)} %reshape.167.refs_1_), custom_call_target="tpu_custom_call" | custom-call | tf_op jit(solution)/shard_map/pallas_call | solution.py:220
  184.8 6.4 %copy.184 = f32[6,2,16,4,2,64,2]{2,6,5,4,3,1,0:T(2,128)} copy(f32[6,2,16,4,2,64,2]{5,2,6,4,1,3,0:T(8,128)S(1)} %convolution_bitcast_fusion) | data formatting | bytes 1572864 | tf_op jit(solution)/shard_map/ixvs,ioabc->xaovbsc/transpose | solution.py:246
  191.2 4.4 %copy.185 = f32[12,16,8,128]{3,2,1,0:T(8,128)S(1)} copy(f32[12,16,8,128]{1,3,2,0:T(8,128)} %bitcast.164) | data formatting | bytes 1572864 | tf_op jit(solution)/shard_map/reshape | solution.py:248
  199.5 3.7 %collective-permute-done.15 = bf16[10,16,1,128]{3,2,1,0:T(2,128)(2,1)S(1)} collective-permute-done((bf16[10,16,1,128]{3,2,1,0:T(2,128)(2,1)S(1)}, bf16[10,16,1,128]{3,2,1,0:T(2,128)(2,1)S(1)}, u32[]{:S(2)}, u32[]{:S(2)}) %collective-permute-start.15) | collective-permute-done | bytes 40992 | tf_op jit(solution)/shard_map/ppermute | solution.py:133
  209.9 7.3 %shard_map.149 = f32[4,8,8,128]{3,2,1,0:T(8,128)} custom-call(bf16[10,256,128]{2,1,0:T(8,128)(2,1)} %bitcast.167, bf16[10,8,256]{2,1,0:T(8,128)(2,1)} %pad.39.refs_1_, bf16[27,16,16]{2,1,0:T(8,128)(2,1)} %bitcast.181, bf16[32,128]{1,0:T(8,128)(2,1)} %convert_element_type.137.refs_3_), custom_call_target="tpu_custom_call" | custom-call | tf_op jit(solution)/shard_map/pallas_call | solution.py:162
  (160 shorter events, 66.0 us)
Async XLA Ops:
  0.0 135.3 %copy-start = (bf16[256,256]{1,0:T(8,128)(2,1)S(1)}, bf16[256,256]{1,0:T(8,128)(2,1)}, u32[]{:S(2)}) copy-start(bf16[256,256]{1,0:T(8,128)(2,1)} %param.22) | copy-start | bytes 393220
  0.9 5.3 %collective-permute-start = (bf16[8,4,8,128]{3,2,1,0:T(8,128)(2,1)S(1)}, bf16[8,4,8,128]{3,2,1,0:T(8,128)(2,1)S(1)}, u32[]{:S(2)}, u32[]{:S(2)}) collective-permute-start(bf16[8,4,8,128]{3,2,1,0:T(8,128)(2,1)S(1)} %bitcast.175), channel_id=1, source_target_pairs={{0,8},{8,16},{16,24},{24,32},{32,40},{40,48},{48,56},{56,64},{64,7... | collective-permute-start | bytes 196616 | tf_op jit(solution)/shard_map/ppermute | solution.py:33
  4.8 5.0 %collective-permute-start.1 = (bf16[8,4,8,128]{3,2,1,0:T(8,128)(2,1)S(1)}, bf16[8,4,8,128]{3,2,1,0:T(8,128)(2,1)S(1)}, u32[]{:S(2)}, u32[]{:S(2)}) collective-permute-start(bf16[8,4,8,128]{3,2,1,0:T(8,128)(2,1)S(1)} %bitcast.176), channel_id=1, source_target_pairs={{8,0},{16,8},{24,16},{32,24},{40,32},{48,40},{56,48},{64,56},{72,6... | collective-permute-start | bytes 196616 | tf_op jit(solution)/shard_map/ppermute | solution.py:34
  10.1 5.7 %collective-permute-start.2 = (bf16[24,8,1,128]{3,2,1,0:T(2,128)(2,1)S(1)}, bf16[24,8,1,128]{3,2,1,0:T(2,128)(2,1)S(1)}, u32[]{:S(2)}, u32[]{:S(2)}) collective-permute-start(bf16[24,8,1,128]{3,2,1,0:T(2,128)(2,1)S(1)} %get-tuple-element.17), channel_id=1, source_target_pairs={{0,1},{1,2},{2,3},{4,5},{5,6},{6,7},{8,9},{9,10},{10,11},{12,13},{... | collective-permute-start | bytes 147464 | tf_op jit(solution)/shard_map/ppermute | solution.py:133
  13.6 5.5 %collective-permute-start.3 = (bf16[24,8,1,128]{3,2,1,0:T(2,128)(2,1)S(1)}, bf16[24,8,1,128]{3,2,1,0:T(2,128)(2,1)S(1)}, u32[]{:S(2)}, u32[]{:S(2)}) collective-permute-start(bf16[24,8,1,128]{3,2,1,0:T(2,128)(2,1)S(1)} %get-tuple-element.18), channel_id=1, source_target_pairs={{1,0},{2,1},{3,2},{5,4},{6,5},{7,6},{9,8},{10,9},{11,10},{13,12},{... | collective-permute-start | bytes 147464 | tf_op jit(solution)/shard_map/ppermute | solution.py:133
  22.6 4.3 %collective-permute-start.4 = (bf16[24,8,16,1]{0,2,3,1:T(8,128)(2,1)S(1)}, bf16[24,8,16,1]{0,2,3,1:T(8,128)(2,1)S(1)}, u32[]{:S(2)}, u32[]{:S(2)}) collective-permute-start(bf16[24,8,16,1]{0,2,3,1:T(8,128)(2,1)S(1)} %broadcast_select_fusion.11), channel_id=1, source_target_pairs={{0,4},{4,0},{1,5},{5,1},{2,6},{6,2},{3,7},{7,3},{8,12},{12,8},{9,1... | collective-permute-start | bytes 18440 | tf_op jit(solution)/shard_map/ppermute | solution.py:129
  40.7 7.1 %collective-permute-start.5 = (bf16[22,16,1,128]{3,2,1,0:T(2,128)(2,1)S(1)}, bf16[22,16,1,128]{3,2,1,0:T(2,128)(2,1)S(1)}, u32[]{:S(2)}, u32[]{:S(2)}) collective-permute-start(bf16[22,16,1,128]{3,2,1,0:T(2,128)(2,1)S(1)} %get-tuple-element.9), channel_id=1, source_target_pairs={{0,1},{1,2},{2,3},{4,5},{5,6},{6,7},{8,9},{9,10},{10,11},{12,13},{... | collective-permute-start | bytes 270344 | tf_op jit(solution)/shard_map/ppermute | solution.py:133
  44.2 9.2 %collective-permute-start.6 = (bf16[22,16,1,128]{3,2,1,0:T(2,128)(2,1)S(1)}, bf16[22,16,1,128]{3,2,1,0:T(2,128)(2,1)S(1)}, u32[]{:S(2)}, u32[]{:S(2)}) collective-permute-start(bf16[22,16,1,128]{3,2,1,0:T(2,128)(2,1)S(1)} %get-tuple-element.10), channel_id=1, source_target_pairs={{1,0},{2,1},{3,2},{5,4},{6,5},{7,6},{9,8},{10,9},{11,10},{13,12},{... | collective-permute-start | bytes 270344 | tf_op jit(solution)/shard_map/ppermute | solution.py:133
  57.7 2.3 %collective-permute-start.7 = (bf16[22,16,16,1]{0,2,3,1:T(8,128)(2,1)S(1)}, bf16[22,16,16,1]{0,2,3,1:T(8,128)(2,1)S(1)}, u32[]{:S(2)}, u32[]{:S(2)}) collective-permute-start(bf16[22,16,16,1]{0,2,3,1:T(8,128)(2,1)S(1)} %copy.157), channel_id=1, source_target_pairs={{0,4},{4,0},{1,5},{5,1},{2,6},{6,2},{3,7},{7,3},{8,12},{12,8},{9,1... | collective-permute-start | bytes 33800 | tf_op jit(solution)/shard_map/ppermute | solution.py:129
  82.3 3.6 %collective-permute-start.8 = (bf16[64,10,4,1]{0,3,2,1:T(2,128)(2,1)S(1)}, bf16[64,10,4,1]{0,3,2,1:T(2,128)(2,1)S(1)}, u32[]{:S(2)}, u32[]{:S(2)}) collective-permute-start(bf16[64,10,4,1]{0,3,2,1:T(2,128)(2,1)S(1)} %broadcast_select_fusion.8), channel_id=1, source_target_pairs={{0,4},{4,0},{1,5},{5,1},{2,6},{6,2},{3,7},{7,3},{8,12},{12,8},{9,1... | collective-permute-start | bytes 15368 | tf_op jit(solution)/shard_map/ppermute | solution.py:27
  86.2 8.0 %collective-permute-start.10 = (bf16[64,10,1,66]{0,3,2,1:T(8,128)(2,1)S(1)}, bf16[64,10,1,66]{0,3,2,1:T(8,128)(2,1)S(1)}, u32[]{:S(2)}, u32[]{:S(2)}) collective-permute-start(bf16[64,10,1,66]{0,3,2,1:T(8,128)(2,1)S(1)} %get-tuple-element.12), channel_id=1, source_target_pairs={{1,0},{2,1},{3,2},{5,4},{6,5},{7,6},{9,8},{10,9},{11,10},{13,12},{... | collective-permute-start | bytes 253448 | tf_op jit(solution)/shard_map/ppermute | solution.py:34
  87.5 7.6 %collective-permute-start.9 = (bf16[64,10,1,66]{0,3,2,1:T(8,128)(2,1)S(1)}, bf16[64,10,1,66]{0,3,2,1:T(8,128)(2,1)S(1)}, u32[]{:S(2)}, u32[]{:S(2)}) collective-permute-start(bf16[64,10,1,66]{0,3,2,1:T(8,128)(2,1)S(1)} %get-tuple-element.11), channel_id=1, source_target_pairs={{0,1},{1,2},{2,3},{4,5},{5,6},{6,7},{8,9},{9,10},{10,11},{12,13},{... | collective-permute-start | bytes 253448 | tf_op jit(solution)/shard_map/ppermute | solution.py:33
  106.8 28.9 %copy-start.11 = (bf16[256,256]{1,0:T(8,128)(2,1)S(1)}, bf16[256,256]{1,0:T(8,128)(2,1)}, u32[]{:S(2)}) copy-start(bf16[256,256]{1,0:T(8,128)(2,1)} %param.21) | copy-start | bytes 393220
  106.9 29.5 %copy-start.12 = (bf16[256,256]{1,0:T(8,128)(2,1)S(1)}, bf16[256,256]{1,0:T(8,128)(2,1)}, u32[]{:S(2)}) copy-start(bf16[256,256]{1,0:T(8,128)(2,1)} %param.23) | copy-start | bytes 393220
  136.8 5.7 %copy-start.7 = (bf16[8,16384]{1,0:T(8,128)(2,1)S(1)}, bf16[8,16384]{1,0:T(8,128)(2,1)}, u32[]{:S(2)}) copy-start(bf16[8,16384]{1,0:T(8,128)(2,1)} %param.25) | copy-start | bytes 786436
  138.6 15.3 %all-to-all-start.1 = ((bf16[256,128,2]{0,2,1:T(2,128)(2,1)}), bf16[256,128,2]{0,2,1:T(2,128)(2,1)S(1)}, u32[]{:S(2)}, u32[]{:S(2)}) async-start(bf16[256,128,2]{0,2,1:T(2,128)(2,1)} %bitcast.33), calls=%async_computation.1 | async-start | bytes 262144 | tf_op jit(solution)/shard_map/all_to_all | solution.py:329
  158.3 5.8 %collective-permute-start.11 = (bf16[64,8,4,1]{3,0,2,1:T(8,128)(2,1)S(1)}, bf16[64,8,4,1]{3,0,2,1:T(8,128)(2,1)S(1)}, u32[]{:S(2)}, u32[]{:S(2)}) collective-permute-start(bf16[64,8,4,1]{3,0,2,1:T(8,128)(2,1)S(1)} %slice_select_fusion.2), channel_id=1, source_target_pairs={{0,4},{4,0},{1,5},{5,1},{2,6},{6,2},{3,7},{7,3},{8,12},{12,8},{9,1... | collective-permute-start | bytes 12296 | tf_op jit(solution)/shard_map/ppermute | solution.py:27
  164.4 7.1 %collective-permute-start.12 = (bf16[64,8,1,66]{3,0,2,1:T(8,128)(2,1)S(1)}, bf16[64,8,1,66]{3,0,2,1:T(8,128)(2,1)S(1)}, u32[]{:S(2)}, u32[]{:S(2)}) collective-permute-start(bf16[64,8,1,66]{3,0,2,1:T(8,128)(2,1)S(1)} %get-tuple-element.5), channel_id=1, source_target_pairs={{0,1},{1,2},{2,3},{4,5},{5,6},{6,7},{8,9},{9,10},{10,11},{12,13},{... | collective-permute-start | bytes 202760 | tf_op jit(solution)/shard_map/ppermute | solution.py:33
  169.3 5.7 %collective-permute-start.13 = (bf16[64,8,1,66]{3,0,2,1:T(8,128)(2,1)S(1)}, bf16[64,8,1,66]{3,0,2,1:T(8,128)(2,1)S(1)}, u32[]{:S(2)}, u32[]{:S(2)}) collective-permute-start(bf16[64,8,1,66]{3,0,2,1:T(8,128)(2,1)S(1)} %get-tuple-element.6), channel_id=1, source_target_pairs={{1,0},{2,1},{3,2},{5,4},{6,5},{7,6},{9,8},{10,9},{11,10},{13,12},{... | collective-permute-start | bytes 202760 | tf_op jit(solution)/shard_map/ppermute | solution.py:34
  176.7 6.5 %copy-start.13 = (bf16[64,16,2,2,2]{0,4,3,2,1:T(2,128)(2,1)S(1)}, bf16[64,16,2,2,2]{0,4,3,2,1:T(2,128)(2,1)}, u32[]{:S(2)}) copy-start(bf16[64,16,2,2,2]{0,4,3,2,1:T(2,128)(2,1)} %param.27) | copy-start | bytes 49156
  195.8 3.7 %collective-permute-start.14 = (bf16[10,16,1,128]{3,2,1,0:T(2,128)(2,1)S(1)}, bf16[10,16,1,128]{3,2,1,0:T(2,128)(2,1)S(1)}, u32[]{:S(2)}, u32[]{:S(2)}) collective-permute-start(bf16[10,16,1,128]{3,2,1,0:T(2,128)(2,1)S(1)} %get-tuple-element.15), channel_id=1, source_target_pairs={{0,1},{1,2},{2,3},{4,5},{5,6},{6,7},{8,9},{9,10},{10,11},{12,13},{... | collective-permute-start | bytes 122888 | tf_op jit(solution)/shard_map/ppermute | solution.py:133
  198.0 5.2 %collective-permute-start.15 = (bf16[10,16,1,128]{3,2,1,0:T(2,128)(2,1)S(1)}, bf16[10,16,1,128]{3,2,1,0:T(2,128)(2,1)S(1)}, u32[]{:S(2)}, u32[]{:S(2)}) collective-permute-start(bf16[10,16,1,128]{3,2,1,0:T(2,128)(2,1)S(1)} %get-tuple-element.16), channel_id=1, source_target_pairs={{1,0},{2,1},{3,2},{5,4},{6,5},{7,6},{9,8},{10,9},{11,10},{13,12},{... | collective-permute-start | bytes 122888 | tf_op jit(solution)/shard_map/ppermute | solution.py:133
  203.7 5.5 %copy-start.3 = (bf16[10,16,16,128]{3,2,1,0:T(8,128)(2,1)}, bf16[10,16,16,128]{3,2,1,0:T(8,128)(2,1)S(1)}, u32[]{:S(2)}) copy-start(bf16[10,16,16,128]{3,2,1,0:T(8,128)(2,1)S(1)} %maximum_maximum_fusion.2) | copy-start | bytes 1966084
  205.0 4.1 %collective-permute-start.16 = (bf16[10,16,16,1]{2,1,3,0:T(8,128)(2,1)S(1)}, bf16[10,16,16,1]{2,1,3,0:T(8,128)(2,1)S(1)}, u32[]{:S(2)}, u32[]{:S(2)}) collective-permute-start(bf16[10,16,16,1]{2,1,3,0:T(8,128)(2,1)S(1)} %copy.186), channel_id=1, source_target_pairs={{0,4},{4,0},{1,5},{5,1},{2,6},{6,2},{3,7},{7,3},{8,12},{12,8},{9,1... | collective-permute-start | bytes 15368 | tf_op jit(solution)/shard_map/ppermute | solution.py:129
  (10 other events, 25.1 us)
